TPU v7x, 1024 devices: a whole 8x8x8 slice. The times are simulated.
1024 devices in a mesh: slab: 64 (over z, y), leaf: 16 (over x, core).
Axes of the slice: x: 8, y: 8, z: 8, core: 2. Of those that a mesh axis runs over, the one named last changes fastest.
Arguments:
- probes: bfloat16 [524288, 128], P(('slab', 'leaf')), may hold values from -6 to 6
- near_blocks: bfloat16 [1024, 3, 512, 512], P(('slab', 'leaf')), may hold values from -0.15625 to 0.15625
- near_offsets: int32 [1024, 3], P(('slab', 'leaf')), may hold values from -1 to 1
- far_basis: bfloat16 [10, 524288, 128], P(None, ('slab', 'leaf')), may hold values from -0.25 to 0.25
Outputs:
- product: float32 [524288, 128], P(('slab', 'leaf'))
Inputs may be any that keep to these rules, and one draw needn't show every extreme that they name: `near_offsets`: offsets that point outside the leaves meet zero probes.
All inputs are finite; a program needn't handle non-finite values.
Results may differ from a plain program's by a relative error of at most 0.0025.
Values may be sent and summed in bfloat16 or wider, within the bound.
No kernel may reach another device: no remote copies, remote signals or barrier semaphores. Data moves between devices by JAX's collectives and lax.ppermute only.
A program may use at most 32 MiB of HBM per device.

v0:
```python
import jax
import jax.numpy as jnp
from jax import lax
from jax.sharding import PartitionSpec as P


def extended(block, sides, width):
    for axis, dim in sides:
        count = lax.axis_size(axis)
        forward = [(i, i + 1) for i in range(count - 1)]
        backward = [(target, source) for source, target in forward]
        low = lax.ppermute(
            lax.slice_in_dim(block, block.shape[dim] - width, None, axis=dim), axis, forward
        )
        high = lax.ppermute(lax.slice_in_dim(block, 0, width, axis=dim), axis, backward)
        block = jnp.concatenate([low, block, high], axis=dim)
    return block


def swapped(value, axis, bit):
    mask = 2**bit
    pairs = [(source, source ^ mask) for source in range(lax.axis_size(axis))]
    return lax.ppermute(value, axis, pairs)


def body(probes, near_blocks, near_offsets, far_basis):
    leaf_rows = probes.shape[0]
    levels = far_basis.shape[0]
    padded = extended(probes, ((("slab", "leaf"), 0),), leaf_rows)
    near_sum = jnp.zeros(probes.shape, jnp.float32)
    for member in range(near_blocks.shape[1]):
        window_start = (near_offsets[0, member] + 1) * leaf_rows
        window = lax.dynamic_slice_in_dim(padded, window_start, leaf_rows, 0)
        near_sum = near_sum + jnp.dot(
            near_blocks[0, member], window, preferred_element_type=jnp.float32
        )
    projected = jnp.einsum("lpr,pq->lrq", far_basis, probes, preferred_element_type=jnp.float32)
    leaf_bits = lax.axis_size("leaf").bit_length() - 1
    sibling = [None] * levels
    partial_sums = [projected[level] for level in range(levels)]
    for tree_bit in range(leaf_bits):
        incoming = swapped(jnp.stack(partial_sums[tree_bit:]), "leaf", tree_bit)
        sibling[tree_bit] = incoming[0]
        for level in range(tree_bit + 1, levels):
            partial_sums[level] = partial_sums[level] + incoming[level - tree_bit]
    for tree_bit in range(levels - leaf_bits):
        level_now = leaf_bits + tree_bit
        incoming = swapped(jnp.stack(partial_sums[level_now:]), "slab", tree_bit)
        sibling[level_now] = incoming[0]
        for level in range(level_now + 1, levels):
            partial_sums[level] = partial_sums[level] + incoming[level - level_now]
    output = near_sum
    for level in range(levels):
        coupling = (sibling[level] * 2.0 ** (-0.5 * level)).astype(jnp.bfloat16)
        output = output + jnp.dot(far_basis[level], coupling, preferred_element_type=jnp.float32)
    return output


def solution(mesh):
    return jax.shard_map(
        body,
        mesh=mesh,
        in_specs=(
            P(("slab", "leaf"), None),
            P(("slab", "leaf"), None, None, None),
            P(("slab", "leaf"), None),
            P(None, ("slab", "leaf"), None),
        ),
        out_specs=P(("slab", "leaf"), None),
        check_vma=False,
    )
```

profile of v0, /device:TPU:54, one launch (start us, length us, event | category | flops | bytes accessed | tf_op | source)
XLA Modules:
  0.0 168.2 jit_solution(17991002277142826760)
XLA Ops:
  0.0 1.9 %fusion.24 = f32[10,128,128]{2,1,0:T(8,128)S(1)} fusion(bf16[10,512,128]{2,1,0:T(8,128)(2,1)} %param.7, bf16[512,128]{1,0:T(8,128)(2,1)} %param.4), kind=kOutput, calls=%fused_computation.36 | convolution fusion | flops 167772160 | bytes 2097152 | tf_op jit(solution)/shard_map/lpr,pq->lrq/dot_general | solution.py:37
  1.9 0.0 copy-start.2
  1.9 0.0 copy-start.3
  1.9 2.1 %collective-permute-start.2 = (f32[10,128,128]{2,1,0:T(8,128)S(1)}, f32[10,128,128]{2,1,0:T(8,128)S(1)}, u32[]{:S(2)}, u32[]{:S(2)}) collective-permute-start(f32[10,128,128]{2,1,0:T(8,128)S(1)} %fusion.24), channel_id=1, source_target_pairs={{0,1},{1,0},{2,3},{3,2},{4,5},{5,4},{6,7},{7,6},{8,9},{9,8},{10,11... | collective-permute-start | bytes 1966088 | tf_op jit(solution)/shard_map/ppermute | solution.py:23
  3.9 2.1 %collective-permute-done.2 = f32[10,128,128]{2,1,0:T(8,128)S(1)} collective-permute-done((f32[10,128,128]{2,1,0:T(8,128)S(1)}, f32[10,128,128]{2,1,0:T(8,128)S(1)}, u32[]{:S(2)}, u32[]{:S(2)}) %collective-permute-start.2) | collective-permute-done | bytes 655392 | tf_op jit(solution)/shard_map/ppermute | solution.py:23
  6.2 2.4 %collective-permute-start.3 = (f32[9,128,128]{2,1,0:T(8,128)S(1)}, f32[9,128,128]{2,1,0:T(8,128)S(1)}, u32[]{:S(2)}, u32[]{:S(2)}) collective-permute-start(f32[9,128,128]{2,1,0:T(8,128)S(1)} %constant_dynamic-update-slice_fusion.3), channel_id=1, source_target_pairs={{0,2},{1,3},{2,0},{3,1},{4,6},{5,7},{6,4},{7,5},{8,10},{9,11},{10,... | collective-permute-start | bytes 1769480 | tf_op jit(solution)/shard_map/ppermute | solution.py:23
  8.6 0.0 copy-done.2
  8.6 1.9 %collective-permute-start = (bf16[512,128]{1,0:T(8,128)(2,1)S(1)}, bf16[512,128]{1,0:T(8,128)(2,1)S(1)}, u32[]{:S(2)}, u32[]{:S(2)}) collective-permute-start(bf16[512,128]{1,0:T(8,128)(2,1)S(1)} %copy-done.2), channel_id=1, source_target_pairs={{0,1},{1,2},{2,3},{3,4},{4,5},{5,6},{6,7},{7,8},{8,9},{9,10},{10,1... | collective-permute-start | bytes 393224 | tf_op jit(solution)/shard_map/ppermute | solution.py:12
  10.6 3.6 %collective-permute-start.1 = (bf16[512,128]{1,0:T(8,128)(2,1)S(1)}, bf16[512,128]{1,0:T(8,128)(2,1)S(1)}, u32[]{:S(2)}, u32[]{:S(2)}) collective-permute-start(bf16[512,128]{1,0:T(8,128)(2,1)S(1)} %copy-done.2), channel_id=1, source_target_pairs={{1,0},{2,1},{3,2},{4,3},{5,4},{6,5},{7,6},{8,7},{9,8},{10,9},{11,1... | collective-permute-start | bytes 393224 | tf_op jit(solution)/shard_map/ppermute | solution.py:15
  14.2 0.0 copy-done.3
  14.2 0.7 fusion.88
  16.8 7.4 %collective-permute-done.3 = f32[9,128,128]{2,1,0:T(8,128)S(1)} collective-permute-done((f32[9,128,128]{2,1,0:T(8,128)S(1)}, f32[9,128,128]{2,1,0:T(8,128)S(1)}, u32[]{:S(2)}, u32[]{:S(2)}) %collective-permute-start.3) | collective-permute-done | bytes 589856 | tf_op jit(solution)/shard_map/ppermute | solution.py:23
  24.3 0.0 copy-start.1
  24.4 2.5 %collective-permute-start.4 = (f32[8,128,128]{2,1,0:T(8,128)S(1)}, f32[8,128,128]{2,1,0:T(8,128)S(1)}, u32[]{:S(2)}, u32[]{:S(2)}) collective-permute-start(f32[8,128,128]{2,1,0:T(8,128)S(1)} %constant_dynamic-update-slice_fusion.12), channel_id=1, source_target_pairs={{0,4},{1,5},{2,6},{3,7},{4,0},{5,1},{6,2},{7,3},{8,12},{9,13},{10,... | collective-permute-start | bytes 1572872 | tf_op jit(solution)/shard_map/ppermute | solution.py:23
  27.0 0.0 collective-permute-done
  27.0 0.0 collective-permute-done.1
  27.1 0.0 copy-done.1
  27.1 0.3 fusion.4
  27.4 23.4 %collective-permute-done.4 = f32[8,128,128]{2,1,0:T(8,128)S(1)} collective-permute-done((f32[8,128,128]{2,1,0:T(8,128)S(1)}, f32[8,128,128]{2,1,0:T(8,128)S(1)}, u32[]{:S(2)}, u32[]{:S(2)}) %collective-permute-start.4) | collective-permute-done | bytes 524320 | tf_op jit(solution)/shard_map/ppermute | solution.py:23
  50.9 0.0 copy-start
  51.0 4.9 %collective-permute-start.5 = (f32[7,128,128]{2,1,0:T(8,128)S(1)}, f32[7,128,128]{2,1,0:T(8,128)S(1)}, u32[]{:S(2)}, u32[]{:S(2)}) collective-permute-start(f32[7,128,128]{2,1,0:T(8,128)S(1)} %get-tuple-element.5), channel_id=1, source_target_pairs={{0,8},{1,9},{2,10},{3,11},{4,12},{5,13},{6,14},{7,15},{8,0},{9,1},... | collective-permute-start | bytes 1376264 | tf_op jit(solution)/shard_map/ppermute | solution.py:23
  55.9 0.3 fusion.6
  56.2 0.0 copy-done
  56.2 0.2 fusion.22
  56.4 21.4 %collective-permute-done.5 = f32[7,128,128]{2,1,0:T(8,128)S(1)} collective-permute-done((f32[7,128,128]{2,1,0:T(8,128)S(1)}, f32[7,128,128]{2,1,0:T(8,128)S(1)}, u32[]{:S(2)}, u32[]{:S(2)}) %collective-permute-start.5) | collective-permute-done | bytes 458784 | tf_op jit(solution)/shard_map/ppermute | solution.py:23
  77.9 2.2 %collective-permute-start.6 = (f32[6,128,128]{2,1,0:T(8,128)S(1)}, f32[6,128,128]{2,1,0:T(8,128)S(1)}, u32[]{:S(2)}, u32[]{:S(2)}) collective-permute-start(f32[6,128,128]{2,1,0:T(8,128)S(1)} %constant_dynamic-update-slice_fusion.27), channel_id=1, source_target_pairs={{0,16},{16,0},{32,48},{48,32},{64,80},{80,64},{96,112},{112,96},{1... | collective-permute-start | bytes 1179656 | tf_op jit(solution)/shard_map/ppermute | solution.py:23
  80.2 0.2 fusion.20
  80.4 0.3 fusion.3
  80.7 10.1 %collective-permute-done.6 = f32[6,128,128]{2,1,0:T(8,128)S(1)} collective-permute-done((f32[6,128,128]{2,1,0:T(8,128)S(1)}, f32[6,128,128]{2,1,0:T(8,128)S(1)}, u32[]{:S(2)}, u32[]{:S(2)}) %collective-permute-start.6) | collective-permute-done | bytes 393248 | tf_op jit(solution)/shard_map/ppermute | solution.py:23
  91.0 6.5 %collective-permute-start.7 = (f32[5,128,128]{2,1,0:T(8,128)S(1)}, f32[5,128,128]{2,1,0:T(8,128)S(1)}, u32[]{:S(2)}, u32[]{:S(2)}) collective-permute-start(f32[5,128,128]{2,1,0:T(8,128)S(1)} %constant_dynamic-update-slice_fusion.33), channel_id=1, source_target_pairs={{0,32},{16,48},{32,0},{48,16},{64,96},{80,112},{96,64},{112,80},{1... | collective-permute-start | bytes 983048 | tf_op jit(solution)/shard_map/ppermute | solution.py:23
  97.5 0.2 convolution_add_fusion.7
  97.7 0.2 convolution_add_fusion.6
  97.9 12.1 %collective-permute-done.7 = f32[5,128,128]{2,1,0:T(8,128)S(1)} collective-permute-done((f32[5,128,128]{2,1,0:T(8,128)S(1)}, f32[5,128,128]{2,1,0:T(8,128)S(1)}, u32[]{:S(2)}, u32[]{:S(2)}) %collective-permute-start.7) | collective-permute-done | bytes 327712 | tf_op jit(solution)/shard_map/ppermute | solution.py:23
  110.0 0.1 slice_add_fusion.9
  110.1 5.0 %collective-permute-start.8 = (f32[4,128,128]{2,1,0:T(8,128)S(1)}, f32[4,128,128]{2,1,0:T(8,128)S(1)}, u32[]{:S(2)}, u32[]{:S(2)}) collective-permute-start(f32[4,128,128]{2,1,0:T(8,128)S(1)} %pad_maximum_fusion), channel_id=1, source_target_pairs={{0,64},{16,80},{32,96},{48,112},{64,0},{80,16},{96,32},{112,48},{1... | collective-permute-start | bytes 786440 | tf_op jit(solution)/shard_map/ppermute | solution.py:23
  115.1 0.2 convolution_add_fusion.5
  115.4 0.2 convolution_add_fusion.4
  115.6 13.2 %collective-permute-done.8 = f32[4,128,128]{2,1,0:T(8,128)S(1)} collective-permute-done((f32[4,128,128]{2,1,0:T(8,128)S(1)}, f32[4,128,128]{2,1,0:T(8,128)S(1)}, u32[]{:S(2)}, u32[]{:S(2)}) %collective-permute-start.8) | collective-permute-done | bytes 262176 | tf_op jit(solution)/shard_map/ppermute | solution.py:23
  128.9 5.2 %collective-permute-start.9 = (f32[3,128,128]{2,1,0:T(8,128)S(1)}, f32[3,128,128]{2,1,0:T(8,128)S(1)}, u32[]{:S(2)}, u32[]{:S(2)}) collective-permute-start(f32[3,128,128]{2,1,0:T(8,128)S(1)} %pad_maximum_fusion.1), channel_id=1, source_target_pairs={{0,128},{16,144},{32,160},{48,176},{64,192},{80,208},{96,224},{112... | collective-permute-start | bytes 589832 | tf_op jit(solution)/shard_map/ppermute | solution.py:23
  134.1 0.2 convolution_add_fusion.3
  134.3 4.9 %collective-permute-done.9 = f32[3,128,128]{2,1,0:T(8,128)S(1)} collective-permute-done((f32[3,128,128]{2,1,0:T(8,128)S(1)}, f32[3,128,128]{2,1,0:T(8,128)S(1)}, u32[]{:S(2)}, u32[]{:S(2)}) %collective-permute-start.9) | collective-permute-done | bytes 196640 | tf_op jit(solution)/shard_map/ppermute | solution.py:23
  139.2 7.9 %collective-permute-start.10 = (f32[2,128,128]{2,1,0:T(8,128)S(1)}, f32[2,128,128]{2,1,0:T(8,128)S(1)}, u32[]{:S(2)}, u32[]{:S(2)}) collective-permute-start(f32[2,128,128]{2,1,0:T(8,128)S(1)} %pad_maximum_fusion.2), channel_id=1, source_target_pairs={{0,256},{16,272},{32,288},{48,304},{64,320},{80,336},{96,352},{112... | collective-permute-start | bytes 393224 | tf_op jit(solution)/shard_map/ppermute | solution.py:23
  147.1 0.2 convolution_add_fusion.2
  147.3 5.7 %collective-permute-done.10 = f32[2,128,128]{2,1,0:T(8,128)S(1)} collective-permute-done((f32[2,128,128]{2,1,0:T(8,128)S(1)}, f32[2,128,128]{2,1,0:T(8,128)S(1)}, u32[]{:S(2)}, u32[]{:S(2)}) %collective-permute-start.10) | collective-permute-done | bytes 131104 | tf_op jit(solution)/shard_map/ppermute | solution.py:23
  153.0 11.8 %collective-permute-start.11 = (f32[1,128,128]{2,1,0:T(8,128)S(1)}, f32[1,128,128]{2,1,0:T(8,128)S(1)}, u32[]{:S(2)}, u32[]{:S(2)}) collective-permute-start(f32[1,128,128]{2,1,0:T(8,128)S(1)} %slice_add_fusion), channel_id=1, source_target_pairs={{0,512},{16,528},{32,544},{48,560},{64,576},{80,592},{96,608},{112... | collective-permute-start | bytes 196616 | tf_op jit(solution)/shard_map/ppermute | solution.py:23
  164.9 0.2 convolution_add_fusion.1
  165.1 2.0 %collective-permute-done.11 = f32[1,128,128]{2,1,0:T(8,128)S(1)} collective-permute-done((f32[1,128,128]{2,1,0:T(8,128)S(1)}, f32[1,128,128]{2,1,0:T(8,128)S(1)}, u32[]{:S(2)}, u32[]{:S(2)}) %collective-permute-start.11) | collective-permute-done | bytes 65568 | tf_op jit(solution)/shard_map/ppermute | solution.py:23
  167.1 0.2 fusion
  167.3 0.8 copy.6
  (44 shorter events, 0.7 us)
Async XLA Ops:
  1.9 6.8 %copy-start.2 = (bf16[512,128]{1,0:T(8,128)(2,1)S(1)}, bf16[512,128]{1,0:T(8,128)(2,1)}, u32[]{:S(2)}) copy-start(bf16[512,128]{1,0:T(8,128)(2,1)} %param.4) | copy-start | bytes 393220
  1.9 12.3 %copy-start.3 = (s32[1,3]{1,0:T(1,128)S(1)}, s32[1,3]{1,0:T(1,128)}, u32[]{:S(2)}) copy-start(s32[1,3]{1,0:T(1,128)} %param.6) | copy-start | bytes 40
  1.9 4.1 %collective-permute-start.2 = (f32[10,128,128]{2,1,0:T(8,128)S(1)}, f32[10,128,128]{2,1,0:T(8,128)S(1)}, u32[]{:S(2)}, u32[]{:S(2)}) collective-permute-start(f32[10,128,128]{2,1,0:T(8,128)S(1)} %fusion.24), channel_id=1, source_target_pairs={{0,1},{1,0},{2,3},{3,2},{4,5},{5,4},{6,7},{7,6},{8,9},{9,8},{10,11... | collective-permute-start | bytes 1966088 | tf_op jit(solution)/shard_map/ppermute | solution.py:23
  6.2 18.1 %collective-permute-start.3 = (f32[9,128,128]{2,1,0:T(8,128)S(1)}, f32[9,128,128]{2,1,0:T(8,128)S(1)}, u32[]{:S(2)}, u32[]{:S(2)}) collective-permute-start(f32[9,128,128]{2,1,0:T(8,128)S(1)} %constant_dynamic-update-slice_fusion.3), channel_id=1, source_target_pairs={{0,2},{1,3},{2,0},{3,1},{4,6},{5,7},{6,4},{7,5},{8,10},{9,11},{10,... | collective-permute-start | bytes 1769480 | tf_op jit(solution)/shard_map/ppermute | solution.py:23
  8.6 18.4 %collective-permute-start = (bf16[512,128]{1,0:T(8,128)(2,1)S(1)}, bf16[512,128]{1,0:T(8,128)(2,1)S(1)}, u32[]{:S(2)}, u32[]{:S(2)}) collective-permute-start(bf16[512,128]{1,0:T(8,128)(2,1)S(1)} %copy-done.2), channel_id=1, source_target_pairs={{0,1},{1,2},{2,3},{3,4},{4,5},{5,6},{6,7},{7,8},{8,9},{9,10},{10,1... | collective-permute-start | bytes 393224 | tf_op jit(solution)/shard_map/ppermute | solution.py:12
  10.6 16.5 %collective-permute-start.1 = (bf16[512,128]{1,0:T(8,128)(2,1)S(1)}, bf16[512,128]{1,0:T(8,128)(2,1)S(1)}, u32[]{:S(2)}, u32[]{:S(2)}) collective-permute-start(bf16[512,128]{1,0:T(8,128)(2,1)S(1)} %copy-done.2), channel_id=1, source_target_pairs={{1,0},{2,1},{3,2},{4,3},{5,4},{6,5},{7,6},{8,7},{9,8},{10,9},{11,1... | collective-permute-start | bytes 393224 | tf_op jit(solution)/shard_map/ppermute | solution.py:15
  24.3 2.8 %copy-start.1 = (bf16[1,3,512,512]{3,2,1,0:T(8,128)(2,1)S(1)}, bf16[1,3,512,512]{3,2,1,0:T(8,128)(2,1)}, u32[]{:S(2)}) copy-start(bf16[1,3,512,512]{3,2,1,0:T(8,128)(2,1)} %param.5) | copy-start | bytes 4718596
  24.4 26.4 %collective-permute-start.4 = (f32[8,128,128]{2,1,0:T(8,128)S(1)}, f32[8,128,128]{2,1,0:T(8,128)S(1)}, u32[]{:S(2)}, u32[]{:S(2)}) collective-permute-start(f32[8,128,128]{2,1,0:T(8,128)S(1)} %constant_dynamic-update-slice_fusion.12), channel_id=1, source_target_pairs={{0,4},{1,5},{2,6},{3,7},{4,0},{5,1},{6,2},{7,3},{8,12},{9,13},{10,... | collective-permute-start | bytes 1572872 | tf_op jit(solution)/shard_map/ppermute | solution.py:23
  50.9 5.3 %copy-start = (bf16[10,512,128]{2,1,0:T(8,128)(2,1)S(1)}, bf16[10,512,128]{2,1,0:T(8,128)(2,1)}, u32[]{:S(2)}) copy-start(bf16[10,512,128]{2,1,0:T(8,128)(2,1)} %param.7) | copy-start | bytes 3932164
  51.0 26.8 %collective-permute-start.5 = (f32[7,128,128]{2,1,0:T(8,128)S(1)}, f32[7,128,128]{2,1,0:T(8,128)S(1)}, u32[]{:S(2)}, u32[]{:S(2)}) collective-permute-start(f32[7,128,128]{2,1,0:T(8,128)S(1)} %get-tuple-element.5), channel_id=1, source_target_pairs={{0,8},{1,9},{2,10},{3,11},{4,12},{5,13},{6,14},{7,15},{8,0},{9,1},... | collective-permute-start | bytes 1376264 | tf_op jit(solution)/shard_map/ppermute | solution.py:23
  77.9 12.9 %collective-permute-start.6 = (f32[6,128,128]{2,1,0:T(8,128)S(1)}, f32[6,128,128]{2,1,0:T(8,128)S(1)}, u32[]{:S(2)}, u32[]{:S(2)}) collective-permute-start(f32[6,128,128]{2,1,0:T(8,128)S(1)} %constant_dynamic-update-slice_fusion.27), channel_id=1, source_target_pairs={{0,16},{16,0},{32,48},{48,32},{64,80},{80,64},{96,112},{112,96},{1... | collective-permute-start | bytes 1179656 | tf_op jit(solution)/shard_map/ppermute | solution.py:23
  91.0 19.1 %collective-permute-start.7 = (f32[5,128,128]{2,1,0:T(8,128)S(1)}, f32[5,128,128]{2,1,0:T(8,128)S(1)}, u32[]{:S(2)}, u32[]{:S(2)}) collective-permute-start(f32[5,128,128]{2,1,0:T(8,128)S(1)} %constant_dynamic-update-slice_fusion.33), channel_id=1, source_target_pairs={{0,32},{16,48},{32,0},{48,16},{64,96},{80,112},{96,64},{112,80},{1... | collective-permute-start | bytes 983048 | tf_op jit(solution)/shard_map/ppermute | solution.py:23
  110.1 18.7 %collective-permute-start.8 = (f32[4,128,128]{2,1,0:T(8,128)S(1)}, f32[4,128,128]{2,1,0:T(8,128)S(1)}, u32[]{:S(2)}, u32[]{:S(2)}) collective-permute-start(f32[4,128,128]{2,1,0:T(8,128)S(1)} %pad_maximum_fusion), channel_id=1, source_target_pairs={{0,64},{16,80},{32,96},{48,112},{64,0},{80,16},{96,32},{112,48},{1... | collective-permute-start | bytes 786440 | tf_op jit(solution)/shard_map/ppermute | solution.py:23
  128.9 10.3 %collective-permute-start.9 = (f32[3,128,128]{2,1,0:T(8,128)S(1)}, f32[3,128,128]{2,1,0:T(8,128)S(1)}, u32[]{:S(2)}, u32[]{:S(2)}) collective-permute-start(f32[3,128,128]{2,1,0:T(8,128)S(1)} %pad_maximum_fusion.1), channel_id=1, source_target_pairs={{0,128},{16,144},{32,160},{48,176},{64,192},{80,208},{96,224},{112... | collective-permute-start | bytes 589832 | tf_op jit(solution)/shard_map/ppermute | solution.py:23
  139.2 13.8 %collective-permute-start.10 = (f32[2,128,128]{2,1,0:T(8,128)S(1)}, f32[2,128,128]{2,1,0:T(8,128)S(1)}, u32[]{:S(2)}, u32[]{:S(2)}) collective-permute-start(f32[2,128,128]{2,1,0:T(8,128)S(1)} %pad_maximum_fusion.2), channel_id=1, source_target_pairs={{0,256},{16,272},{32,288},{48,304},{64,320},{80,336},{96,352},{112... | collective-permute-start | bytes 393224 | tf_op jit(solution)/shard_map/ppermute | solution.py:23
  153.0 14.1 %collective-permute-start.11 = (f32[1,128,128]{2,1,0:T(8,128)S(1)}, f32[1,128,128]{2,1,0:T(8,128)S(1)}, u32[]{:S(2)}, u32[]{:S(2)}) collective-permute-start(f32[1,128,128]{2,1,0:T(8,128)S(1)} %slice_add_fusion), channel_id=1, source_target_pairs={{0,512},{16,528},{32,544},{48,560},{64,576},{80,592},{96,608},{112... | collective-permute-start | bytes 196616 | tf_op jit(solution)/shard_map/ppermute | solution.py:23
where the time goes:
time: 169 us; the launch traced here: 168 us
  waiting for transfers between devices  102 us (60%)
  starting transfers between devices  56.2 us (33%)
  matrix products  4.89 us (3%)
  between operations  2.48 us (1%)
    ppermute x10, waiting for transfers between devices, swapped(): return lax.ppermute(value, axis, pairs)  102 us
    ppermute x10, starting transfers between devices, swapped(): return lax.ppermute(value, axis, pairs)  50.7 us
    ppermute x1, starting transfers between devices, extended(): lax.ppermute(lax.slice_in_dim(block, 0, width, axis=dim), axis, backward)  3.64 us
  transfers between devices with their start and end apart: 12, of which 10 were waited for; matrix products, arithmetic and copies ran while one was open for 2% of the time, Pallas kernels for 0%

commit v1 on v0

--- a/solution.py
+++ b/solution.py
@@ -35,24 +35,58 @@
             near_blocks[0, member], window, preferred_element_type=jnp.float32
         )
     projected = jnp.einsum("lpr,pq->lrq", far_basis, probes, preferred_element_type=jnp.float32)
+    rank, width = projected.shape[1], projected.shape[2]
     leaf_bits = lax.axis_size("leaf").bit_length() - 1
+    slab_bits = levels - leaf_bits
+    leaf_index = lax.axis_index("leaf")
+
+    low = [projected[level] for level in range(leaf_bits)]
+    upper = projected[leaf_bits:]
     sibling = [None] * levels
-    partial_sums = [projected[level] for level in range(levels)]
     for tree_bit in range(leaf_bits):
-        incoming = swapped(jnp.stack(partial_sums[tree_bit:]), "leaf", tree_bit)
-        sibling[tree_bit] = incoming[0]
-        for level in range(tree_bit + 1, levels):
-            partial_sums[level] = partial_sums[level] + incoming[level - tree_bit]
-    for tree_bit in range(levels - leaf_bits):
-        level_now = leaf_bits + tree_bit
-        incoming = swapped(jnp.stack(partial_sums[level_now:]), "slab", tree_bit)
-        sibling[level_now] = incoming[0]
-        for level in range(level_now + 1, levels):
-            partial_sums[level] = partial_sums[level] + incoming[level - level_now]
+        half = upper.shape[1] // 2
+        bit = (leaf_index >> tree_bit) & 1
+        keep = lax.dynamic_slice_in_dim(upper, bit * half, half, axis=1)
+        send = lax.dynamic_slice_in_dim(upper, (1 - bit) * half, half, axis=1)
+        whole = leaf_bits - tree_bit
+        packet = jnp.concatenate(
+            [jnp.stack(low[tree_bit:]).reshape(-1, width), send.reshape(-1, width)], axis=0
+        )
+        incoming = swapped(packet, "leaf", tree_bit)
+        incoming_low = incoming[: whole * rank].reshape(whole, rank, width)
+        incoming_upper = incoming[whole * rank :].reshape(slab_bits, half, width)
+        sibling[tree_bit] = incoming_low[0]
+        for level in range(tree_bit + 1, leaf_bits):
+            low[level] = low[level] + incoming_low[level - tree_bit]
+        upper = keep + incoming_upper
+
+    partial_sums = [upper[step] for step in range(slab_bits)]
+    shares = []
+    for step in range(slab_bits):
+        incoming = swapped(jnp.stack(partial_sums[step:]), "slab", step)
+        level = leaf_bits + step
+        shares.append((incoming[0] * 2.0 ** (-0.5 * level)).astype(jnp.bfloat16))
+        for later in range(step + 1, slab_bits):
+            partial_sums[later] = partial_sums[later] + incoming[later - step]
+
+    gathered = jnp.stack(shares)
+    for tree_bit in reversed(range(leaf_bits)):
+        bit = (leaf_index >> tree_bit) & 1
+        other = swapped(gathered, "leaf", tree_bit)
+        gathered = jnp.where(
+            bit == 0,
+            jnp.concatenate([gathered, other], axis=1),
+            jnp.concatenate([other, gathered], axis=1),
+        )
+
     output = near_sum
-    for level in range(levels):
+    for level in range(leaf_bits):
         coupling = (sibling[level] * 2.0 ** (-0.5 * level)).astype(jnp.bfloat16)
         output = output + jnp.dot(far_basis[level], coupling, preferred_element_type=jnp.float32)
+    for step in range(slab_bits):
+        output = output + jnp.dot(
+            far_basis[leaf_bits + step], gathered[step], preferred_element_type=jnp.float32
+        )
     return output
 
 

time: 169 us -> 126 us (0.75)
  the two profiles are of different devices: /device:TPU:54 before, /device:TPU:1 now
where the time goes in v1:
time: 126 us; the launch traced here: 125 us
  starting transfers between devices  65 us (52%)
  waiting for transfers between devices  50.8 us (40%)
  matrix products  4.9 us (4%)
  between operations  2.5 us (2%)
  local copies, waits for them, and re-layouts  1.71 us (1%)
    ppermute x14, starting transfers between devices, swapped(): return lax.ppermute(value, axis, pairs)  59.2 us
    ppermute x14, waiting for transfers between devices, swapped(): return lax.ppermute(value, axis, pairs)  50.8 us
    ppermute x1, starting transfers between devices, extended(): lax.ppermute(lax.slice_in_dim(block, block.shape[dim] - width, None, axis...  3.9 us
  transfers between devices with their start and end apart: 16, of which 13 were waited for; matrix products, arithmetic and copies ran while one was open for 2% of the time, Pallas kernels for 0%

profile of v1, /device:TPU:1, one launch (start us, length us, event | category | flops | bytes accessed | tf_op | source)
XLA Modules:
  0.0 125.4 jit_solution(8915777601113699908)
XLA Ops:
  0.0 1.9 %fusion.30 = f32[10,128,128]{2,1,0:T(8,128)S(1)} fusion(bf16[10,512,128]{2,1,0:T(8,128)(2,1)} %param.7, bf16[512,128]{1,0:T(8,128)(2,1)} %param.4), kind=kOutput, calls=%fused_computation.43 | convolution fusion | flops 167772160 | bytes 2097152 | tf_op jit(solution)/shard_map/lpr,pq->lrq/dot_general | solution.py:37
  2.0 16.0 %collective-permute-start.2 = (f32[896,128]{1,0:T(8,128)S(1)}, f32[896,128]{1,0:T(8,128)S(1)}, u32[]{:S(2)}, u32[]{:S(2)}) collective-permute-start(f32[896,128]{1,0:T(8,128)S(1)} %pad_maximum_fusion), channel_id=1, source_target_pairs={{0,1},{1,0},{2,3},{3,2},{4,5},{5,4},{6,7},{7,6},{8,9},{9,8},{10,11... | collective-permute-start | bytes 1376264 | tf_op jit(solution)/shard_map/ppermute | solution.py:23
  18.0 0.0 copy-start.2
  18.0 0.0 copy-start.3
  18.1 1.4 %collective-permute-done.2 = f32[896,128]{1,0:T(8,128)S(1)} collective-permute-done((f32[896,128]{1,0:T(8,128)S(1)}, f32[896,128]{1,0:T(8,128)S(1)}, u32[]{:S(2)}, u32[]{:S(2)}) %collective-permute-start.2) | collective-permute-done | bytes 458784 | tf_op jit(solution)/shard_map/ppermute | solution.py:23
  19.6 1.9 %collective-permute-start.3 = (f32[576,128]{1,0:T(8,128)S(1)}, f32[576,128]{1,0:T(8,128)S(1)}, u32[]{:S(2)}, u32[]{:S(2)}) collective-permute-start(f32[576,128]{1,0:T(8,128)S(1)} %pad_maximum_fusion.1), channel_id=1, source_target_pairs={{0,2},{1,3},{2,0},{3,1},{4,6},{5,7},{6,4},{7,5},{8,10},{9,11},{10,... | collective-permute-start | bytes 884744 | tf_op jit(solution)/shard_map/ppermute | solution.py:23
  21.5 0.0 copy-done.2
  21.6 3.9 %collective-permute-start = (bf16[512,128]{1,0:T(8,128)(2,1)S(1)}, bf16[512,128]{1,0:T(8,128)(2,1)S(1)}, u32[]{:S(2)}, u32[]{:S(2)}) collective-permute-start(bf16[512,128]{1,0:T(8,128)(2,1)S(1)} %copy-done.2), channel_id=1, source_target_pairs={{0,1},{1,2},{2,3},{3,4},{4,5},{5,6},{6,7},{7,8},{8,9},{9,10},{10,1... | collective-permute-start | bytes 393224 | tf_op jit(solution)/shard_map/ppermute | solution.py:12
  25.5 1.9 %collective-permute-start.1 = (bf16[512,128]{1,0:T(8,128)(2,1)S(1)}, bf16[512,128]{1,0:T(8,128)(2,1)S(1)}, u32[]{:S(2)}, u32[]{:S(2)}) collective-permute-start(bf16[512,128]{1,0:T(8,128)(2,1)S(1)} %copy-done.2), channel_id=1, source_target_pairs={{1,0},{2,1},{3,2},{4,3},{5,4},{6,5},{7,6},{8,7},{9,8},{10,9},{11,1... | collective-permute-start | bytes 393224 | tf_op jit(solution)/shard_map/ppermute | solution.py:15
  27.4 0.0 copy-done.3
  27.4 0.7 fusion.70
  30.0 0.0 collective-permute-done
  30.0 0.0 collective-permute-done.3
  30.1 0.0 copy-start.1
  30.2 2.1 %collective-permute-start.4 = (f32[352,128]{1,0:T(8,128)S(1)}, f32[352,128]{1,0:T(8,128)S(1)}, u32[]{:S(2)}, u32[]{:S(2)}) collective-permute-start(f32[352,128]{1,0:T(8,128)S(1)} %pad_maximum_fusion.3), channel_id=1, source_target_pairs={{0,4},{1,5},{2,6},{3,7},{4,0},{5,1},{6,2},{7,3},{8,12},{9,13},{10,... | collective-permute-start | bytes 540680 | tf_op jit(solution)/shard_map/ppermute | solution.py:23
  32.3 0.0 collective-permute-done.1
  32.3 11.0 %collective-permute-done.4 = f32[352,128]{1,0:T(8,128)S(1)} collective-permute-done((f32[352,128]{1,0:T(8,128)S(1)}, f32[352,128]{1,0:T(8,128)S(1)}, u32[]{:S(2)}, u32[]{:S(2)}) %collective-permute-start.4) | collective-permute-done | bytes 180256 | tf_op jit(solution)/shard_map/ppermute | solution.py:23
  43.3 0.0 copy-start
  43.4 2.1 %collective-permute-start.5 = (f32[176,128]{1,0:T(8,128)S(1)}, f32[176,128]{1,0:T(8,128)S(1)}, u32[]{:S(2)}, u32[]{:S(2)}) collective-permute-start(f32[176,128]{1,0:T(8,128)S(1)} %pad_maximum_fusion.5), channel_id=1, source_target_pairs={{0,8},{1,9},{2,10},{3,11},{4,12},{5,13},{6,14},{7,15},{8,0},{9,1},... | collective-permute-start | bytes 270344 | tf_op jit(solution)/shard_map/ppermute | solution.py:23
  45.4 0.0 copy-done.1
  45.5 0.3 fusion.7
  45.8 6.9 %collective-permute-done.5 = f32[176,128]{1,0:T(8,128)S(1)} collective-permute-done((f32[176,128]{1,0:T(8,128)S(1)}, f32[176,128]{1,0:T(8,128)S(1)}, u32[]{:S(2)}, u32[]{:S(2)}) %collective-permute-start.5) | collective-permute-done | bytes 90144 | tf_op jit(solution)/shard_map/ppermute | solution.py:23
  52.7 1.9 %collective-permute-start.6 = (f32[6,8,128]{2,1,0:T(8,128)S(1)}, f32[6,8,128]{2,1,0:T(8,128)S(1)}, u32[]{:S(2)}, u32[]{:S(2)}) collective-permute-start(f32[6,8,128]{2,1,0:T(8,128)S(1)} %fusion.58), channel_id=1, source_target_pairs={{0,16},{16,0},{32,48},{48,32},{64,80},{80,64},{96,112},{112,96},{1... | collective-permute-start | bytes 73736 | tf_op jit(solution)/shard_map/ppermute | solution.py:23
  54.6 0.3 fusion.9
  54.9 2.3 %collective-permute-done.6 = f32[6,8,128]{2,1,0:T(8,128)S(1)} collective-permute-done((f32[6,8,128]{2,1,0:T(8,128)S(1)}, f32[6,8,128]{2,1,0:T(8,128)S(1)}, u32[]{:S(2)}, u32[]{:S(2)}) %collective-permute-start.6) | collective-permute-done | bytes 24608 | tf_op jit(solution)/shard_map/ppermute | solution.py:23
  57.3 1.9 %collective-permute-start.7 = (f32[5,8,128]{2,1,0:T(8,128)S(1)}, f32[5,8,128]{2,1,0:T(8,128)S(1)}, u32[]{:S(2)}, u32[]{:S(2)}) collective-permute-start(f32[5,8,128]{2,1,0:T(8,128)S(1)} %constant_dynamic-update-slice_fusion.3), channel_id=1, source_target_pairs={{0,32},{16,48},{32,0},{48,16},{64,96},{80,112},{96,64},{112,80},{1... | collective-permute-start | bytes 61448 | tf_op jit(solution)/shard_map/ppermute | solution.py:23
  59.2 3.5 %collective-permute-done.7 = f32[5,8,128]{2,1,0:T(8,128)S(1)} collective-permute-done((f32[5,8,128]{2,1,0:T(8,128)S(1)}, f32[5,8,128]{2,1,0:T(8,128)S(1)}, u32[]{:S(2)}, u32[]{:S(2)}) %collective-permute-start.7) | collective-permute-done | bytes 20512 | tf_op jit(solution)/shard_map/ppermute | solution.py:23
  62.7 1.9 %collective-permute-start.8 = (f32[4,8,128]{2,1,0:T(8,128)S(1)}, f32[4,8,128]{2,1,0:T(8,128)S(1)}, u32[]{:S(2)}, u32[]{:S(2)}) collective-permute-start(f32[4,8,128]{2,1,0:T(8,128)S(1)} %pad_maximum_fusion.6), channel_id=1, source_target_pairs={{0,64},{16,80},{32,96},{48,112},{64,0},{80,16},{96,32},{112,48},{1... | collective-permute-start | bytes 49160 | tf_op jit(solution)/shard_map/ppermute | solution.py:23
  64.7 6.4 %collective-permute-done.8 = f32[4,8,128]{2,1,0:T(8,128)S(1)} collective-permute-done((f32[4,8,128]{2,1,0:T(8,128)S(1)}, f32[4,8,128]{2,1,0:T(8,128)S(1)}, u32[]{:S(2)}, u32[]{:S(2)}) %collective-permute-start.8) | collective-permute-done | bytes 16416 | tf_op jit(solution)/shard_map/ppermute | solution.py:23
  71.1 1.9 %collective-permute-start.9 = (f32[3,8,128]{2,1,0:T(8,128)S(1)}, f32[3,8,128]{2,1,0:T(8,128)S(1)}, u32[]{:S(2)}, u32[]{:S(2)}) collective-permute-start(f32[3,8,128]{2,1,0:T(8,128)S(1)} %pad_maximum_fusion.7), channel_id=1, source_target_pairs={{0,128},{16,144},{32,160},{48,176},{64,192},{80,208},{96,224},{112... | collective-permute-start | bytes 36872 | tf_op jit(solution)/shard_map/ppermute | solution.py:23
  73.1 2.8 %collective-permute-done.9 = f32[3,8,128]{2,1,0:T(8,128)S(1)} collective-permute-done((f32[3,8,128]{2,1,0:T(8,128)S(1)}, f32[3,8,128]{2,1,0:T(8,128)S(1)}, u32[]{:S(2)}, u32[]{:S(2)}) %collective-permute-start.9) | collective-permute-done | bytes 12320 | tf_op jit(solution)/shard_map/ppermute | solution.py:23
  75.9 1.9 %collective-permute-start.10 = (f32[2,8,128]{2,1,0:T(8,128)S(1)}, f32[2,8,128]{2,1,0:T(8,128)S(1)}, u32[]{:S(2)}, u32[]{:S(2)}) collective-permute-start(f32[2,8,128]{2,1,0:T(8,128)S(1)} %pad_maximum_fusion.8), channel_id=1, source_target_pairs={{0,256},{16,272},{32,288},{48,304},{64,320},{80,336},{96,352},{112... | collective-permute-start | bytes 24584 | tf_op jit(solution)/shard_map/ppermute | solution.py:23
  77.8 3.5 %collective-permute-done.10 = f32[2,8,128]{2,1,0:T(8,128)S(1)} collective-permute-done((f32[2,8,128]{2,1,0:T(8,128)S(1)}, f32[2,8,128]{2,1,0:T(8,128)S(1)}, u32[]{:S(2)}, u32[]{:S(2)}) %collective-permute-start.10) | collective-permute-done | bytes 8224 | tf_op jit(solution)/shard_map/ppermute | solution.py:23
  81.3 4.5 %collective-permute-start.11 = (f32[1,8,128]{2,1,0:T(8,128)S(1)}, f32[1,8,128]{2,1,0:T(8,128)S(1)}, u32[]{:S(2)}, u32[]{:S(2)}) collective-permute-start(f32[1,8,128]{2,1,0:T(8,128)S(1)} %slice_add_fusion.1), channel_id=1, source_target_pairs={{0,512},{16,528},{32,544},{48,560},{64,576},{80,592},{96,608},{112... | collective-permute-start | bytes 12296 | tf_op jit(solution)/shard_map/ppermute | solution.py:23
  85.8 3.7 %collective-permute-done.11 = f32[1,8,128]{2,1,0:T(8,128)S(1)} collective-permute-done((f32[1,8,128]{2,1,0:T(8,128)S(1)}, f32[1,8,128]{2,1,0:T(8,128)S(1)}, u32[]{:S(2)}, u32[]{:S(2)}) %collective-permute-start.11) | collective-permute-done | bytes 4128 | tf_op jit(solution)/shard_map/ppermute | solution.py:23
  89.5 4.3 %collective-permute-start.12 = (bf16[6,8,128]{2,1,0:T(8,128)(2,1)S(1)}, bf16[6,8,128]{2,1,0:T(8,128)(2,1)S(1)}, u32[]{:S(2)}, u32[]{:S(2)}) collective-permute-start(bf16[6,8,128]{2,1,0:T(8,128)(2,1)S(1)} %constant_dynamic-update-slice_fusion.8), channel_id=1, source_target_pairs={{0,8},{1,9},{2,10},{3,11},{4,12},{5,13},{6,14},{7,15},{8,0},{9,1},... | collective-permute-start | bytes 36872 | tf_op jit(solution)/shard_map/ppermute | solution.py:23
  93.9 0.0 copy-done
  93.9 0.2 fusion.28
  94.1 3.8 %collective-permute-done.12 = bf16[6,8,128]{2,1,0:T(8,128)(2,1)S(1)} collective-permute-done((bf16[6,8,128]{2,1,0:T(8,128)(2,1)S(1)}, bf16[6,8,128]{2,1,0:T(8,128)(2,1)S(1)}, u32[]{:S(2)}, u32[]{:S(2)}) %collective-permute-start.12) | collective-permute-done | bytes 12320 | tf_op jit(solution)/shard_map/ppermute | solution.py:23
  97.9 1.9 %collective-permute-start.13 = (bf16[6,16,128]{2,1,0:T(8,128)(2,1)S(1)}, bf16[6,16,128]{2,1,0:T(8,128)(2,1)S(1)}, u32[]{:S(2)}, u32[]{:S(2)}) collective-permute-start(bf16[6,16,128]{2,1,0:T(8,128)(2,1)S(1)} %maximum_select_fusion.3), channel_id=1, source_target_pairs={{0,4},{1,5},{2,6},{3,7},{4,0},{5,1},{6,2},{7,3},{8,12},{9,13},{10,... | collective-permute-start | bytes 73736 | tf_op jit(solution)/shard_map/ppermute | solution.py:23
  99.8 0.2 fusion.26
  100.0 3.3 %collective-permute-done.13 = bf16[6,16,128]{2,1,0:T(8,128)(2,1)S(1)} collective-permute-done((bf16[6,16,128]{2,1,0:T(8,128)(2,1)S(1)}, bf16[6,16,128]{2,1,0:T(8,128)(2,1)S(1)}, u32[]{:S(2)}, u32[]{:S(2)}) %collective-permute-start.13) | collective-permute-done | bytes 24608 | tf_op jit(solution)/shard_map/ppermute | solution.py:23
  103.4 3.1 %collective-permute-start.14 = (bf16[6,32,128]{2,1,0:T(8,128)(2,1)S(1)}, bf16[6,32,128]{2,1,0:T(8,128)(2,1)S(1)}, u32[]{:S(2)}, u32[]{:S(2)}) collective-permute-start(bf16[6,32,128]{2,1,0:T(8,128)(2,1)S(1)} %maximum_select_fusion.2), channel_id=1, source_target_pairs={{0,2},{1,3},{2,0},{3,1},{4,6},{5,7},{6,4},{7,5},{8,10},{9,11},{10,... | collective-permute-start | bytes 147464 | tf_op jit(solution)/shard_map/ppermute | solution.py:23
  106.5 0.2 fusion.24
  106.7 1.5 %collective-permute-done.14 = bf16[6,32,128]{2,1,0:T(8,128)(2,1)S(1)} collective-permute-done((bf16[6,32,128]{2,1,0:T(8,128)(2,1)S(1)}, bf16[6,32,128]{2,1,0:T(8,128)(2,1)S(1)}, u32[]{:S(2)}, u32[]{:S(2)}) %collective-permute-start.14) | collective-permute-done | bytes 49184 | tf_op jit(solution)/shard_map/ppermute | solution.py:23
  108.2 13.6 %collective-permute-start.15 = (bf16[6,64,128]{2,1,0:T(8,128)(2,1)S(1)}, bf16[6,64,128]{2,1,0:T(8,128)(2,1)S(1)}, u32[]{:S(2)}, u32[]{:S(2)}) collective-permute-start(bf16[6,64,128]{2,1,0:T(8,128)(2,1)S(1)} %maximum_select_fusion.1), channel_id=1, source_target_pairs={{0,1},{1,0},{2,3},{3,2},{4,5},{5,4},{6,7},{7,6},{8,9},{9,8},{10,11... | collective-permute-start | bytes 294920 | tf_op jit(solution)/shard_map/ppermute | solution.py:23
  121.9 0.2 fusion.22
  122.1 0.7 collective-permute-done.15
  122.8 0.1 maximum_select_fusion
  122.9 0.2 fusion.20
  123.1 0.4 fusion.6
  123.4 0.2 convolution_add_fusion.4
  123.7 0.2 convolution_add_fusion.3
  123.9 0.2 convolution_add_fusion.2
  124.1 0.2 convolution_add_fusion.1
  124.3 0.2 fusion
  124.5 0.8 copy.6
  (46 shorter events, 0.6 us)
Async XLA Ops:
  2.0 17.5 %collective-permute-start.2 = (f32[896,128]{1,0:T(8,128)S(1)}, f32[896,128]{1,0:T(8,128)S(1)}, u32[]{:S(2)}, u32[]{:S(2)}) collective-permute-start(f32[896,128]{1,0:T(8,128)S(1)} %pad_maximum_fusion), channel_id=1, source_target_pairs={{0,1},{1,0},{2,3},{3,2},{4,5},{5,4},{6,7},{7,6},{8,9},{9,8},{10,11... | collective-permute-start | bytes 1376264 | tf_op jit(solution)/shard_map/ppermute | solution.py:23
  18.0 3.5 %copy-start.2 = (bf16[512,128]{1,0:T(8,128)(2,1)S(1)}, bf16[512,128]{1,0:T(8,128)(2,1)}, u32[]{:S(2)}) copy-start(bf16[512,128]{1,0:T(8,128)(2,1)} %param.4) | copy-start | bytes 393220
  18.0 9.4 %copy-start.3 = (s32[1,3]{1,0:T(1,128)S(1)}, s32[1,3]{1,0:T(1,128)}, u32[]{:S(2)}) copy-start(s32[1,3]{1,0:T(1,128)} %param.6) | copy-start | bytes 40
  19.6 10.4 %collective-permute-start.3 = (f32[576,128]{1,0:T(8,128)S(1)}, f32[576,128]{1,0:T(8,128)S(1)}, u32[]{:S(2)}, u32[]{:S(2)}) collective-permute-start(f32[576,128]{1,0:T(8,128)S(1)} %pad_maximum_fusion.1), channel_id=1, source_target_pairs={{0,2},{1,3},{2,0},{3,1},{4,6},{5,7},{6,4},{7,5},{8,10},{9,11},{10,... | collective-permute-start | bytes 884744 | tf_op jit(solution)/shard_map/ppermute | solution.py:23
  21.6 8.5 %collective-permute-start = (bf16[512,128]{1,0:T(8,128)(2,1)S(1)}, bf16[512,128]{1,0:T(8,128)(2,1)S(1)}, u32[]{:S(2)}, u32[]{:S(2)}) collective-permute-start(bf16[512,128]{1,0:T(8,128)(2,1)S(1)} %copy-done.2), channel_id=1, source_target_pairs={{0,1},{1,2},{2,3},{3,4},{4,5},{5,6},{6,7},{7,8},{8,9},{9,10},{10,1... | collective-permute-start | bytes 393224 | tf_op jit(solution)/shard_map/ppermute | solution.py:12
  25.5 6.8 %collective-permute-start.1 = (bf16[512,128]{1,0:T(8,128)(2,1)S(1)}, bf16[512,128]{1,0:T(8,128)(2,1)S(1)}, u32[]{:S(2)}, u32[]{:S(2)}) collective-permute-start(bf16[512,128]{1,0:T(8,128)(2,1)S(1)} %copy-done.2), channel_id=1, source_target_pairs={{1,0},{2,1},{3,2},{4,3},{5,4},{6,5},{7,6},{8,7},{9,8},{10,9},{11,1... | collective-permute-start | bytes 393224 | tf_op jit(solution)/shard_map/ppermute | solution.py:15
  30.1 15.4 %copy-start.1 = (bf16[1,3,512,512]{3,2,1,0:T(8,128)(2,1)S(1)}, bf16[1,3,512,512]{3,2,1,0:T(8,128)(2,1)}, u32[]{:S(2)}) copy-start(bf16[1,3,512,512]{3,2,1,0:T(8,128)(2,1)} %param.5) | copy-start | bytes 4718596
  30.2 13.1 %collective-permute-start.4 = (f32[352,128]{1,0:T(8,128)S(1)}, f32[352,128]{1,0:T(8,128)S(1)}, u32[]{:S(2)}, u32[]{:S(2)}) collective-permute-start(f32[352,128]{1,0:T(8,128)S(1)} %pad_maximum_fusion.3), channel_id=1, source_target_pairs={{0,4},{1,5},{2,6},{3,7},{4,0},{5,1},{6,2},{7,3},{8,12},{9,13},{10,... | collective-permute-start | bytes 540680 | tf_op jit(solution)/shard_map/ppermute | solution.py:23
  43.3 50.5 %copy-start = (bf16[10,512,128]{2,1,0:T(8,128)(2,1)S(1)}, bf16[10,512,128]{2,1,0:T(8,128)(2,1)}, u32[]{:S(2)}) copy-start(bf16[10,512,128]{2,1,0:T(8,128)(2,1)} %param.7) | copy-start | bytes 3932164
  43.4 9.3 %collective-permute-start.5 = (f32[176,128]{1,0:T(8,128)S(1)}, f32[176,128]{1,0:T(8,128)S(1)}, u32[]{:S(2)}, u32[]{:S(2)}) collective-permute-start(f32[176,128]{1,0:T(8,128)S(1)} %pad_maximum_fusion.5), channel_id=1, source_target_pairs={{0,8},{1,9},{2,10},{3,11},{4,12},{5,13},{6,14},{7,15},{8,0},{9,1},... | collective-permute-start | bytes 270344 | tf_op jit(solution)/shard_map/ppermute | solution.py:23
  52.7 4.6 %collective-permute-start.6 = (f32[6,8,128]{2,1,0:T(8,128)S(1)}, f32[6,8,128]{2,1,0:T(8,128)S(1)}, u32[]{:S(2)}, u32[]{:S(2)}) collective-permute-start(f32[6,8,128]{2,1,0:T(8,128)S(1)} %fusion.58), channel_id=1, source_target_pairs={{0,16},{16,0},{32,48},{48,32},{64,80},{80,64},{96,112},{112,96},{1... | collective-permute-start | bytes 73736 | tf_op jit(solution)/shard_map/ppermute | solution.py:23
  57.3 5.4 %collective-permute-start.7 = (f32[5,8,128]{2,1,0:T(8,128)S(1)}, f32[5,8,128]{2,1,0:T(8,128)S(1)}, u32[]{:S(2)}, u32[]{:S(2)}) collective-permute-start(f32[5,8,128]{2,1,0:T(8,128)S(1)} %constant_dynamic-update-slice_fusion.3), channel_id=1, source_target_pairs={{0,32},{16,48},{32,0},{48,16},{64,96},{80,112},{96,64},{112,80},{1... | collective-permute-start | bytes 61448 | tf_op jit(solution)/shard_map/ppermute | solution.py:23
  62.7 8.4 %collective-permute-start.8 = (f32[4,8,128]{2,1,0:T(8,128)S(1)}, f32[4,8,128]{2,1,0:T(8,128)S(1)}, u32[]{:S(2)}, u32[]{:S(2)}) collective-permute-start(f32[4,8,128]{2,1,0:T(8,128)S(1)} %pad_maximum_fusion.6), channel_id=1, source_target_pairs={{0,64},{16,80},{32,96},{48,112},{64,0},{80,16},{96,32},{112,48},{1... | collective-permute-start | bytes 49160 | tf_op jit(solution)/shard_map/ppermute | solution.py:23
  71.1 4.7 %collective-permute-start.9 = (f32[3,8,128]{2,1,0:T(8,128)S(1)}, f32[3,8,128]{2,1,0:T(8,128)S(1)}, u32[]{:S(2)}, u32[]{:S(2)}) collective-permute-start(f32[3,8,128]{2,1,0:T(8,128)S(1)} %pad_maximum_fusion.7), channel_id=1, source_target_pairs={{0,128},{16,144},{32,160},{48,176},{64,192},{80,208},{96,224},{112... | collective-permute-start | bytes 36872 | tf_op jit(solution)/shard_map/ppermute | solution.py:23
  75.9 5.4 %collective-permute-start.10 = (f32[2,8,128]{2,1,0:T(8,128)S(1)}, f32[2,8,128]{2,1,0:T(8,128)S(1)}, u32[]{:S(2)}, u32[]{:S(2)}) collective-permute-start(f32[2,8,128]{2,1,0:T(8,128)S(1)} %pad_maximum_fusion.8), channel_id=1, source_target_pairs={{0,256},{16,272},{32,288},{48,304},{64,320},{80,336},{96,352},{112... | collective-permute-start | bytes 24584 | tf_op jit(solution)/shard_map/ppermute | solution.py:23
  81.3 8.2 %collective-permute-start.11 = (f32[1,8,128]{2,1,0:T(8,128)S(1)}, f32[1,8,128]{2,1,0:T(8,128)S(1)}, u32[]{:S(2)}, u32[]{:S(2)}) collective-permute-start(f32[1,8,128]{2,1,0:T(8,128)S(1)} %slice_add_fusion.1), channel_id=1, source_target_pairs={{0,512},{16,528},{32,544},{48,560},{64,576},{80,592},{96,608},{112... | collective-permute-start | bytes 12296 | tf_op jit(solution)/shard_map/ppermute | solution.py:23
  89.5 8.3 %collective-permute-start.12 = (bf16[6,8,128]{2,1,0:T(8,128)(2,1)S(1)}, bf16[6,8,128]{2,1,0:T(8,128)(2,1)S(1)}, u32[]{:S(2)}, u32[]{:S(2)}) collective-permute-start(bf16[6,8,128]{2,1,0:T(8,128)(2,1)S(1)} %constant_dynamic-update-slice_fusion.8), channel_id=1, source_target_pairs={{0,8},{1,9},{2,10},{3,11},{4,12},{5,13},{6,14},{7,15},{8,0},{9,1},... | collective-permute-start | bytes 36872 | tf_op jit(solution)/shard_map/ppermute | solution.py:23
  97.9 5.5 %collective-permute-start.13 = (bf16[6,16,128]{2,1,0:T(8,128)(2,1)S(1)}, bf16[6,16,128]{2,1,0:T(8,128)(2,1)S(1)}, u32[]{:S(2)}, u32[]{:S(2)}) collective-permute-start(bf16[6,16,128]{2,1,0:T(8,128)(2,1)S(1)} %maximum_select_fusion.3), channel_id=1, source_target_pairs={{0,4},{1,5},{2,6},{3,7},{4,0},{5,1},{6,2},{7,3},{8,12},{9,13},{10,... | collective-permute-start | bytes 73736 | tf_op jit(solution)/shard_map/ppermute | solution.py:23
  103.4 4.8 %collective-permute-start.14 = (bf16[6,32,128]{2,1,0:T(8,128)(2,1)S(1)}, bf16[6,32,128]{2,1,0:T(8,128)(2,1)S(1)}, u32[]{:S(2)}, u32[]{:S(2)}) collective-permute-start(bf16[6,32,128]{2,1,0:T(8,128)(2,1)S(1)} %maximum_select_fusion.2), channel_id=1, source_target_pairs={{0,2},{1,3},{2,0},{3,1},{4,6},{5,7},{6,4},{7,5},{8,10},{9,11},{10,... | collective-permute-start | bytes 147464 | tf_op jit(solution)/shard_map/ppermute | solution.py:23
  108.2 14.6 %collective-permute-start.15 = (bf16[6,64,128]{2,1,0:T(8,128)(2,1)S(1)}, bf16[6,64,128]{2,1,0:T(8,128)(2,1)S(1)}, u32[]{:S(2)}, u32[]{:S(2)}) collective-permute-start(bf16[6,64,128]{2,1,0:T(8,128)(2,1)S(1)} %maximum_select_fusion.1), channel_id=1, source_target_pairs={{0,1},{1,0},{2,3},{3,2},{4,5},{5,4},{6,7},{7,6},{8,9},{9,8},{10,11... | collective-permute-start | bytes 294920 | tf_op jit(solution)/shard_map/ppermute | solution.py:23

commit v2 on v0

v2 whole, which is shorter than its diff:
```python
import jax
import jax.numpy as jnp
from jax import lax
from jax.sharding import PartitionSpec as P


def extended(block, sides, width):
    for axis, dim in sides:
        count = lax.axis_size(axis)
        forward = [(i, i + 1) for i in range(count - 1)]
        backward = [(target, source) for source, target in forward]
        low = lax.ppermute(
            lax.slice_in_dim(block, block.shape[dim] - width, None, axis=dim), axis, forward
        )
        high = lax.ppermute(lax.slice_in_dim(block, 0, width, axis=dim), axis, backward)
        block = jnp.concatenate([low, block, high], axis=dim)
    return block


def body(probes, near_blocks, near_offsets, far_basis):
    leaf_rows = probes.shape[0]
    levels = far_basis.shape[0]
    padded = extended(probes, ((("slab", "leaf"), 0),), leaf_rows)
    near_sum = jnp.zeros(probes.shape, jnp.float32)
    for member in range(near_blocks.shape[1]):
        window_start = (near_offsets[0, member] + 1) * leaf_rows
        window = lax.dynamic_slice_in_dim(padded, window_start, leaf_rows, 0)
        near_sum = near_sum + jnp.dot(
            near_blocks[0, member], window, preferred_element_type=jnp.float32
        )
    projected = jnp.einsum("lpr,pq->lrq", far_basis, probes, preferred_element_type=jnp.float32)
    rank, width = projected.shape[1], projected.shape[2]
    leaves = lax.axis_size("leaf")
    slabs = lax.axis_size("slab")
    leaf_bits = leaves.bit_length() - 1
    slab_bits = levels - leaf_bits
    share = rank // leaves

    parts = lax.all_to_all(
        projected.reshape(levels, leaves, share, width), "leaf", 1, 1, tiled=True
    )
    couplings_low = []
    for level in range(leaf_bits):
        nodes = leaves >> (level + 1)
        grouped = parts[level].reshape(nodes, 2, 2**level, share, width).sum(axis=2)[:, ::-1]
        sibling = jnp.broadcast_to(
            grouped[:, :, None], (nodes, 2, 2**level, share, width)
        ).reshape(leaves, share, width)
        couplings_low.append((sibling * 2.0 ** (-0.5 * level)).astype(jnp.bfloat16))
    totals = parts[leaf_bits:].sum(axis=1)

    slab_index = lax.axis_index("slab")
    relative = jnp.arange(slabs, dtype=jnp.int32)
    distance = jnp.bitwise_xor(relative, slab_index)
    level_of = jnp.zeros_like(distance)
    for bit in range(1, slab_bits):
        level_of = level_of + (distance >= 2**bit).astype(jnp.int32)
    received = lax.all_to_all(jnp.take(totals, level_of, axis=0), "slab", 0, 0, tiled=True)
    by_distance = jnp.take(received, distance, axis=0)
    couplings_high = []
    for step in range(slab_bits):
        level = leaf_bits + step
        sibling = by_distance[2**step : 2 ** (step + 1)].sum(axis=0)
        couplings_high.append((sibling * 2.0 ** (-0.5 * level)).astype(jnp.bfloat16))

    outgoing = jnp.concatenate(
        [
            jnp.stack(couplings_low, axis=1),
            jnp.broadcast_to(jnp.stack(couplings_high)[None], (leaves, slab_bits, share, width)),
        ],
        axis=1,
    )
    coupling = lax.all_to_all(outgoing, "leaf", 0, 0, tiled=True)
    coupling = coupling.transpose(1, 0, 2, 3).reshape(levels, rank, width)
    output = near_sum + jnp.einsum(
        "lpr,lrq->pq", far_basis, coupling, preferred_element_type=jnp.float32
    )
    return output


def solution(mesh):
    return jax.shard_map(
        body,
        mesh=mesh,
        in_specs=(
            P(("slab", "leaf"), None),
            P(("slab", "leaf"), None, None, None),
            P(("slab", "leaf"), None),
            P(None, ("slab", "leaf"), None),
        ),
        out_specs=P(("slab", "leaf"), None),
        check_vma=False,
    )
```

time: 169 us -> 94.3 us (0.56)
  the two profiles are of different devices: /device:TPU:54 before, /device:TPU:1 now
where the time goes in v2:
time: 94.3 us; the launch traced here: 93.8 us
  starting transfers between devices  42.9 us (45%)
  waiting for transfers between devices  29.6 us (31%)
  local copies, waits for them, and re-layouts  11.5 us (12%)
  matrix products  6.35 us (7%)
  between operations  2.18 us (2%)
  other arithmetic  1.23 us (1%)
    all_to_all x1, starting transfers between devices, body(): lax.all_to_all(projected.reshape(levels, leaves, share, width), 'leaf', 1...  17.5 us
    all_to_all x1, starting transfers between devices, body(): lax.all_to_all(jnp.take(totals, level_of, axis=0), 'slab', 0, 0, tiled=True)  13.9 us
    all_to_all x1, waiting for transfers between devices, body(): lax.all_to_all(jnp.take(totals, level_of, axis=0), 'slab', 0, 0, tiled=True)  10.7 us
    ppermute x1, waiting for transfers between devices, extended(): lax.ppermute(lax.slice_in_dim(block, block.shape[dim] - width, None, axis...  7.88 us
    all_to_all x1, waiting for transfers between devices, body(): coupling = lax.all_to_all(outgoing, 'leaf', 0, 0, tiled=True)  7.59 us
    all_to_all x1, starting transfers between devices, body(): coupling = lax.all_to_all(outgoing, 'leaf', 0, 0, tiled=True)  6.07 us
    unnamed x16, local copies, waits for them, and re-layouts  5.51 us
    dot_general x3, matrix products, body(): jnp.dot(near_blocks[0, member], window, preferred_element_type=jnp.float32)  4.35 us
  transfers between devices with their start and end apart: 5, of which 4 were waited for; matrix products, arithmetic and copies ran while one was open for 13% of the time, Pallas kernels for 0%

profile of v2, /device:TPU:1, one launch (start us, length us, event | category | flops | bytes accessed | tf_op | source)
XLA Modules:
  0.0 93.8 jit_solution(9722532812662559418)
XLA Ops:
  0.0 0.0 copy-start
  0.0 1.3 %copy-done = bf16[10,512,128]{2,1,0:T(8,128)(2,1)S(1)} copy-done((bf16[10,512,128]{2,1,0:T(8,128)(2,1)S(1)}, bf16[10,512,128]{2,1,0:T(8,128)(2,1)}, u32[]{:S(2)}) %copy-start) | copy-done | bytes 1310744
  1.3 1.4 %convolution_bitcast_fusion = f32[10,16,8,128]{3,2,1,0:T(8,128)S(1)} fusion(bf16[10,512,128]{2,1,0:T(8,128)(2,1)S(1)} %copy-done, bf16[512,128]{1,0:T(8,128)(2,1)} %param.4), kind=kOutput, calls=%fused_computation.2 | convolution fusion | flops 167772160 | bytes 2097152 | tf_op jit(solution)/shard_map/lpr,pq->lrq/dot_general | solution.py:31
  2.8 0.0 copy-start.3
  2.8 0.0 copy-start.4
  2.8 0.9 copy.12
  3.7 17.5 %all-to-all-start = ((f32[10,16,8,128]{3,2,0,1:T(8,128)}), f32[10,16,8,128]{3,2,0,1:T(8,128)S(1)}, u32[]{:S(2)}, u32[]{:S(2)}) async-start(f32[10,16,8,128]{3,2,0,1:T(8,128)} %copy.12), calls=%async_computation | async-start | bytes 1310720 | tf_op jit(solution)/shard_map/all_to_all | solution.py:39
  21.2 0.0 copy-done.3
  21.2 3.5 %collective-permute-start = (bf16[512,128]{1,0:T(8,128)(2,1)S(1)}, bf16[512,128]{1,0:T(8,128)(2,1)S(1)}, u32[]{:S(2)}, u32[]{:S(2)}) collective-permute-start(bf16[512,128]{1,0:T(8,128)(2,1)S(1)} %copy-done.3), channel_id=1, source_target_pairs={{0,1},{1,2},{2,3},{3,4},{4,5},{5,6},{6,7},{7,8},{8,9},{9,10},{10,1... | collective-permute-start | bytes 393224 | tf_op jit(solution)/shard_map/ppermute | solution.py:12
  24.7 1.9 %collective-permute-start.1 = (bf16[512,128]{1,0:T(8,128)(2,1)S(1)}, bf16[512,128]{1,0:T(8,128)(2,1)}, u32[]{:S(2)}, u32[]{:S(2)}) collective-permute-start(bf16[512,128]{1,0:T(8,128)(2,1)S(1)} %copy-done.3), channel_id=1, source_target_pairs={{1,0},{2,1},{3,2},{4,3},{5,4},{6,5},{7,6},{8,7},{9,8},{10,9},{11,1... | collective-permute-start | bytes 393224 | tf_op jit(solution)/shard_map/ppermute | solution.py:15
  26.7 0.0 copy-done.4
  26.7 0.6 fusion.37
  29.3 7.9 %collective-permute-done = bf16[512,128]{1,0:T(8,128)(2,1)S(1)} collective-permute-done((bf16[512,128]{1,0:T(8,128)(2,1)S(1)}, bf16[512,128]{1,0:T(8,128)(2,1)S(1)}, u32[]{:S(2)}, u32[]{:S(2)}) %collective-permute-start) | collective-permute-done | bytes 131104 | tf_op jit(solution)/shard_map/ppermute | solution.py:12
  37.2 0.6 constant_dynamic-update-slice_fusion.2
  37.8 3.5 %all-to-all-done = f32[10,16,8,128]{3,2,0,1:T(8,128)S(1)} async-done(((f32[10,16,8,128]{3,2,0,1:T(8,128)}), f32[10,16,8,128]{3,2,0,1:T(8,128)S(1)}, u32[]{:S(2)}, u32[]{:S(2)}) %all-to-all-start) | async-done | bytes 655392 | tf_op jit(solution)/shard_map/all_to_all | solution.py:39
  41.3 0.6 gather_fusion
  41.9 0.8 broadcast_select_fusion.1
  42.8 13.9 %all-to-all-start.1 = ((f32[64,8,128]{2,1,0:T(8,128)}), f32[64,8,128]{2,1,0:T(8,128)S(1)}, u32[]{:S(2)}, u32[]{:S(2)}) async-start(f32[64,8,128]{2,1,0:T(8,128)} %broadcast_select_fusion.1), calls=%async_computation.1 | async-start | bytes 524288 | tf_op jit(solution)/shard_map/all_to_all | solution.py:58
  56.8 0.0 copy-start.1
  56.8 0.6 constant_dynamic-update-slice_fusion.12
  57.4 0.6 constant_dynamic-update-slice_fusion.11
  58.1 0.6 constant_dynamic-update-slice_fusion.10
  58.7 0.6 constant_dynamic-update-slice_fusion.9
  59.3 10.7 %all-to-all-done.1 = f32[64,8,128]{2,1,0:T(8,128)S(1)} async-done(((f32[64,8,128]{2,1,0:T(8,128)}), f32[64,8,128]{2,1,0:T(8,128)S(1)}, u32[]{:S(2)}, u32[]{:S(2)}) %all-to-all-start.1) | async-done | bytes 262176 | tf_op jit(solution)/shard_map/all_to_all | solution.py:58
  70.0 0.6 gather_fusion.1
  70.7 0.1 broadcast_select_fusion
  71.0 0.7 broadcast_dynamic-update-slice_fusion
  71.7 6.1 %all-to-all-start.2 = ((bf16[16,10,8,128]{3,2,1,0:T(8,128)(2,1)}), bf16[16,10,8,128]{3,2,1,0:T(8,128)(2,1)S(1)}, u32[]{:S(2)}, u32[]{:S(2)}) async-start(bf16[16,10,8,128]{3,2,1,0:T(8,128)(2,1)} %broadcast_dynamic-update-slice_fusion), calls=%async_computation.2 | async-start | bytes 655360 | tf_op jit(solution)/shard_map/all_to_all | solution.py:73
  77.8 0.7 constant_dynamic-update-slice_fusion.1
  78.4 0.0 collective-permute-done.1
  78.4 1.6 %constant_dynamic-update-slice_fusion = bf16[1536,128]{1,0:T(8,128)(2,1)} fusion(bf16[1536,128]{1,0:T(8,128)(2,1)} %constant_dynamic-update-slice_fusion.1, bf16[512,128]{1,0:T(8,128)(2,1)} %collective-permute-done.1), kind=kLoop, calls=%fused_computation.31 | loop fusion | bytes 262144 | tf_op jit(solution)/shard_map/concatenate | solution.py:16
  80.0 0.0 copy-done.1
  80.0 1.2 %fusion.3 = f32[128,512]{1,0:T(8,128)S(1)} fusion(bf16[1,3,512,512]{3,2,1,0:T(8,128)(2,1)S(1)} %copy-done.1, bf16[1536,128]{1,0:T(8,128)(2,1)} %constant_dynamic-update-slice_fusion, s32[]{:T(128)S(6)} %select_n.50), kind=kOutput, calls=%fused_computation.8 | convolution fusion | flops 67108864 | bytes 917508 | tf_op jit(solution)/shard_map/dot_general | solution.py:28
  81.2 1.9 %fusion.5 = f32[128,512]{1,0:T(8,128)} fusion(bf16[1,3,512,512]{3,2,1,0:T(8,128)(2,1)S(1)} %copy-done.1, bf16[1536,128]{1,0:T(8,128)(2,1)} %constant_dynamic-update-slice_fusion, s32[]{:T(128)S(6)} %select_n.49), kind=kOutput, calls=%fused_computation.10 | convolution fusion | flops 67108864 | bytes 917508 | tf_op jit(solution)/shard_map/dot_general | solution.py:28
  83.2 7.6 %all-to-all-done.2 = bf16[16,10,8,128]{3,2,1,0:T(8,128)(2,1)S(1)} async-done(((bf16[16,10,8,128]{3,2,1,0:T(8,128)(2,1)}), bf16[16,10,8,128]{3,2,1,0:T(8,128)(2,1)S(1)}, u32[]{:S(2)}, u32[]{:S(2)}) %all-to-all-start.2) | async-done | bytes 327712 | tf_op jit(solution)/shard_map/all_to_all | solution.py:73
  90.7 0.0 copy-start.2
  90.7 0.6 convolution_bitcast_fusion.1
  91.3 0.4 copy-done.2
  91.7 1.2 %fusion.2 = f32[512,128]{0,1:T(8,128)S(1)} fusion(f32[128,512]{1,0:T(8,128)S(1)} %convolution_bitcast_fusion.1, f32[128,512]{1,0:T(8,128)S(1)} %fusion.3, f32[128,512]{1,0:T(8,128)S(1)} %copy-done.2, bf16[1,3,512,512]{3,2,1,0:T(8,128)(2,1)S(1)} %copy-done.1, bf16[1536,128]{1,0:T(8,128)(2,1)} %constant_dynamic-update-slice_fusion, s32[]{:T(128)S(6)} %select_n.48), kind=kOutput, calls=%fused_computation.6 | convolution fusion | flops 67305472 | bytes 1703940 | tf_op jit(solution)/shard_map/dot_general | solution.py:28
  92.9 0.8 copy.15
  (30 shorter events, 0.3 us)
Async XLA Ops:
  0.0 1.3 %copy-start = (bf16[10,512,128]{2,1,0:T(8,128)(2,1)S(1)}, bf16[10,512,128]{2,1,0:T(8,128)(2,1)}, u32[]{:S(2)}) copy-start(bf16[10,512,128]{2,1,0:T(8,128)(2,1)} %param.7) | copy-start | bytes 3932164
  2.8 18.4 %copy-start.3 = (bf16[512,128]{1,0:T(8,128)(2,1)S(1)}, bf16[512,128]{1,0:T(8,128)(2,1)}, u32[]{:S(2)}) copy-start(bf16[512,128]{1,0:T(8,128)(2,1)} %param.4) | copy-start | bytes 393220
  2.8 23.9 %copy-start.4 = (s32[1,3]{1,0:T(1,128)S(1)}, s32[1,3]{1,0:T(1,128)}, u32[]{:S(2)}) copy-start(s32[1,3]{1,0:T(1,128)} %param.6) | copy-start | bytes 40
  3.7 37.6 %all-to-all-start = ((f32[10,16,8,128]{3,2,0,1:T(8,128)}), f32[10,16,8,128]{3,2,0,1:T(8,128)S(1)}, u32[]{:S(2)}, u32[]{:S(2)}) async-start(f32[10,16,8,128]{3,2,0,1:T(8,128)} %copy.12), calls=%async_computation | async-start | bytes 1310720 | tf_op jit(solution)/shard_map/all_to_all | solution.py:39
  21.2 16.0 %collective-permute-start = (bf16[512,128]{1,0:T(8,128)(2,1)S(1)}, bf16[512,128]{1,0:T(8,128)(2,1)S(1)}, u32[]{:S(2)}, u32[]{:S(2)}) collective-permute-start(bf16[512,128]{1,0:T(8,128)(2,1)S(1)} %copy-done.3), channel_id=1, source_target_pairs={{0,1},{1,2},{2,3},{3,4},{4,5},{5,6},{6,7},{7,8},{8,9},{9,10},{10,1... | collective-permute-start | bytes 393224 | tf_op jit(solution)/shard_map/ppermute | solution.py:12
  24.7 53.7 %collective-permute-start.1 = (bf16[512,128]{1,0:T(8,128)(2,1)S(1)}, bf16[512,128]{1,0:T(8,128)(2,1)}, u32[]{:S(2)}, u32[]{:S(2)}) collective-permute-start(bf16[512,128]{1,0:T(8,128)(2,1)S(1)} %copy-done.3), channel_id=1, source_target_pairs={{1,0},{2,1},{3,2},{4,3},{5,4},{6,5},{7,6},{8,7},{9,8},{10,9},{11,1... | collective-permute-start | bytes 393224 | tf_op jit(solution)/shard_map/ppermute | solution.py:15
  42.8 27.3 %all-to-all-start.1 = ((f32[64,8,128]{2,1,0:T(8,128)}), f32[64,8,128]{2,1,0:T(8,128)S(1)}, u32[]{:S(2)}, u32[]{:S(2)}) async-start(f32[64,8,128]{2,1,0:T(8,128)} %broadcast_select_fusion.1), calls=%async_computation.1 | async-start | bytes 524288 | tf_op jit(solution)/shard_map/all_to_all | solution.py:58
  56.8 23.2 %copy-start.1 = (bf16[1,3,512,512]{3,2,1,0:T(8,128)(2,1)S(1)}, bf16[1,3,512,512]{3,2,1,0:T(8,128)(2,1)}, u32[]{:S(2)}) copy-start(bf16[1,3,512,512]{3,2,1,0:T(8,128)(2,1)} %param.5) | copy-start | bytes 4718596
  71.7 19.0 %all-to-all-start.2 = ((bf16[16,10,8,128]{3,2,1,0:T(8,128)(2,1)}), bf16[16,10,8,128]{3,2,1,0:T(8,128)(2,1)S(1)}, u32[]{:S(2)}, u32[]{:S(2)}) async-start(bf16[16,10,8,128]{3,2,1,0:T(8,128)(2,1)} %broadcast_dynamic-update-slice_fusion), calls=%async_computation.2 | async-start | bytes 655360 | tf_op jit(solution)/shard_map/all_to_all | solution.py:73
  90.7 1.0 %copy-start.2 = (f32[128,512]{1,0:T(8,128)S(1)}, f32[128,512]{1,0:T(8,128)}, u32[]{:S(2)}) copy-start(f32[128,512]{1,0:T(8,128)} %fusion.5) | copy-start | bytes 786436

commit v3 on v2

v3 whole, which is shorter than its diff:
```python
import jax
import jax.numpy as jnp
from jax import lax
from jax.sharding import PartitionSpec as P


def extended(block, sides, width):
    for axis, dim in sides:
        count = lax.axis_size(axis)
        forward = [(i, i + 1) for i in range(count - 1)]
        backward = [(target, source) for source, target in forward]
        low = lax.ppermute(
            lax.slice_in_dim(block, block.shape[dim] - width, None, axis=dim), axis, forward
        )
        high = lax.ppermute(lax.slice_in_dim(block, 0, width, axis=dim), axis, backward)
        block = jnp.concatenate([low, block, high], axis=dim)
    return block


def body(probes, near_blocks, near_offsets, far_basis):
    leaf_rows = probes.shape[0]
    levels = far_basis.shape[0]
    padded = extended(probes, ((("z", "y", "leaf"), 0),), leaf_rows)
    near_sum = jnp.zeros(probes.shape, jnp.float32)
    for member in range(near_blocks.shape[1]):
        window_start = (near_offsets[0, member] + 1) * leaf_rows
        window = lax.dynamic_slice_in_dim(padded, window_start, leaf_rows, 0)
        near_sum = near_sum + jnp.dot(
            near_blocks[0, member], window, preferred_element_type=jnp.float32
        )
    projected = jnp.einsum("lpr,pq->lrq", far_basis, probes, preferred_element_type=jnp.float32)
    rank, width = projected.shape[1], projected.shape[2]
    leaves = lax.axis_size("leaf")
    leaf_bits = leaves.bit_length() - 1
    slab_bits = levels - leaf_bits
    share = rank // leaves
    shares = projected.reshape(levels, leaves, share, width)

    parts = lax.all_to_all(shares, "leaf", 1, 1, tiled=True)
    couplings_low = []
    for level in range(leaf_bits):
        nodes = leaves >> (level + 1)
        grouped = parts[level].reshape(nodes, 2, 2**level, share, width).sum(axis=2)[:, ::-1]
        sibling = jnp.broadcast_to(
            grouped[:, :, None], (nodes, 2, 2**level, share, width)
        ).reshape(leaves, share, width)
        couplings_low.append((sibling * 2.0 ** (-0.5 * level)).astype(jnp.bfloat16))
    totals = parts[leaf_bits:].sum(axis=1)

    couplings_high = []
    pending = totals
    for axis in SLAB_AXES:
        members = lax.axis_size(axis)
        bits = members.bit_length() - 1
        index = lax.axis_index(axis)
        distance = jnp.bitwise_xor(jnp.arange(members, dtype=jnp.int32), index)
        level_of = jnp.zeros_like(distance)
        for bit in range(1, bits):
            level_of = level_of + (distance >= 2**bit).astype(jnp.int32)
        outgoing = jnp.take(pending[:bits], level_of, axis=0)[:, None]
        if pending.shape[0] > bits:
            rest = jnp.broadcast_to(
                pending[bits:][None], (members,) + pending[bits:].shape
            )
            outgoing = jnp.concatenate([outgoing, rest], axis=1)
        received = lax.all_to_all(outgoing, axis, 0, 0, tiled=True)
        for bit in range(bits):
            level = leaf_bits + len(couplings_high)
            begin = jnp.bitwise_xor(index >> bit, 1) << bit
            sibling = lax.dynamic_slice_in_dim(received[:, 0], begin, 2**bit, 0).sum(axis=0)
            couplings_high.append((sibling * 2.0 ** (-0.5 * level)).astype(jnp.bfloat16))
        pending = received[:, 1:].sum(axis=0)

    high = jnp.stack(couplings_high)
    outgoing = jnp.concatenate(
        [
            jnp.stack(couplings_low, axis=1),
            jnp.broadcast_to(high[None], (leaves,) + high.shape),
        ],
        axis=1,
    )
    coupling = lax.all_to_all(outgoing, "leaf", 0, 0, tiled=True)
    coupling = coupling.transpose(1, 0, 2, 3).reshape(levels, rank, width)
    output = near_sum + jnp.einsum(
        "lpr,lrq->pq", far_basis, coupling, preferred_element_type=jnp.float32
    )
    return output


SLAB_AXES = ("y", "z")


def solution(mesh):
    slabs, leaves = mesh.devices.shape
    inner = 2 ** ((slabs.bit_length() - 1) // 2)
    mesh = jax.sharding.Mesh(
        mesh.devices.reshape(slabs // inner, inner, leaves), ("z", "y", "leaf")
    )
    placed = ("z", "y", "leaf")
    return jax.shard_map(
        body,
        mesh=mesh,
        in_specs=(
            P(placed, None),
            P(placed, None, None, None),
            P(placed, None),
            P(None, placed, None),
        ),
        out_specs=P(placed, None),
        check_vma=False,
    )
```

time: 94.3 us -> 101 us (1.071)
  other arithmetic: 1.23 us -> 8.15 us
  waiting for transfers between devices: 29.6 us -> 24.3 us
  local copies, waits for them, and re-layouts: 11.5 us -> 15.1 us
  starting transfers between devices: 42.9 us -> 44.2 us
    all_to_all x2 -> x3, waiting for transfers between devices: 14.2 us -> 10.8 us  [the longest x2 7.4 us: body(): received = lax.all_to_all(outgoing, axis, 0, 0, tiled=True)]
    reduce_sum x3, other arithmetic: 0.03 us -> 3.15 us  [body(): parts[level].reshape(nodes, 2, 2 ** level, share, width).sum(axis=2)]
    broadcast_in_dim x0 -> x2, other arithmetic: none -> 1.39 us  [body(): outgoing = jnp.take(pending[:bits], level_of, axis=0)[:, None]]
    all_to_all x1, starting transfers between devices: 6.07 us -> 7.35 us  [body(): coupling = lax.all_to_all(outgoing, 'leaf', 0, 0, tiled=True)]
    slice x2, local copies, waits for them, and re-layouts: 0.02 us -> 1.28 us  [body(): parts[level].reshape(nodes, 2, 2 ** level, share, width).sum(axis=2)]
    ppermute x1, waiting for transfers between devices: 7.88 us -> 6.87 us  [extended(): lax.ppermute(lax.slice_in_dim(block, block.shape[dim] - width, None, axis...]
    unnamed x16 -> x14, local copies, waits for them, and re-layouts: 5.51 us -> 6.41 us
    all_to_all x2 -> x3, starting transfers between devices: 31.4 us -> 31.4 us  [the longest x1 17.5 us: body(): parts = lax.all_to_all(shares, 'leaf', 1, 1, tiled=True)]
  transfers between devices with their start and end apart: 5 -> 6, of which waited for: 4 -> 5; matrix products, arithmetic and copies ran while one was open for 13% -> 23% of each run, Pallas kernels for 0% -> 0%
where the time goes in v3:
time: 101 us; the launch traced here: 100 us
  starting transfers between devices  44.2 us (44%)
  waiting for transfers between devices  24.3 us (24%)
  local copies, waits for them, and re-layouts  15.1 us (15%)
  other arithmetic  8.15 us (8%)
  matrix products  6.34 us (6%)
  between operations  2.12 us (2%)
    all_to_all x1, starting transfers between devices, body(): parts = lax.all_to_all(shares, 'leaf', 1, 1, tiled=True)  17.5 us
    all_to_all x2, starting transfers between devices, body(): received = lax.all_to_all(outgoing, axis, 0, 0, tiled=True)  13.9 us
    all_to_all x2, waiting for transfers between devices, body(): received = lax.all_to_all(outgoing, axis, 0, 0, tiled=True)  7.4 us
    all_to_all x1, starting transfers between devices, body(): coupling = lax.all_to_all(outgoing, 'leaf', 0, 0, tiled=True)  7.35 us
    ppermute x1, waiting for transfers between devices, extended(): lax.ppermute(lax.slice_in_dim(block, block.shape[dim] - width, None, axis...  6.87 us
    all_to_all x1, waiting for transfers between devices, body(): coupling = lax.all_to_all(outgoing, 'leaf', 0, 0, tiled=True)  6.69 us
    unnamed x14, local copies, waits for them, and re-layouts  6.41 us
    dot_general x3, matrix products, body(): jnp.dot(near_blocks[0, member], window, preferred_element_type=jnp.float32)  4.34 us
  transfers between devices with their start and end apart: 6, of which 5 were waited for; matrix products, arithmetic and copies ran while one was open for 23% of the time, Pallas kernels for 0%

profile of v3, /device:TPU:1, one launch (start us, length us, event | category | flops | bytes accessed | tf_op | source)
XLA Modules:
  0.0 100.2 jit_solution(707000034792799349)
XLA Ops:
  0.0 0.0 copy-start
  0.0 1.3 %copy-done = bf16[10,512,128]{2,1,0:T(8,128)(2,1)S(1)} copy-done((bf16[10,512,128]{2,1,0:T(8,128)(2,1)S(1)}, bf16[10,512,128]{2,1,0:T(8,128)(2,1)}, u32[]{:S(2)}) %copy-start) | copy-done | bytes 1310744
  1.3 1.4 %convolution_bitcast_fusion = f32[10,16,8,128]{3,2,1,0:T(8,128)S(1)} fusion(bf16[10,512,128]{2,1,0:T(8,128)(2,1)S(1)} %copy-done, bf16[512,128]{1,0:T(8,128)(2,1)} %param.6), kind=kOutput, calls=%fused_computation.2 | convolution fusion | flops 167772160 | bytes 2097152 | tf_op jit(solution)/shard_map/lpr,pq->lrq/dot_general | solution.py:31
  2.8 0.0 copy-start.3
  2.8 0.9 copy.12
  3.6 17.5 %all-to-all-start = ((f32[10,16,8,128]{3,2,0,1:T(8,128)}), f32[10,16,8,128]{3,2,0,1:T(8,128)S(1)}, u32[]{:S(2)}, u32[]{:S(2)}) async-start(f32[10,16,8,128]{3,2,0,1:T(8,128)} %copy.12), calls=%async_computation | async-start | bytes 1310720 | tf_op jit(solution)/shard_map/all_to_all | solution.py:39
  21.1 3.5 %collective-permute-start = (bf16[512,128]{1,0:T(8,128)(2,1)}, bf16[512,128]{1,0:T(8,128)(2,1)S(1)}, u32[]{:S(2)}, u32[]{:S(2)}) collective-permute-start(bf16[512,128]{1,0:T(8,128)(2,1)} %param.6), channel_id=1, source_target_pairs={{0,1},{1,2},{2,3},{3,4},{4,5},{5,6},{6,7},{7,8},{8,9},{9,10},{10,1... | collective-permute-start | bytes 393224 | tf_op jit(solution)/shard_map/ppermute | solution.py:12
  24.7 1.9 %collective-permute-start.1 = (bf16[512,128]{1,0:T(8,128)(2,1)}, bf16[512,128]{1,0:T(8,128)(2,1)}, u32[]{:S(2)}, u32[]{:S(2)}) collective-permute-start(bf16[512,128]{1,0:T(8,128)(2,1)} %param.6), channel_id=1, source_target_pairs={{1,0},{2,1},{3,2},{4,3},{5,4},{6,5},{7,6},{8,7},{9,8},{10,9},{11,1... | collective-permute-start | bytes 393224 | tf_op jit(solution)/shard_map/ppermute | solution.py:15
  26.7 0.0 copy-done.3
  26.7 0.6 fusion.30
  27.3 0.5 compare_and_fusion
  29.8 0.6 pad_clamp_fusion
  30.4 6.9 %collective-permute-done = bf16[512,128]{1,0:T(8,128)(2,1)S(1)} collective-permute-done((bf16[512,128]{1,0:T(8,128)(2,1)}, bf16[512,128]{1,0:T(8,128)(2,1)S(1)}, u32[]{:S(2)}, u32[]{:S(2)}) %collective-permute-start) | collective-permute-done | bytes 131104 | tf_op jit(solution)/shard_map/ppermute | solution.py:12
  37.3 0.6 constant_dynamic-update-slice_fusion.2
  37.9 3.4 %all-to-all-done = f32[10,16,8,128]{3,2,0,1:T(8,128)S(1)} async-done(((f32[10,16,8,128]{3,2,0,1:T(8,128)}), f32[10,16,8,128]{3,2,0,1:T(8,128)S(1)}, u32[]{:S(2)}, u32[]{:S(2)}) %all-to-all-start) | async-done | bytes 655392 | tf_op jit(solution)/shard_map/all_to_all | solution.py:39
  41.3 0.6 gather_fusion
  41.9 0.1 select_bitcast_fusion.1
  42.0 0.7 pad_maximum_fusion
  42.6 4.0 %all-to-all-start.1 = ((f32[8,4,8,128]{3,2,1,0:T(8,128)}), f32[8,4,8,128]{3,2,1,0:T(8,128)}, u32[]{:S(2)}, u32[]{:S(2)}) async-start(f32[8,4,8,128]{3,2,1,0:T(8,128)} %pad_maximum_fusion), calls=%async_computation.1 | async-start | bytes 262144 | tf_op jit(solution)/shard_map/all_to_all | solution.py:66
  46.6 0.0 copy-start.1
  46.7 0.7 fusion.28
  47.3 1.4 %reduce_sum.96 = f32[4,2,8,128]{3,2,1,0:T(8,128)} reduce(f32[4,2,2,8,128]{4,3,2,1,0:T(8,128)} %bitcast.68, f32[]{:T(128)} %constant.24.clone.1), dimensions={2}, to_apply=%region_0.0 | reduce | flops 8192 | bytes 98308 | tf_op jit(solution)/shard_map/reduce_sum | solution.py:43
  48.8 0.8 multiply_convert_fusion
  49.5 0.6 slice.66
  50.1 0.8 rev.16
  50.9 0.6 constant_dynamic-update-slice_fusion.12
  51.5 0.8 reduce_sum.97
  52.4 0.9 reduce_sum.98
  53.2 0.6 constant_dynamic-update-slice_fusion.11
  53.9 0.6 constant_dynamic-update-slice_fusion.10
  54.5 0.6 constant_dynamic-update-slice_fusion.9
  55.1 0.5 all-to-all-done.1
  55.7 0.8 slice.73
  56.5 0.9 slice_reduce_fusion.1
  57.4 0.7 gather_fusion.1
  58.1 1.3 %select_bitcast_fusion = f32[8,1,8,128]{3,2,1,0:T(8,128)} fusion(f32[8,8,128]{2,1,0:T(8,128)S(1)} %gather_fusion.1, pred[8]{0:T(512)(128)(4,1)} %compare_and_fusion), kind=kLoop, calls=%fused_computation.27 | loop fusion | flops 8192 | bytes 65544 | tf_op jit(solution)/shard_map/broadcast_in_dim | solution.py:60
  59.4 9.9 %all-to-all-start.2 = ((f32[8,1,8,128]{3,2,1,0:T(8,128)}), f32[8,1,8,128]{3,2,1,0:T(8,128)S(1)}, u32[]{:S(2)}, u32[]{:S(2)}) async-start(f32[8,1,8,128]{3,2,1,0:T(8,128)} %select_bitcast_fusion), calls=%async_computation.2 | async-start | bytes 65536 | tf_op jit(solution)/shard_map/all_to_all | solution.py:66
  69.3 6.9 %all-to-all-done.2 = f32[8,1,8,128]{3,2,1,0:T(8,128)S(1)} async-done(((f32[8,1,8,128]{3,2,1,0:T(8,128)}), f32[8,1,8,128]{3,2,1,0:T(8,128)S(1)}, u32[]{:S(2)}, u32[]{:S(2)}) %all-to-all-start.2) | async-done | bytes 32800 | tf_op jit(solution)/shard_map/all_to_all | solution.py:66
  76.2 0.7 broadcast_dynamic-update-slice_fusion
  76.9 7.4 %all-to-all-start.3 = ((bf16[16,10,8,128]{3,2,1,0:T(8,128)(2,1)}), bf16[16,10,8,128]{3,2,1,0:T(8,128)(2,1)S(1)}, u32[]{:S(2)}, u32[]{:S(2)}) async-start(bf16[16,10,8,128]{3,2,1,0:T(8,128)(2,1)} %broadcast_dynamic-update-slice_fusion), calls=%async_computation.3 | async-start | bytes 655360 | tf_op jit(solution)/shard_map/all_to_all | solution.py:82
  84.2 1.6 %constant_dynamic-update-slice_fusion.1 = bf16[1536,128]{1,0:T(8,128)(2,1)} fusion(bf16[1536,128]{1,0:T(8,128)(2,1)} %constant_dynamic-update-slice_fusion.2, bf16[512,128]{1,0:T(8,128)(2,1)} %param.6), kind=kLoop, calls=%fused_computation.31 | loop fusion | bytes 262144
  85.8 0.0 collective-permute-done.1
  85.8 1.6 %constant_dynamic-update-slice_fusion = bf16[1536,128]{1,0:T(8,128)(2,1)} fusion(bf16[1536,128]{1,0:T(8,128)(2,1)} %constant_dynamic-update-slice_fusion.1, bf16[512,128]{1,0:T(8,128)(2,1)} %collective-permute-done.1), kind=kLoop, calls=%fused_computation.30 | loop fusion | bytes 262144 | tf_op jit(solution)/shard_map/concatenate | solution.py:16
  87.4 0.0 copy-done.1
  87.4 1.2 %fusion.3 = f32[128,512]{1,0:T(8,128)S(1)} fusion(bf16[1,3,512,512]{3,2,1,0:T(8,128)(2,1)S(1)} %copy-done.1, bf16[1536,128]{1,0:T(8,128)(2,1)} %constant_dynamic-update-slice_fusion, s32[]{:T(128)S(6)} %select_n.36), kind=kOutput, calls=%fused_computation.8 | convolution fusion | flops 67108864 | bytes 917508 | tf_op jit(solution)/shard_map/dot_general | solution.py:28
  88.6 1.9 %fusion.5 = f32[128,512]{1,0:T(8,128)} fusion(bf16[1,3,512,512]{3,2,1,0:T(8,128)(2,1)S(1)} %copy-done.1, bf16[1536,128]{1,0:T(8,128)(2,1)} %constant_dynamic-update-slice_fusion, s32[]{:T(128)S(6)} %select_n.35), kind=kOutput, calls=%fused_computation.10 | convolution fusion | flops 67108864 | bytes 917508 | tf_op jit(solution)/shard_map/dot_general | solution.py:28
  90.5 6.7 %all-to-all-done.3 = bf16[16,10,8,128]{3,2,1,0:T(8,128)(2,1)S(1)} async-done(((bf16[16,10,8,128]{3,2,1,0:T(8,128)(2,1)}), bf16[16,10,8,128]{3,2,1,0:T(8,128)(2,1)S(1)}, u32[]{:S(2)}, u32[]{:S(2)}) %all-to-all-start.3) | async-done | bytes 327712 | tf_op jit(solution)/shard_map/all_to_all | solution.py:82
  97.2 0.0 copy-start.2
  97.2 0.6 convolution_bitcast_fusion.1
  97.8 0.4 copy-done.2
  98.2 1.2 %fusion.2 = f32[512,128]{0,1:T(8,128)S(1)} fusion(f32[128,512]{1,0:T(8,128)S(1)} %convolution_bitcast_fusion.1, f32[128,512]{1,0:T(8,128)S(1)} %fusion.3, f32[128,512]{1,0:T(8,128)S(1)} %copy-done.2, bf16[1,3,512,512]{3,2,1,0:T(8,128)(2,1)S(1)} %copy-done.1, bf16[1536,128]{1,0:T(8,128)(2,1)} %constant_dynamic-update-slice_fusion, s32[]{:T(128)S(6)} %select_n.34), kind=kOutput, calls=%fused_computation.6 | convolution fusion | flops 67305472 | bytes 1703940 | tf_op jit(solution)/shard_map/dot_general | solution.py:28
  99.4 0.8 copy.16
  (22 shorter events, 0.2 us)
Async XLA Ops:
  0.0 1.3 %copy-start = (bf16[10,512,128]{2,1,0:T(8,128)(2,1)S(1)}, bf16[10,512,128]{2,1,0:T(8,128)(2,1)}, u32[]{:S(2)}) copy-start(bf16[10,512,128]{2,1,0:T(8,128)(2,1)} %param.9) | copy-start | bytes 3932164
  2.8 23.9 %copy-start.3 = (s32[1,3]{1,0:T(1,128)S(1)}, s32[1,3]{1,0:T(1,128)}, u32[]{:S(2)}) copy-start(s32[1,3]{1,0:T(1,128)} %param.8) | copy-start | bytes 40
  3.6 37.6 %all-to-all-start = ((f32[10,16,8,128]{3,2,0,1:T(8,128)}), f32[10,16,8,128]{3,2,0,1:T(8,128)S(1)}, u32[]{:S(2)}, u32[]{:S(2)}) async-start(f32[10,16,8,128]{3,2,0,1:T(8,128)} %copy.12), calls=%async_computation | async-start | bytes 1310720 | tf_op jit(solution)/shard_map/all_to_all | solution.py:39
  21.1 16.1 %collective-permute-start = (bf16[512,128]{1,0:T(8,128)(2,1)}, bf16[512,128]{1,0:T(8,128)(2,1)S(1)}, u32[]{:S(2)}, u32[]{:S(2)}) collective-permute-start(bf16[512,128]{1,0:T(8,128)(2,1)} %param.6), channel_id=1, source_target_pairs={{0,1},{1,2},{2,3},{3,4},{4,5},{5,6},{6,7},{7,8},{8,9},{9,10},{10,1... | collective-permute-start | bytes 393224 | tf_op jit(solution)/shard_map/ppermute | solution.py:12
  24.7 61.1 %collective-permute-start.1 = (bf16[512,128]{1,0:T(8,128)(2,1)}, bf16[512,128]{1,0:T(8,128)(2,1)}, u32[]{:S(2)}, u32[]{:S(2)}) collective-permute-start(bf16[512,128]{1,0:T(8,128)(2,1)} %param.6), channel_id=1, source_target_pairs={{1,0},{2,1},{3,2},{4,3},{5,4},{6,5},{7,6},{8,7},{9,8},{10,9},{11,1... | collective-permute-start | bytes 393224 | tf_op jit(solution)/shard_map/ppermute | solution.py:15
  42.6 13.1 %all-to-all-start.1 = ((f32[8,4,8,128]{3,2,1,0:T(8,128)}), f32[8,4,8,128]{3,2,1,0:T(8,128)}, u32[]{:S(2)}, u32[]{:S(2)}) async-start(f32[8,4,8,128]{3,2,1,0:T(8,128)} %pad_maximum_fusion), calls=%async_computation.1 | async-start | bytes 262144 | tf_op jit(solution)/shard_map/all_to_all | solution.py:66
  46.6 40.7 %copy-start.1 = (bf16[1,3,512,512]{3,2,1,0:T(8,128)(2,1)S(1)}, bf16[1,3,512,512]{3,2,1,0:T(8,128)(2,1)}, u32[]{:S(2)}) copy-start(bf16[1,3,512,512]{3,2,1,0:T(8,128)(2,1)} %param.7) | copy-start | bytes 4718596
  59.4 16.7 %all-to-all-start.2 = ((f32[8,1,8,128]{3,2,1,0:T(8,128)}), f32[8,1,8,128]{3,2,1,0:T(8,128)S(1)}, u32[]{:S(2)}, u32[]{:S(2)}) async-start(f32[8,1,8,128]{3,2,1,0:T(8,128)} %select_bitcast_fusion), calls=%async_computation.2 | async-start | bytes 65536 | tf_op jit(solution)/shard_map/all_to_all | solution.py:66
  76.9 20.3 %all-to-all-start.3 = ((bf16[16,10,8,128]{3,2,1,0:T(8,128)(2,1)}), bf16[16,10,8,128]{3,2,1,0:T(8,128)(2,1)S(1)}, u32[]{:S(2)}, u32[]{:S(2)}) async-start(bf16[16,10,8,128]{3,2,1,0:T(8,128)(2,1)} %broadcast_dynamic-update-slice_fusion), calls=%async_computation.3 | async-start | bytes 655360 | tf_op jit(solution)/shard_map/all_to_all | solution.py:82
  97.2 1.0 copy-start.2

commit v4 on v2

v4 whole, which is shorter than its diff:
```python
import jax
import jax.numpy as jnp
from jax import lax
from jax.sharding import PartitionSpec as P

PLACED = ("slab", "x", "core")


def extended(block, sides, width):
    for axis, dim in sides:
        count = lax.axis_size(axis)
        forward = [(i, i + 1) for i in range(count - 1)]
        backward = [(target, source) for source, target in forward]
        low = lax.ppermute(
            lax.slice_in_dim(block, block.shape[dim] - width, None, axis=dim), axis, forward
        )
        high = lax.ppermute(lax.slice_in_dim(block, 0, width, axis=dim), axis, backward)
        block = jnp.concatenate([low, block, high], axis=dim)
    return block


def body(probes, near_blocks, near_offsets, far_basis):
    leaf_rows = probes.shape[0]
    levels = far_basis.shape[0]
    padded = extended(probes, ((PLACED, 0),), leaf_rows)
    near_sum = jnp.zeros(probes.shape, jnp.float32)
    for member in range(near_blocks.shape[1]):
        window_start = (near_offsets[0, member] + 1) * leaf_rows
        window = lax.dynamic_slice_in_dim(padded, window_start, leaf_rows, 0)
        near_sum = near_sum + jnp.dot(
            near_blocks[0, member], window, preferred_element_type=jnp.float32
        )
    projected = jnp.einsum("lpr,pq->lrq", far_basis, probes, preferred_element_type=jnp.float32)
    rank, width = projected.shape[1], projected.shape[2]
    chips = lax.axis_size("x")
    slabs = lax.axis_size("slab")
    leaf_bits = chips.bit_length()
    slab_bits = levels - leaf_bits
    half = rank // 2
    share = half // chips
    core = lax.axis_index("core")
    swap = [(0, 1), (1, 0)]

    keep = lax.dynamic_slice_in_dim(projected[1:], core * half, half, axis=1)
    send = lax.dynamic_slice_in_dim(projected[1:], (1 - core) * half, half, axis=1)
    incoming = lax.ppermute(
        jnp.concatenate([projected[0], send.reshape(-1, width)], axis=0), "core", swap
    )
    coupling_first = (incoming[:rank] * 2.0**0).astype(jnp.bfloat16)
    paired = keep + incoming[rank:].reshape(levels - 1, half, width)

    parts = lax.all_to_all(
        paired.reshape(levels - 1, chips, share, width), "x", 1, 1, tiled=True
    )
    couplings_low = []
    for level in range(1, leaf_bits):
        sub = level - 1
        nodes = chips >> (sub + 1)
        grouped = parts[sub].reshape(nodes, 2, 2**sub, share, width).sum(axis=2)[:, ::-1]
        sibling = jnp.broadcast_to(
            grouped[:, :, None], (nodes, 2, 2**sub, share, width)
        ).reshape(chips, share, width)
        couplings_low.append((sibling * 2.0 ** (-0.5 * level)).astype(jnp.bfloat16))
    totals = parts[leaf_bits - 1 :].sum(axis=1)

    slab_index = lax.axis_index("slab")
    relative = jnp.arange(slabs, dtype=jnp.int32)
    distance = jnp.bitwise_xor(relative, slab_index)
    level_of = jnp.zeros_like(distance)
    for bit in range(1, slab_bits):
        level_of = level_of + (distance >= 2**bit).astype(jnp.int32)
    received = lax.all_to_all(jnp.take(totals, level_of, axis=0), "slab", 0, 0, tiled=True)
    by_distance = jnp.take(received, distance, axis=0)
    couplings_high = []
    for step in range(slab_bits):
        level = leaf_bits + step
        sibling = by_distance[2**step : 2 ** (step + 1)].sum(axis=0)
        couplings_high.append((sibling * 2.0 ** (-0.5 * level)).astype(jnp.bfloat16))

    high = jnp.stack(couplings_high)
    outgoing = jnp.concatenate(
        [
            jnp.stack(couplings_low, axis=1),
            jnp.broadcast_to(high[None], (chips,) + high.shape),
        ],
        axis=1,
    )
    returned = lax.all_to_all(outgoing, "x", 0, 0, tiled=True)
    mine = returned.transpose(1, 0, 2, 3).reshape(levels - 1, half, width)
    other = lax.ppermute(mine, "core", swap)
    coupling_rest = jnp.where(
        core == 0,
        jnp.concatenate([mine, other], axis=1),
        jnp.concatenate([other, mine], axis=1),
    )
    output = near_sum + jnp.dot(far_basis[0], coupling_first, preferred_element_type=jnp.float32)
    output = output + jnp.einsum(
        "lpr,lrq->pq", far_basis[1:], coupling_rest, preferred_element_type=jnp.float32
    )
    return output


def solution(mesh):
    slabs, leaves = mesh.devices.shape
    mesh = jax.sharding.Mesh(mesh.devices.reshape(slabs, leaves // 2, 2), PLACED)
    return jax.shard_map(
        body,
        mesh=mesh,
        in_specs=(
            P(PLACED, None),
            P(PLACED, None, None, None),
            P(PLACED, None),
            P(None, PLACED, None),
        ),
        out_specs=P(PLACED, None),
        check_vma=False,
    )
```

time: 94.3 us -> 95.8 us (1.016)
  local copies, waits for them, and re-layouts: 11.5 us -> 4.64 us
  starting transfers between devices: 42.9 us -> 49.2 us
  waiting for transfers between devices: 29.6 us -> 30.8 us
    all_to_all x2, starting transfers between devices: 23.6 us -> 7.42 us  [the longest x1 4 us: body(): returned = lax.all_to_all(outgoing, 'x', 0, 0, tiled=True)]
    ppermute x1, starting transfers between devices: 1.92 us -> 12.8 us  [extended(): lax.ppermute(lax.slice_in_dim(block, 0, width, axis=dim), axis, backward)]
    ppermute x0 -> x2, starting transfers between devices: none -> 8.38 us  [the longest x1 6.46 us: body(): other = lax.ppermute(mine, 'core', swap)]
    ppermute x1, waiting for transfers between devices: 7.88 us -> 0.01 us  [extended(): lax.ppermute(lax.slice_in_dim(block, block.shape[dim] - width, None, axis...]
    all_to_all x2, waiting for transfers between devices: 11.1 us -> 17.6 us  [the longest x1 10.9 us: body(): lax.all_to_all(paired.reshape(levels - 1, chips, share, width), 'x', 1, 1...]
    unnamed x16 -> x14, local copies, waits for them, and re-layouts: 5.51 us -> 0.06 us
    all_to_all x1, starting transfers between devices: 13.9 us -> 16.1 us  [body(): lax.all_to_all(jnp.take(totals, level_of, axis=0), 'slab', 0, 0, tiled=True)]
    all_to_all x1, waiting for transfers between devices: 10.7 us -> 12.4 us  [body(): lax.all_to_all(jnp.take(totals, level_of, axis=0), 'slab', 0, 0, tiled=True)]
  transfers between devices with their start and end apart: 5 -> 7, of which waited for: 4 -> 4; matrix products, arithmetic and copies ran while one was open for 13% -> 6% of each run, Pallas kernels for 0% -> 0%
where the time goes in v4:
time: 95.8 us; the launch traced here: 95.2 us
  starting transfers between devices  49.2 us (51%)
  waiting for transfers between devices  30.8 us (32%)
  matrix products  6.18 us (6%)
  local copies, waits for them, and re-layouts  4.64 us (5%)
  between operations  2.38 us (2%)
  other arithmetic  1.96 us (2%)
    all_to_all x1, starting transfers between devices, body(): lax.all_to_all(jnp.take(totals, level_of, axis=0), 'slab', 0, 0, tiled=True)  16.1 us
    ppermute x1, starting transfers between devices, extended(): lax.ppermute(lax.slice_in_dim(block, 0, width, axis=dim), axis, backward)  12.8 us
    all_to_all x1, waiting for transfers between devices, body(): lax.all_to_all(jnp.take(totals, level_of, axis=0), 'slab', 0, 0, tiled=True)  12.4 us
    all_to_all x1, waiting for transfers between devices, body(): lax.all_to_all(paired.reshape(levels - 1, chips, share, width), 'x', 1, 1...  10.9 us
    all_to_all x1, waiting for transfers between devices, body(): returned = lax.all_to_all(outgoing, 'x', 0, 0, tiled=True)  6.63 us
    ppermute x1, starting transfers between devices, body(): other = lax.ppermute(mine, 'core', swap)  6.46 us
    ppermute x1, starting transfers between devices, extended(): lax.ppermute(lax.slice_in_dim(block, block.shape[dim] - width, None, axis...  4.49 us
    all_to_all x1, starting transfers between devices, body(): returned = lax.all_to_all(outgoing, 'x', 0, 0, tiled=True)  4 us
  transfers between devices with their start and end apart: 7, of which 4 were waited for; matrix products, arithmetic and copies ran while one was open for 6% of the time, Pallas kernels for 0%

profile of v4, /device:TPU:1, one launch (start us, length us, event | category | flops | bytes accessed | tf_op | source)
XLA Modules:
  0.0 95.2 jit_solution(6540255677522748834)
XLA Ops:
  0.0 4.5 %collective-permute-start = (bf16[512,128]{1,0:T(8,128)(2,1)}, bf16[512,128]{1,0:T(8,128)(2,1)S(1)}, u32[]{:S(2)}, u32[]{:S(2)}) collective-permute-start(bf16[512,128]{1,0:T(8,128)(2,1)} %param.4), channel_id=1, source_target_pairs={{0,1},{1,2},{2,3},{3,4},{4,5},{5,6},{6,7},{7,8},{8,9},{9,10},{10,1... | collective-permute-start | bytes 393224 | tf_op jit(solution)/shard_map/ppermute | solution.py:14
  4.5 12.8 %collective-permute-start.1 = (bf16[512,128]{1,0:T(8,128)(2,1)}, bf16[512,128]{1,0:T(8,128)(2,1)S(1)}, u32[]{:S(2)}, u32[]{:S(2)}) collective-permute-start(bf16[512,128]{1,0:T(8,128)(2,1)} %param.4), channel_id=1, source_target_pairs={{1,0},{2,1},{3,2},{4,3},{5,4},{6,5},{7,6},{8,7},{9,8},{10,9},{11,1... | collective-permute-start | bytes 393224 | tf_op jit(solution)/shard_map/ppermute | solution.py:17
  17.3 1.9 %fusion.25 = f32[10,128,128]{2,1,0:T(8,128)S(1)} fusion(bf16[10,512,128]{2,1,0:T(8,128)(2,1)} %param.7, bf16[512,128]{1,0:T(8,128)(2,1)} %param.4), kind=kOutput, calls=%fused_computation.33 | convolution fusion | flops 167772160 | bytes 2097152 | tf_op jit(solution)/shard_map/lpr,pq->lrq/dot_general | solution.py:33
  19.2 0.0 copy-start.5
  19.3 1.9 %collective-permute-start.2 = (f32[704,128]{1,0:T(8,128)S(1)}, f32[704,128]{1,0:T(8,128)S(1)}, u32[]{:S(2)}, u32[]{:S(2)}) collective-permute-start(f32[704,128]{1,0:T(8,128)S(1)} %pad_maximum_fusion), channel_id=1, source_target_pairs={{0,1},{1,0},{2,3},{3,2},{4,5},{5,4},{6,7},{7,6},{8,9},{9,8},{10,11... | collective-permute-start | bytes 1081352 | tf_op jit(solution)/shard_map/ppermute | solution.py:46
  21.3 0.0 copy-done.5
  21.3 0.7 fusion.52
  22.0 0.9 collective-permute-done.2
  22.9 0.0 copy-start.4
  22.9 0.0 copy-start.3
  23.0 0.7 copy.12
  23.7 3.4 %all-to-all-start = ((f32[9,8,8,128]{3,2,0,1:T(8,128)}), f32[9,8,8,128]{3,2,0,1:T(8,128)S(1)}, u32[]{:S(2)}, u32[]{:S(2)}) async-start(f32[9,8,8,128]{3,2,0,1:T(8,128)} %copy.12), calls=%async_computation | async-start | bytes 589824 | tf_op jit(solution)/shard_map/all_to_all | solution.py:52
  29.1 0.0 copy-done.4
  29.1 0.0 collective-permute-done
  29.2 0.0 copy-done.3
  29.2 0.0 collective-permute-done.1
  29.2 0.0 copy-start.2
  29.2 10.9 %all-to-all-done = f32[9,8,8,128]{3,2,0,1:T(8,128)S(1)} async-done(((f32[9,8,8,128]{3,2,0,1:T(8,128)}), f32[9,8,8,128]{3,2,0,1:T(8,128)S(1)}, u32[]{:S(2)}, u32[]{:S(2)}) %all-to-all-start) | async-done | bytes 294944 | tf_op jit(solution)/shard_map/all_to_all | solution.py:52
  40.2 0.6 gather_fusion
  40.8 0.8 broadcast_select_fusion.1
  41.7 16.1 %all-to-all-start.1 = ((f32[64,8,128]{2,1,0:T(8,128)}), f32[64,8,128]{2,1,0:T(8,128)S(1)}, u32[]{:S(2)}, u32[]{:S(2)}) async-start(f32[64,8,128]{2,1,0:T(8,128)} %broadcast_select_fusion.1), calls=%async_computation.1 | async-start | bytes 524288 | tf_op jit(solution)/shard_map/all_to_all | solution.py:72
  57.8 0.0 copy-start.1
  57.9 12.4 %all-to-all-done.1 = f32[64,8,128]{2,1,0:T(8,128)S(1)} async-done(((f32[64,8,128]{2,1,0:T(8,128)}), f32[64,8,128]{2,1,0:T(8,128)S(1)}, u32[]{:S(2)}, u32[]{:S(2)}) %all-to-all-start.1) | async-done | bytes 262176 | tf_op jit(solution)/shard_map/all_to_all | solution.py:72
  70.3 0.6 gather_fusion.1
  70.9 0.1 broadcast_select_fusion
  71.3 0.0 copy-start
  71.3 0.7 pad_maximum_fusion.1
  72.0 4.0 %all-to-all-start.2 = ((bf16[8,9,8,128]{3,2,1,0:T(8,128)(2,1)}), bf16[8,9,8,128]{3,2,1,0:T(8,128)(2,1)}, u32[]{:S(2)}, u32[]{:S(2)}) async-start(bf16[8,9,8,128]{3,2,1,0:T(8,128)(2,1)} %pad_maximum_fusion.1), calls=%async_computation.2 | async-start | bytes 294912 | tf_op jit(solution)/shard_map/all_to_all | solution.py:88
  76.0 0.0 copy-done.2
  76.0 0.0 copy-done.1
  76.0 0.3 fusion.11
  76.3 1.2 %fusion.9 = f32[128,512]{1,0:T(8,128)S(1)} fusion(bf16[1,3,512,512]{3,2,1,0:T(8,128)(2,1)S(1)} %copy-done.1, bf16[1536,128]{1,0:T(8,128)(2,1)} %copy-done.2, s32[]{:T(128)S(6)} %select_n.64), kind=kOutput, calls=%fused_computation.10 | convolution fusion | flops 67108864 | bytes 917508 | tf_op jit(solution)/shard_map/dot_general | solution.py:30
  77.5 6.6 %all-to-all-done.2 = bf16[8,9,8,128]{3,2,1,0:T(8,128)(2,1)} async-done(((bf16[8,9,8,128]{3,2,1,0:T(8,128)(2,1)}), bf16[8,9,8,128]{3,2,1,0:T(8,128)(2,1)}, u32[]{:S(2)}, u32[]{:S(2)}) %all-to-all-start.2) | async-done | bytes 147488 | tf_op jit(solution)/shard_map/all_to_all | solution.py:88
  84.1 0.9 copy.19
  85.1 6.5 %collective-permute-start.3 = (bf16[9,64,128]{2,1,0:T(8,128)(2,1)S(1)}, bf16[9,64,128]{2,1,0:T(8,128)(2,1)S(1)}, u32[]{:S(2)}, u32[]{:S(2)}) collective-permute-start(bf16[9,64,128]{2,1,0:T(8,128)(2,1)S(1)} %bitcast.66), channel_id=1, source_target_pairs={{0,1},{1,0},{2,3},{3,2},{4,5},{5,4},{6,7},{7,6},{8,9},{9,8},{10,11... | collective-permute-start | bytes 442376 | tf_op jit(solution)/shard_map/ppermute | solution.py:90
  91.6 0.0 copy-done
  91.6 1.0 %fusion.23 = f32[128,512]{1,0:T(8,128)S(1)} fusion(bf16[10,512,128]{2,1,0:T(8,128)(2,1)S(1)} %copy-done, f32[704,128]{1,0:T(8,128)} %copy-done.4), kind=kOutput, calls=%fused_computation.31 | convolution fusion | flops 16777216 | bytes 425984 | tf_op jit(solution)/shard_map/dot_general | solution.py:96
  92.6 0.0 collective-permute-done.3
  92.6 0.5 fusion.6
  93.2 1.2 %fusion.5 = f32[512,128]{0,1:T(8,128)S(1)} fusion(f32[128,512]{1,0:T(8,128)S(1)} %fusion.6, f32[128,512]{1,0:T(8,128)S(1)} %fusion.23, f32[128,512]{1,0:T(8,128)S(1)} %fusion.9, f32[128,512]{1,0:T(8,128)S(1)} %fusion.11, bf16[1,3,512,512]{3,2,1,0:T(8,128)(2,1)S(1)} %copy-done.1, bf16[1536,128]{1,0:T(8,128)(2,1)} %copy-done.2, s32[]{:T(128)S(6)} %select_n.62), kind=kOutput, calls=%fused_computation.8 | convolution fusion | flops 67371008 | bytes 1966084 | tf_op jit(solution)/shard_map/dot_general | solution.py:30
  94.4 0.8 copy.15
  (36 shorter events, 0.5 us)
Async XLA Ops:
  0.0 29.1 %collective-permute-start = (bf16[512,128]{1,0:T(8,128)(2,1)}, bf16[512,128]{1,0:T(8,128)(2,1)S(1)}, u32[]{:S(2)}, u32[]{:S(2)}) collective-permute-start(bf16[512,128]{1,0:T(8,128)(2,1)} %param.4), channel_id=1, source_target_pairs={{0,1},{1,2},{2,3},{3,4},{4,5},{5,6},{6,7},{7,8},{8,9},{9,10},{10,1... | collective-permute-start | bytes 393224 | tf_op jit(solution)/shard_map/ppermute | solution.py:14
  4.5 24.7 %collective-permute-start.1 = (bf16[512,128]{1,0:T(8,128)(2,1)}, bf16[512,128]{1,0:T(8,128)(2,1)S(1)}, u32[]{:S(2)}, u32[]{:S(2)}) collective-permute-start(bf16[512,128]{1,0:T(8,128)(2,1)} %param.4), channel_id=1, source_target_pairs={{1,0},{2,1},{3,2},{4,3},{5,4},{6,5},{7,6},{8,7},{9,8},{10,9},{11,1... | collective-permute-start | bytes 393224 | tf_op jit(solution)/shard_map/ppermute | solution.py:17
  19.2 2.1 %copy-start.5 = (s32[1,3]{1,0:T(1,128)S(1)}, s32[1,3]{1,0:T(1,128)}, u32[]{:S(2)}) copy-start(s32[1,3]{1,0:T(1,128)} %param.6) | copy-start | bytes 40
  19.3 3.6 %collective-permute-start.2 = (f32[704,128]{1,0:T(8,128)S(1)}, f32[704,128]{1,0:T(8,128)S(1)}, u32[]{:S(2)}, u32[]{:S(2)}) collective-permute-start(f32[704,128]{1,0:T(8,128)S(1)} %pad_maximum_fusion), channel_id=1, source_target_pairs={{0,1},{1,0},{2,3},{3,2},{4,5},{5,4},{6,7},{7,6},{8,9},{9,8},{10,11... | collective-permute-start | bytes 1081352 | tf_op jit(solution)/shard_map/ppermute | solution.py:46
  22.9 6.2 %copy-start.4 = (f32[704,128]{1,0:T(8,128)}, f32[704,128]{1,0:T(8,128)S(1)}, u32[]{:S(2)}) copy-start(f32[704,128]{1,0:T(8,128)S(1)} %collective-permute-done.2) | copy-start | bytes 1081348
  22.9 6.2 %copy-start.3 = (bf16[512,128]{1,0:T(8,128)(2,1)S(1)}, bf16[512,128]{1,0:T(8,128)(2,1)}, u32[]{:S(2)}) copy-start(bf16[512,128]{1,0:T(8,128)(2,1)} %param.4) | copy-start | bytes 393220
  23.7 16.4 %all-to-all-start = ((f32[9,8,8,128]{3,2,0,1:T(8,128)}), f32[9,8,8,128]{3,2,0,1:T(8,128)S(1)}, u32[]{:S(2)}, u32[]{:S(2)}) async-start(f32[9,8,8,128]{3,2,0,1:T(8,128)} %copy.12), calls=%async_computation | async-start | bytes 589824 | tf_op jit(solution)/shard_map/all_to_all | solution.py:52
  29.2 46.7 %copy-start.2 = (bf16[1536,128]{1,0:T(8,128)(2,1)}, bf16[1536,128]{1,0:T(8,128)(2,1)S(1)}, u32[]{:S(2)}) copy-start(bf16[1536,128]{1,0:T(8,128)(2,1)S(1)} %constant_dynamic-update-slice_fusion) | copy-start | bytes 1179652
  41.7 28.6 %all-to-all-start.1 = ((f32[64,8,128]{2,1,0:T(8,128)}), f32[64,8,128]{2,1,0:T(8,128)S(1)}, u32[]{:S(2)}, u32[]{:S(2)}) async-start(f32[64,8,128]{2,1,0:T(8,128)} %broadcast_select_fusion.1), calls=%async_computation.1 | async-start | bytes 524288 | tf_op jit(solution)/shard_map/all_to_all | solution.py:72
  57.8 18.2 %copy-start.1 = (bf16[1,3,512,512]{3,2,1,0:T(8,128)(2,1)S(1)}, bf16[1,3,512,512]{3,2,1,0:T(8,128)(2,1)}, u32[]{:S(2)}) copy-start(bf16[1,3,512,512]{3,2,1,0:T(8,128)(2,1)} %param.5) | copy-start | bytes 4718596
  71.3 20.3 %copy-start = (bf16[10,512,128]{2,1,0:T(8,128)(2,1)S(1)}, bf16[10,512,128]{2,1,0:T(8,128)(2,1)}, u32[]{:S(2)}) copy-start(bf16[10,512,128]{2,1,0:T(8,128)(2,1)} %param.7) | copy-start | bytes 3932164
  72.0 12.2 %all-to-all-start.2 = ((bf16[8,9,8,128]{3,2,1,0:T(8,128)(2,1)}), bf16[8,9,8,128]{3,2,1,0:T(8,128)(2,1)}, u32[]{:S(2)}, u32[]{:S(2)}) async-start(bf16[8,9,8,128]{3,2,1,0:T(8,128)(2,1)} %pad_maximum_fusion.1), calls=%async_computation.2 | async-start | bytes 294912 | tf_op jit(solution)/shard_map/all_to_all | solution.py:88
  85.1 7.5 %collective-permute-start.3 = (bf16[9,64,128]{2,1,0:T(8,128)(2,1)S(1)}, bf16[9,64,128]{2,1,0:T(8,128)(2,1)S(1)}, u32[]{:S(2)}, u32[]{:S(2)}) collective-permute-start(bf16[9,64,128]{2,1,0:T(8,128)(2,1)S(1)} %bitcast.66), channel_id=1, source_target_pairs={{0,1},{1,0},{2,3},{3,2},{4,5},{5,4},{6,7},{7,6},{8,9},{9,8},{10,11... | collective-permute-start | bytes 442376 | tf_op jit(solution)/shard_map/ppermute | solution.py:90

commit v5 on v4

--- a/solution.py
+++ b/solution.py
@@ -6,30 +6,9 @@
 PLACED = ("slab", "x", "core")
 
 
-def extended(block, sides, width):
-    for axis, dim in sides:
-        count = lax.axis_size(axis)
-        forward = [(i, i + 1) for i in range(count - 1)]
-        backward = [(target, source) for source, target in forward]
-        low = lax.ppermute(
-            lax.slice_in_dim(block, block.shape[dim] - width, None, axis=dim), axis, forward
-        )
-        high = lax.ppermute(lax.slice_in_dim(block, 0, width, axis=dim), axis, backward)
-        block = jnp.concatenate([low, block, high], axis=dim)
-    return block
-
-
 def body(probes, near_blocks, near_offsets, far_basis):
     leaf_rows = probes.shape[0]
     levels = far_basis.shape[0]
-    padded = extended(probes, ((PLACED, 0),), leaf_rows)
-    near_sum = jnp.zeros(probes.shape, jnp.float32)
-    for member in range(near_blocks.shape[1]):
-        window_start = (near_offsets[0, member] + 1) * leaf_rows
-        window = lax.dynamic_slice_in_dim(padded, window_start, leaf_rows, 0)
-        near_sum = near_sum + jnp.dot(
-            near_blocks[0, member], window, preferred_element_type=jnp.float32
-        )
     projected = jnp.einsum("lpr,pq->lrq", far_basis, probes, preferred_element_type=jnp.float32)
     rank, width = projected.shape[1], projected.shape[2]
     chips = lax.axis_size("x")
@@ -44,10 +23,36 @@
     keep = lax.dynamic_slice_in_dim(projected[1:], core * half, half, axis=1)
     send = lax.dynamic_slice_in_dim(projected[1:], (1 - core) * half, half, axis=1)
     incoming = lax.ppermute(
-        jnp.concatenate([projected[0], send.reshape(-1, width)], axis=0), "core", swap
+        jnp.concatenate(
+            [projected[0], send.reshape(-1, width), probes.astype(jnp.float32)], axis=0
+        ),
+        "core",
+        swap,
     )
     coupling_first = (incoming[:rank] * 2.0**0).astype(jnp.bfloat16)
-    paired = keep + incoming[rank:].reshape(levels - 1, half, width)
+    paired = keep + incoming[rank : rank + (levels - 1) * half].reshape(levels - 1, half, width)
+
+    partner = incoming[rank + (levels - 1) * half :].astype(probes.dtype)
+    devices = slabs * chips * 2
+    pairs = []
+    for odd in range(1, devices - 1, 2):
+        pairs += [(odd, odd + 1), (odd + 1, odd)]
+    across = lax.ppermute(probes, PLACED, pairs)
+    padded = jnp.concatenate(
+        [
+            jnp.where(core == 0, across, partner),
+            probes,
+            jnp.where(core == 0, partner, across),
+        ],
+        axis=0,
+    )
+    near_sum = jnp.zeros(probes.shape, jnp.float32)
+    for member in range(near_blocks.shape[1]):
+        window_start = (near_offsets[0, member] + 1) * leaf_rows
+        window = lax.dynamic_slice_in_dim(padded, window_start, leaf_rows, 0)
+        near_sum = near_sum + jnp.dot(
+            near_blocks[0, member], window, preferred_element_type=jnp.float32
+        )
 
     parts = lax.all_to_all(
         paired.reshape(levels - 1, chips, share, width), "x", 1, 1, tiled=True

time: 95.8 us -> 93.1 us (0.972)
  starting transfers between devices: 49.2 us -> 45.5 us
  matrix products: 6.18 us -> 4.29 us
  waiting for transfers between devices: 30.8 us -> 32.2 us
  other arithmetic: 1.96 us -> 2.99 us
    ppermute x3 -> x2, starting transfers between devices: 19.2 us -> 16.7 us  [the longest x1 12.2 us: body(): lax.ppermute(jnp.concatenate([projected[0], send.reshape(-1, width), prob...]
    dot_general x3, matrix products: 2.76 us -> 0.94 us  [body(): jnp.dot(near_blocks[0, member], window, preferred_element_type=jnp.float32)]
  transfers between devices with their start and end apart: 7 -> 6, of which waited for: 4 -> 5; matrix products, arithmetic and copies ran while one was open for 6% -> 6% of each run, Pallas kernels for 0% -> 0%
where the time goes in v5:
time: 93.1 us; the launch traced here: 92.5 us
  starting transfers between devices  45.5 us (49%)
  waiting for transfers between devices  32.2 us (35%)
  local copies, waits for them, and re-layouts  5.16 us (6%)
  matrix products  4.29 us (5%)
  other arithmetic  2.99 us (3%)
  between operations  2.32 us (2%)
    all_to_all x1, starting transfers between devices, body(): lax.all_to_all(jnp.take(totals, level_of, axis=0), 'slab', 0, 0, tiled=True)  15.5 us
    all_to_all x1, waiting for transfers between devices, body(): lax.all_to_all(jnp.take(totals, level_of, axis=0), 'slab', 0, 0, tiled=True)  12.9 us
    ppermute x1, starting transfers between devices, body(): lax.ppermute(jnp.concatenate([projected[0], send.reshape(-1, width), prob...  12.2 us
    all_to_all x1, waiting for transfers between devices, body(): lax.all_to_all(paired.reshape(levels - 1, chips, share, width), 'x', 1, 1...  10.3 us
    all_to_all x1, waiting for transfers between devices, body(): returned = lax.all_to_all(outgoing, 'x', 0, 0, tiled=True)  7.42 us
    ppermute x1, starting transfers between devices, body(): other = lax.ppermute(mine, 'core', swap)  5.96 us
    ppermute x1, starting transfers between devices, body(): across = lax.ppermute(probes, PLACED, pairs)  4.49 us
    all_to_all x1, starting transfers between devices, body(): returned = lax.all_to_all(outgoing, 'x', 0, 0, tiled=True)  4 us
  transfers between devices with their start and end apart: 6, of which 5 were waited for; matrix products, arithmetic and copies ran while one was open for 6% of the time, Pallas kernels for 0%

profile of v5, /device:TPU:1, one launch (start us, length us, event | category | flops | bytes accessed | tf_op | source)
XLA Modules:
  0.0 92.5 jit_solution(2165400619056696518)
XLA Ops:
  0.0 4.5 %collective-permute-start = (bf16[512,128]{1,0:T(8,128)(2,1)}, bf16[512,128]{1,0:T(8,128)(2,1)S(1)}, u32[]{:S(2)}, u32[]{:S(2)}) collective-permute-start(bf16[512,128]{1,0:T(8,128)(2,1)} %param.4), channel_id=1, source_target_pairs={{1,2},{2,1},{3,4},{4,3},{5,6},{6,5},{7,8},{8,7},{9,10},{10,9},{11,... | collective-permute-start | bytes 393224 | tf_op jit(solution)/shard_map/ppermute | solution.py:40
  4.5 0.9 %convert_element_type.185 = f32[512,128]{1,0:T(8,128)S(1)} convert(bf16[512,128]{1,0:T(8,128)(2,1)} %param.4) | non-fusion elementwise | flops 65536 | bytes 393216 | tf_op jit(solution)/shard_map/convert_element_type | solution.py:27
  5.4 1.9 %fusion.21 = f32[10,128,128]{2,1,0:T(8,128)S(1)} fusion(bf16[10,512,128]{2,1,0:T(8,128)(2,1)} %param.7, bf16[512,128]{1,0:T(8,128)(2,1)} %param.4), kind=kOutput, calls=%fused_computation.32 | convolution fusion | flops 167772160 | bytes 2097152 | tf_op jit(solution)/shard_map/lpr,pq->lrq/dot_general | solution.py:12
  7.3 0.0 copy-start.4
  7.5 12.2 %collective-permute-start.1 = (f32[1216,128]{1,0:T(8,128)S(1)}, f32[1216,128]{1,0:T(8,128)S(1)}, u32[]{:S(2)}, u32[]{:S(2)}) collective-permute-start(f32[1216,128]{1,0:T(8,128)S(1)} %pad_maximum_fusion), channel_id=1, source_target_pairs={{0,1},{1,0},{2,3},{3,2},{4,5},{5,4},{6,7},{7,6},{8,9},{9,8},{10,11... | collective-permute-start | bytes 1867784 | tf_op jit(solution)/shard_map/ppermute | solution.py:25
  19.7 0.0 copy-done.4
  19.7 0.6 fusion.49
  20.3 1.0 %collective-permute-done.1 = f32[1216,128]{1,0:T(8,128)S(1)} collective-permute-done((f32[1216,128]{1,0:T(8,128)S(1)}, f32[1216,128]{1,0:T(8,128)S(1)}, u32[]{:S(2)}, u32[]{:S(2)}) %collective-permute-start.1) | collective-permute-done | bytes 622624 | tf_op jit(solution)/shard_map/ppermute | solution.py:25
  21.4 0.0 copy-start.2
  21.4 0.7 copy.12
  22.1 3.4 %all-to-all-start = ((f32[9,8,8,128]{3,2,0,1:T(8,128)}), f32[9,8,8,128]{3,2,0,1:T(8,128)S(1)}, u32[]{:S(2)}, u32[]{:S(2)}) async-start(f32[9,8,8,128]{3,2,0,1:T(8,128)} %copy.12), calls=%async_computation | async-start | bytes 589824 | tf_op jit(solution)/shard_map/all_to_all | solution.py:57
  27.5 0.0 copy-start.3
  27.5 0.0 collective-permute-done
  27.6 0.7 copy-done.3
  28.2 0.0 copy-done.2
  28.3 10.3 %all-to-all-done = f32[9,8,8,128]{3,2,0,1:T(8,128)S(1)} async-done(((f32[9,8,8,128]{3,2,0,1:T(8,128)}), f32[9,8,8,128]{3,2,0,1:T(8,128)S(1)}, u32[]{:S(2)}, u32[]{:S(2)}) %all-to-all-start) | async-done | bytes 294944 | tf_op jit(solution)/shard_map/all_to_all | solution.py:57
  38.5 0.6 gather_fusion
  39.2 0.8 broadcast_select_fusion.1
  40.0 15.5 %all-to-all-start.1 = ((f32[64,8,128]{2,1,0:T(8,128)}), f32[64,8,128]{2,1,0:T(8,128)S(1)}, u32[]{:S(2)}, u32[]{:S(2)}) async-start(f32[64,8,128]{2,1,0:T(8,128)} %broadcast_select_fusion.1), calls=%async_computation.1 | async-start | bytes 524288 | tf_op jit(solution)/shard_map/all_to_all | solution.py:77
  55.5 0.0 copy-start.1
  55.6 12.9 %all-to-all-done.1 = f32[64,8,128]{2,1,0:T(8,128)S(1)} async-done(((f32[64,8,128]{2,1,0:T(8,128)}), f32[64,8,128]{2,1,0:T(8,128)S(1)}, u32[]{:S(2)}, u32[]{:S(2)}) %all-to-all-start.1) | async-done | bytes 262176 | tf_op jit(solution)/shard_map/all_to_all | solution.py:77
  68.5 0.6 gather_fusion.1
  69.1 0.1 broadcast_select_fusion
  69.4 0.7 pad_maximum_fusion.2
  70.1 4.0 %all-to-all-start.2 = ((bf16[8,9,8,128]{3,2,1,0:T(8,128)(2,1)}), bf16[8,9,8,128]{3,2,1,0:T(8,128)(2,1)}, u32[]{:S(2)}, u32[]{:S(2)}) async-start(bf16[8,9,8,128]{3,2,1,0:T(8,128)(2,1)} %pad_maximum_fusion.2), calls=%async_computation.2 | async-start | bytes 294912 | tf_op jit(solution)/shard_map/all_to_all | solution.py:93
  74.1 0.0 copy-done.1
  74.1 0.3 fusion.8
  74.5 0.0 copy-start
  74.5 0.3 convolution_add_fusion.2
  74.8 7.4 %all-to-all-done.2 = bf16[8,9,8,128]{3,2,1,0:T(8,128)(2,1)} async-done(((bf16[8,9,8,128]{3,2,1,0:T(8,128)(2,1)}), bf16[8,9,8,128]{3,2,1,0:T(8,128)(2,1)}, u32[]{:S(2)}, u32[]{:S(2)}) %all-to-all-start.2) | async-done | bytes 147488 | tf_op jit(solution)/shard_map/all_to_all | solution.py:93
  82.2 0.9 %copy.19 = bf16[8,9,8,128]{3,2,0,1:T(8,128)(2,1)S(1)} copy(bf16[8,9,8,128]{3,2,1,0:T(8,128)(2,1)} %all-to-all-done.2) | data formatting | bytes 294912 | tf_op jit(solution)/shard_map/all_to_all | solution.py:93
  83.2 6.0 %collective-permute-start.2 = (bf16[9,64,128]{2,1,0:T(8,128)(2,1)S(1)}, bf16[9,64,128]{2,1,0:T(8,128)(2,1)S(1)}, u32[]{:S(2)}, u32[]{:S(2)}) collective-permute-start(bf16[9,64,128]{2,1,0:T(8,128)(2,1)S(1)} %bitcast.66), channel_id=1, source_target_pairs={{0,1},{1,0},{2,3},{3,2},{4,5},{5,4},{6,7},{7,6},{8,9},{9,8},{10,11... | collective-permute-start | bytes 442376 | tf_op jit(solution)/shard_map/ppermute | solution.py:95
  89.1 0.3 convolution_add_fusion.1
  89.5 0.7 collective-permute-done.2
  90.1 0.0 copy-done
  90.1 0.5 fusion.4
  90.7 1.0 %fusion.3 = f32[512,128]{0,1:T(8,128)S(1)} fusion(f32[128,512]{1,0:T(8,128)S(1)} %fusion.4, f32[128,512]{1,0:T(8,128)S(1)} %convolution_add_fusion.1, bf16[10,512,128]{2,1,0:T(8,128)(2,1)S(1)} %copy-done, bf16[1216,128]{1,0:T(8,128)(2,1)} %copy-done.3), kind=kOutput, calls=%fused_computation.6 | convolution fusion | flops 16908288 | bytes 950272 | tf_op jit(solution)/shard_map/dot_general | solution.py:101
  91.6 0.8 copy.15
  (36 shorter events, 0.5 us)
Async XLA Ops:
  0.0 27.5 %collective-permute-start = (bf16[512,128]{1,0:T(8,128)(2,1)}, bf16[512,128]{1,0:T(8,128)(2,1)S(1)}, u32[]{:S(2)}, u32[]{:S(2)}) collective-permute-start(bf16[512,128]{1,0:T(8,128)(2,1)} %param.4), channel_id=1, source_target_pairs={{1,2},{2,1},{3,4},{4,3},{5,6},{6,5},{7,8},{8,7},{9,10},{10,9},{11,... | collective-permute-start | bytes 393224 | tf_op jit(solution)/shard_map/ppermute | solution.py:40
  7.3 12.4 %copy-start.4 = (s32[1,3]{1,0:T(1,128)S(1)}, s32[1,3]{1,0:T(1,128)}, u32[]{:S(2)}) copy-start(s32[1,3]{1,0:T(1,128)} %param.6) | copy-start | bytes 40
  7.5 13.8 %collective-permute-start.1 = (f32[1216,128]{1,0:T(8,128)S(1)}, f32[1216,128]{1,0:T(8,128)S(1)}, u32[]{:S(2)}, u32[]{:S(2)}) collective-permute-start(f32[1216,128]{1,0:T(8,128)S(1)} %pad_maximum_fusion), channel_id=1, source_target_pairs={{0,1},{1,0},{2,3},{3,2},{4,5},{5,4},{6,7},{7,6},{8,9},{9,8},{10,11... | collective-permute-start | bytes 1867784 | tf_op jit(solution)/shard_map/ppermute | solution.py:25
  21.4 6.9 %copy-start.2 = (bf16[512,128]{1,0:T(8,128)(2,1)S(1)}, bf16[512,128]{1,0:T(8,128)(2,1)}, u32[]{:S(2)}) copy-start(bf16[512,128]{1,0:T(8,128)(2,1)} %param.4) | copy-start | bytes 393220
  22.1 16.4 %all-to-all-start = ((f32[9,8,8,128]{3,2,0,1:T(8,128)}), f32[9,8,8,128]{3,2,0,1:T(8,128)S(1)}, u32[]{:S(2)}, u32[]{:S(2)}) async-start(f32[9,8,8,128]{3,2,0,1:T(8,128)} %copy.12), calls=%async_computation | async-start | bytes 589824 | tf_op jit(solution)/shard_map/all_to_all | solution.py:57
  27.5 0.7 copy-start.3
  40.0 28.4 %all-to-all-start.1 = ((f32[64,8,128]{2,1,0:T(8,128)}), f32[64,8,128]{2,1,0:T(8,128)S(1)}, u32[]{:S(2)}, u32[]{:S(2)}) async-start(f32[64,8,128]{2,1,0:T(8,128)} %broadcast_select_fusion.1), calls=%async_computation.1 | async-start | bytes 524288 | tf_op jit(solution)/shard_map/all_to_all | solution.py:77
  55.5 18.6 %copy-start.1 = (bf16[1,3,512,512]{3,2,1,0:T(8,128)(2,1)S(1)}, bf16[1,3,512,512]{3,2,1,0:T(8,128)(2,1)}, u32[]{:S(2)}) copy-start(bf16[1,3,512,512]{3,2,1,0:T(8,128)(2,1)} %param.5) | copy-start | bytes 4718596
  70.1 12.1 %all-to-all-start.2 = ((bf16[8,9,8,128]{3,2,1,0:T(8,128)(2,1)}), bf16[8,9,8,128]{3,2,1,0:T(8,128)(2,1)}, u32[]{:S(2)}, u32[]{:S(2)}) async-start(bf16[8,9,8,128]{3,2,1,0:T(8,128)(2,1)} %pad_maximum_fusion.2), calls=%async_computation.2 | async-start | bytes 294912 | tf_op jit(solution)/shard_map/all_to_all | solution.py:93
  74.5 15.7 %copy-start = (bf16[10,512,128]{2,1,0:T(8,128)(2,1)S(1)}, bf16[10,512,128]{2,1,0:T(8,128)(2,1)}, u32[]{:S(2)}) copy-start(bf16[10,512,128]{2,1,0:T(8,128)(2,1)} %param.7) | copy-start | bytes 3932164
  83.2 6.9 %collective-permute-start.2 = (bf16[9,64,128]{2,1,0:T(8,128)(2,1)S(1)}, bf16[9,64,128]{2,1,0:T(8,128)(2,1)S(1)}, u32[]{:S(2)}, u32[]{:S(2)}) collective-permute-start(bf16[9,64,128]{2,1,0:T(8,128)(2,1)S(1)} %bitcast.66), channel_id=1, source_target_pairs={{0,1},{1,0},{2,3},{3,2},{4,5},{5,4},{6,7},{7,6},{8,9},{9,8},{10,11... | collective-permute-start | bytes 442376 | tf_op jit(solution)/shard_map/ppermute | solution.py:95

commit v6 on v5

--- a/solution.py
+++ b/solution.py
@@ -90,13 +90,14 @@
         ],
         axis=1,
     )
-    returned = lax.all_to_all(outgoing, "x", 0, 0, tiled=True)
-    mine = returned.transpose(1, 0, 2, 3).reshape(levels - 1, half, width)
-    other = lax.ppermute(mine, "core", swap)
-    coupling_rest = jnp.where(
-        core == 0,
-        jnp.concatenate([mine, other], axis=1),
-        jnp.concatenate([other, mine], axis=1),
+    everyone = jnp.broadcast_to(outgoing[:, None], (chips, 2) + outgoing.shape[1:])
+    returned = lax.all_to_all(
+        everyone.reshape((chips * 2,) + outgoing.shape[1:]), ("x", "core"), 0, 0, tiled=True
+    )
+    coupling_rest = (
+        returned.reshape((chips, 2) + outgoing.shape[1:])
+        .transpose(2, 1, 0, 3, 4)
+        .reshape(levels - 1, rank, width)
     )
     output = near_sum + jnp.dot(far_basis[0], coupling_first, preferred_element_type=jnp.float32)
     output = output + jnp.einsum(

time: 93.1 us -> 93.7 us (level)
  waiting for transfers between devices: 32.2 us -> 35.8 us
  starting transfers between devices: 45.5 us -> 42.4 us
    ppermute x1 -> x0, starting transfers between devices: 5.96 us -> none  [body(): other = lax.ppermute(mine, 'core', swap)]
    all_to_all x1, waiting for transfers between devices: 7.42 us -> 11.7 us  [body(): lax.all_to_all(everyone.reshape((chips * 2,) + outgoing.shape[1:]), ('x',...]
    all_to_all x1, starting transfers between devices: 4 us -> 6.82 us  [body(): lax.all_to_all(everyone.reshape((chips * 2,) + outgoing.shape[1:]), ('x',...]
    transpose x0 -> x1, local copies, waits for them, and re-layouts: none -> 1.03 us  [body(): coupling_rest = returned.reshape((chips, 2) + outgoing.shape[1:]).transpo...]
  transfers between devices with their start and end apart: 6 -> 5, of which waited for: 5 -> 4; matrix products, arithmetic and copies ran while one was open for 6% -> 6% of each run, Pallas kernels for 0% -> 0%
where the time goes in v6:
time: 93.7 us; the launch traced here: 93.1 us
  starting transfers between devices  42.4 us (45%)
  waiting for transfers between devices  35.8 us (38%)
  local copies, waits for them, and re-layouts  6.02 us (6%)
  matrix products  4.29 us (5%)
  other arithmetic  2.33 us (2%)
  between operations  2.32 us (2%)
    all_to_all x1, starting transfers between devices, body(): lax.all_to_all(jnp.take(totals, level_of, axis=0), 'slab', 0, 0, tiled=True)  15.5 us
    all_to_all x1, waiting for transfers between devices, body(): lax.all_to_all(jnp.take(totals, level_of, axis=0), 'slab', 0, 0, tiled=True)  12.9 us
    ppermute x1, starting transfers between devices, body(): lax.ppermute(jnp.concatenate([projected[0], send.reshape(-1, width), prob...  12.2 us
    all_to_all x1, waiting for transfers between devices, body(): lax.all_to_all(everyone.reshape((chips * 2,) + outgoing.shape[1:]), ('x',...  11.7 us
    all_to_all x1, waiting for transfers between devices, body(): lax.all_to_all(paired.reshape(levels - 1, chips, share, width), 'x', 1, 1...  10.3 us
    all_to_all x1, starting transfers between devices, body(): lax.all_to_all(everyone.reshape((chips * 2,) + outgoing.shape[1:]), ('x',...  6.82 us
    ppermute x1, starting transfers between devices, body(): across = lax.ppermute(probes, PLACED, pairs)  4.49 us
    all_to_all x1, starting transfers between devices, body(): lax.all_to_all(paired.reshape(levels - 1, chips, share, width), 'x', 1, 1...  3.42 us
  transfers between devices with their start and end apart: 5, of which 4 were waited for; matrix products, arithmetic and copies ran while one was open for 6% of the time, Pallas kernels for 0%

profile of v6, /device:TPU:1, one launch (start us, length us, event | category | flops | bytes accessed | tf_op | source)
XLA Modules:
  0.0 93.1 jit_solution(17242107235221207589)
XLA Ops:
  0.0 4.5 %collective-permute-start = (bf16[512,128]{1,0:T(8,128)(2,1)}, bf16[512,128]{1,0:T(8,128)(2,1)S(1)}, u32[]{:S(2)}, u32[]{:S(2)}) collective-permute-start(bf16[512,128]{1,0:T(8,128)(2,1)} %param.4), channel_id=1, source_target_pairs={{1,2},{2,1},{3,4},{4,3},{5,6},{6,5},{7,8},{8,7},{9,10},{10,9},{11,... | collective-permute-start | bytes 393224 | tf_op jit(solution)/shard_map/ppermute | solution.py:40
  4.5 0.9 %convert_element_type.185 = f32[512,128]{1,0:T(8,128)S(1)} convert(bf16[512,128]{1,0:T(8,128)(2,1)} %param.4) | non-fusion elementwise | flops 65536 | bytes 393216 | tf_op jit(solution)/shard_map/convert_element_type | solution.py:27
  5.4 1.9 %fusion.15 = f32[10,128,128]{2,1,0:T(8,128)S(1)} fusion(bf16[10,512,128]{2,1,0:T(8,128)(2,1)} %param.7, bf16[512,128]{1,0:T(8,128)(2,1)} %param.4), kind=kOutput, calls=%fused_computation.24 | convolution fusion | flops 167772160 | bytes 2097152 | tf_op jit(solution)/shard_map/lpr,pq->lrq/dot_general | solution.py:12
  7.3 0.0 copy-start.4
  7.5 12.2 %collective-permute-start.1 = (f32[1216,128]{1,0:T(8,128)S(1)}, f32[1216,128]{1,0:T(8,128)S(1)}, u32[]{:S(2)}, u32[]{:S(2)}) collective-permute-start(f32[1216,128]{1,0:T(8,128)S(1)} %pad_maximum_fusion), channel_id=1, source_target_pairs={{0,1},{1,0},{2,3},{3,2},{4,5},{5,4},{6,7},{7,6},{8,9},{9,8},{10,11... | collective-permute-start | bytes 1867784 | tf_op jit(solution)/shard_map/ppermute | solution.py:25
  19.7 0.0 copy-done.4
  19.7 0.6 fusion.42
  20.3 1.0 %collective-permute-done.1 = f32[1216,128]{1,0:T(8,128)S(1)} collective-permute-done((f32[1216,128]{1,0:T(8,128)S(1)}, f32[1216,128]{1,0:T(8,128)S(1)}, u32[]{:S(2)}, u32[]{:S(2)}) %collective-permute-start.1) | collective-permute-done | bytes 622624 | tf_op jit(solution)/shard_map/ppermute | solution.py:25
  21.4 0.0 copy-start.2
  21.4 0.7 copy.16
  22.1 3.4 %all-to-all-start = ((f32[9,8,8,128]{3,2,0,1:T(8,128)}), f32[9,8,8,128]{3,2,0,1:T(8,128)S(1)}, u32[]{:S(2)}, u32[]{:S(2)}) async-start(f32[9,8,8,128]{3,2,0,1:T(8,128)} %copy.16), calls=%async_computation | async-start | bytes 589824 | tf_op jit(solution)/shard_map/all_to_all | solution.py:57
  27.5 0.0 copy-start.3
  27.5 0.0 collective-permute-done
  27.6 0.7 copy-done.3
  28.2 0.0 copy-done.2
  28.3 10.3 %all-to-all-done = f32[9,8,8,128]{3,2,0,1:T(8,128)S(1)} async-done(((f32[9,8,8,128]{3,2,0,1:T(8,128)}), f32[9,8,8,128]{3,2,0,1:T(8,128)S(1)}, u32[]{:S(2)}, u32[]{:S(2)}) %all-to-all-start) | async-done | bytes 294944 | tf_op jit(solution)/shard_map/all_to_all | solution.py:57
  38.5 0.6 gather_fusion
  39.2 0.8 broadcast_select_fusion.1
  40.0 15.5 %all-to-all-start.1 = ((f32[64,8,128]{2,1,0:T(8,128)}), f32[64,8,128]{2,1,0:T(8,128)S(1)}, u32[]{:S(2)}, u32[]{:S(2)}) async-start(f32[64,8,128]{2,1,0:T(8,128)} %broadcast_select_fusion.1), calls=%async_computation.1 | async-start | bytes 524288 | tf_op jit(solution)/shard_map/all_to_all | solution.py:77
  55.6 0.0 copy-start.1
  55.6 12.9 %all-to-all-done.1 = f32[64,8,128]{2,1,0:T(8,128)S(1)} async-done(((f32[64,8,128]{2,1,0:T(8,128)}), f32[64,8,128]{2,1,0:T(8,128)S(1)}, u32[]{:S(2)}, u32[]{:S(2)}) %all-to-all-start.1) | async-done | bytes 262176 | tf_op jit(solution)/shard_map/all_to_all | solution.py:77
  68.5 0.6 gather_fusion.1
  69.1 0.1 broadcast_select_fusion
  69.5 0.8 broadcast_in_dim.48
  70.2 6.8 %all-to-all-start.2 = ((bf16[16,9,8,128]{3,2,1,0:T(8,128)(2,1)}), bf16[16,9,8,128]{3,2,1,0:T(8,128)(2,1)}, u32[]{:S(2)}, u32[]{:S(2)}) async-start(bf16[16,9,8,128]{3,2,1,0:T(8,128)(2,1)} %bitcast.26), calls=%async_computation.2 | async-start | bytes 589824 | tf_op jit(solution)/shard_map/all_to_all | solution.py:94
  77.1 0.0 copy-done.1
  77.1 0.3 fusion.8
  77.4 0.0 copy-start
  77.4 0.3 convolution_add_fusion.2
  77.7 0.3 convolution_add_fusion.1
  78.0 11.7 %all-to-all-done.2 = bf16[16,9,8,128]{3,2,1,0:T(8,128)(2,1)} async-done(((bf16[16,9,8,128]{3,2,1,0:T(8,128)(2,1)}), bf16[16,9,8,128]{3,2,1,0:T(8,128)(2,1)}, u32[]{:S(2)}, u32[]{:S(2)}) %all-to-all-start.2) | async-done | bytes 294944 | tf_op jit(solution)/shard_map/all_to_all | solution.py:94
  89.8 1.0 %copy.18 = bf16[9,2,8,8,128]{4,3,2,1,0:T(8,128)(2,1)S(1)} copy(bf16[9,2,8,8,128]{4,3,0,1,2:T(8,128)(2,1)} %bitcast.28) | data formatting | bytes 589824 | tf_op jit(solution)/shard_map/transpose | solution.py:99
  90.8 0.0 copy-done
  90.8 0.5 fusion.4
  91.3 1.0 %fusion.3 = f32[512,128]{0,1:T(8,128)S(1)} fusion(f32[128,512]{1,0:T(8,128)S(1)} %fusion.4, f32[128,512]{1,0:T(8,128)S(1)} %convolution_add_fusion.1, bf16[10,512,128]{2,1,0:T(8,128)(2,1)S(1)} %copy-done, bf16[1216,128]{1,0:T(8,128)(2,1)} %copy-done.3), kind=kOutput, calls=%fused_computation.6 | convolution fusion | flops 16908288 | bytes 950272 | tf_op jit(solution)/shard_map/dot_general | solution.py:102
  92.3 0.8 copy.20
  (37 shorter events, 0.6 us)
Async XLA Ops:
  0.0 27.5 %collective-permute-start = (bf16[512,128]{1,0:T(8,128)(2,1)}, bf16[512,128]{1,0:T(8,128)(2,1)S(1)}, u32[]{:S(2)}, u32[]{:S(2)}) collective-permute-start(bf16[512,128]{1,0:T(8,128)(2,1)} %param.4), channel_id=1, source_target_pairs={{1,2},{2,1},{3,4},{4,3},{5,6},{6,5},{7,8},{8,7},{9,10},{10,9},{11,... | collective-permute-start | bytes 393224 | tf_op jit(solution)/shard_map/ppermute | solution.py:40
  7.3 12.4 %copy-start.4 = (s32[1,3]{1,0:T(1,128)S(1)}, s32[1,3]{1,0:T(1,128)}, u32[]{:S(2)}) copy-start(s32[1,3]{1,0:T(1,128)} %param.6) | copy-start | bytes 40
  7.5 13.8 %collective-permute-start.1 = (f32[1216,128]{1,0:T(8,128)S(1)}, f32[1216,128]{1,0:T(8,128)S(1)}, u32[]{:S(2)}, u32[]{:S(2)}) collective-permute-start(f32[1216,128]{1,0:T(8,128)S(1)} %pad_maximum_fusion), channel_id=1, source_target_pairs={{0,1},{1,0},{2,3},{3,2},{4,5},{5,4},{6,7},{7,6},{8,9},{9,8},{10,11... | collective-permute-start | bytes 1867784 | tf_op jit(solution)/shard_map/ppermute | solution.py:25
  21.4 6.9 %copy-start.2 = (bf16[512,128]{1,0:T(8,128)(2,1)S(1)}, bf16[512,128]{1,0:T(8,128)(2,1)}, u32[]{:S(2)}) copy-start(bf16[512,128]{1,0:T(8,128)(2,1)} %param.4) | copy-start | bytes 393220
  22.1 16.4 %all-to-all-start = ((f32[9,8,8,128]{3,2,0,1:T(8,128)}), f32[9,8,8,128]{3,2,0,1:T(8,128)S(1)}, u32[]{:S(2)}, u32[]{:S(2)}) async-start(f32[9,8,8,128]{3,2,0,1:T(8,128)} %copy.16), calls=%async_computation | async-start | bytes 589824 | tf_op jit(solution)/shard_map/all_to_all | solution.py:57
  27.5 0.7 copy-start.3
  40.0 28.4 %all-to-all-start.1 = ((f32[64,8,128]{2,1,0:T(8,128)}), f32[64,8,128]{2,1,0:T(8,128)S(1)}, u32[]{:S(2)}, u32[]{:S(2)}) async-start(f32[64,8,128]{2,1,0:T(8,128)} %broadcast_select_fusion.1), calls=%async_computation.1 | async-start | bytes 524288 | tf_op jit(solution)/shard_map/all_to_all | solution.py:77
  55.6 21.5 %copy-start.1 = (bf16[1,3,512,512]{3,2,1,0:T(8,128)(2,1)S(1)}, bf16[1,3,512,512]{3,2,1,0:T(8,128)(2,1)}, u32[]{:S(2)}) copy-start(bf16[1,3,512,512]{3,2,1,0:T(8,128)(2,1)} %param.5) | copy-start | bytes 4718596
  70.2 19.5 %all-to-all-start.2 = ((bf16[16,9,8,128]{3,2,1,0:T(8,128)(2,1)}), bf16[16,9,8,128]{3,2,1,0:T(8,128)(2,1)}, u32[]{:S(2)}, u32[]{:S(2)}) async-start(bf16[16,9,8,128]{3,2,1,0:T(8,128)(2,1)} %bitcast.26), calls=%async_computation.2 | async-start | bytes 589824 | tf_op jit(solution)/shard_map/all_to_all | solution.py:94
  77.4 13.4 %copy-start = (bf16[10,512,128]{2,1,0:T(8,128)(2,1)S(1)}, bf16[10,512,128]{2,1,0:T(8,128)(2,1)}, u32[]{:S(2)}) copy-start(bf16[10,512,128]{2,1,0:T(8,128)(2,1)} %param.7) | copy-start | bytes 3932164

commit v7 on v4

--- a/solution.py
+++ b/solution.py
@@ -6,30 +6,9 @@
 PLACED = ("slab", "x", "core")
 
 
-def extended(block, sides, width):
-    for axis, dim in sides:
-        count = lax.axis_size(axis)
-        forward = [(i, i + 1) for i in range(count - 1)]
-        backward = [(target, source) for source, target in forward]
-        low = lax.ppermute(
-            lax.slice_in_dim(block, block.shape[dim] - width, None, axis=dim), axis, forward
-        )
-        high = lax.ppermute(lax.slice_in_dim(block, 0, width, axis=dim), axis, backward)
-        block = jnp.concatenate([low, block, high], axis=dim)
-    return block
-
-
 def body(probes, near_blocks, near_offsets, far_basis):
     leaf_rows = probes.shape[0]
     levels = far_basis.shape[0]
-    padded = extended(probes, ((PLACED, 0),), leaf_rows)
-    near_sum = jnp.zeros(probes.shape, jnp.float32)
-    for member in range(near_blocks.shape[1]):
-        window_start = (near_offsets[0, member] + 1) * leaf_rows
-        window = lax.dynamic_slice_in_dim(padded, window_start, leaf_rows, 0)
-        near_sum = near_sum + jnp.dot(
-            near_blocks[0, member], window, preferred_element_type=jnp.float32
-        )
     projected = jnp.einsum("lpr,pq->lrq", far_basis, probes, preferred_element_type=jnp.float32)
     rank, width = projected.shape[1], projected.shape[2]
     chips = lax.axis_size("x")
@@ -77,6 +56,29 @@
         sibling = by_distance[2**step : 2 ** (step + 1)].sum(axis=0)
         couplings_high.append((sibling * 2.0 ** (-0.5 * level)).astype(jnp.bfloat16))
 
+    sent, _ = lax.optimization_barrier((probes, received))
+    partner = lax.ppermute(sent, "core", swap)
+    devices = slabs * chips * 2
+    pairs = []
+    for odd in range(1, devices - 1, 2):
+        pairs += [(odd, odd + 1), (odd + 1, odd)]
+    across = lax.ppermute(sent, PLACED, pairs)
+    padded = jnp.concatenate(
+        [
+            jnp.where(core == 0, across, partner),
+            probes,
+            jnp.where(core == 0, partner, across),
+        ],
+        axis=0,
+    )
+    near_sum = jnp.zeros(probes.shape, jnp.float32)
+    for member in range(near_blocks.shape[1]):
+        window_start = (near_offsets[0, member] + 1) * leaf_rows
+        window = lax.dynamic_slice_in_dim(padded, window_start, leaf_rows, 0)
+        near_sum = near_sum + jnp.dot(
+            near_blocks[0, member], window, preferred_element_type=jnp.float32
+        )
+
     high = jnp.stack(couplings_high)
     outgoing = jnp.concatenate(
         [
@@ -85,17 +87,19 @@
         ],
         axis=1,
     )
-    returned = lax.all_to_all(outgoing, "x", 0, 0, tiled=True)
-    mine = returned.transpose(1, 0, 2, 3).reshape(levels - 1, half, width)
-    other = lax.ppermute(mine, "core", swap)
-    coupling_rest = jnp.where(
-        core == 0,
-        jnp.concatenate([mine, other], axis=1),
-        jnp.concatenate([other, mine], axis=1),
+    everyone = jnp.broadcast_to(outgoing[:, None], (chips, 2) + outgoing.shape[1:])
+    returned = lax.all_to_all(
+        everyone.reshape((chips * 2,) + outgoing.shape[1:]), ("x", "core"), 0, 0, tiled=True
+    )
+    far_rest = (
+        far_basis[1:]
+        .reshape(levels - 1, leaf_rows, 2, chips, share)
+        .transpose(1, 3, 2, 0, 4)
+        .reshape(leaf_rows, -1)
     )
     output = near_sum + jnp.dot(far_basis[0], coupling_first, preferred_element_type=jnp.float32)
-    output = output + jnp.einsum(
-        "lpr,lrq->pq", far_basis[1:], coupling_rest, preferred_element_type=jnp.float32
+    output = output + jnp.dot(
+        far_rest, returned.reshape(-1, width), preferred_element_type=jnp.float32
     )
     return output
 

time: 95.8 us -> 97.8 us (1.021)
  waiting for transfers between devices: 30.8 us -> 35.9 us
  starting transfers between devices: 49.2 us -> 44.7 us
  local copies, waits for them, and re-layouts: 4.64 us -> 6.79 us
    ppermute x3 -> x2, starting transfers between devices: 23.8 us -> 6.73 us  [the longest x1 4.81 us: body(): partner = lax.ppermute(sent, 'core', swap)]
    ppermute x1, starting transfers between devices: 1.92 us -> 16.1 us  [body(): lax.ppermute(jnp.concatenate([projected[0], send.reshape(-1, width)], axi...]
    all_to_all x1, waiting for transfers between devices: 6.63 us -> 10.1 us  [body(): lax.all_to_all(everyone.reshape((chips * 2,) + outgoing.shape[1:]), ('x',...]
    all_to_all x1, starting transfers between devices: 16.1 us -> 13.6 us  [body(): lax.all_to_all(jnp.take(totals, level_of, axis=0), 'slab', 0, 0, tiled=True)]
    all_to_all x1, waiting for transfers between devices: 10.9 us -> 12.9 us  [body(): lax.all_to_all(paired.reshape(levels - 1, chips, share, width), 'x', 1, 1...]
    unnamed x14 -> x13, local copies, waits for them, and re-layouts: 0.06 us -> 1.4 us
    slice x1, local copies, waits for them, and re-layouts: 0.02 us -> 1.01 us  [body(): paired = keep + incoming[rank:].reshape(levels - 1, half, width)]
  transfers between devices with their start and end apart: 7 -> 6, of which waited for: 4 -> 3; matrix products, arithmetic and copies ran while one was open for 6% -> 5% of each run, Pallas kernels for 0% -> 0%
where the time goes in v7:
time: 97.8 us; the launch traced here: 97.2 us
  starting transfers between devices  44.7 us (46%)
  waiting for transfers between devices  35.9 us (37%)
  local copies, waits for them, and re-layouts  6.79 us (7%)
  matrix products  5.36 us (5%)
  between operations  2.37 us (2%)
  other arithmetic  2.09 us (2%)
    ppermute x1, starting transfers between devices, body(): lax.ppermute(jnp.concatenate([projected[0], send.reshape(-1, width)], axi...  16.1 us
    all_to_all x1, starting transfers between devices, body(): lax.all_to_all(jnp.take(totals, level_of, axis=0), 'slab', 0, 0, tiled=True)  13.6 us
    all_to_all x1, waiting for transfers between devices, body(): lax.all_to_all(paired.reshape(levels - 1, chips, share, width), 'x', 1, 1...  12.9 us
    all_to_all x1, waiting for transfers between devices, body(): lax.all_to_all(jnp.take(totals, level_of, axis=0), 'slab', 0, 0, tiled=True)  12.9 us
    all_to_all x1, waiting for transfers between devices, body(): lax.all_to_all(everyone.reshape((chips * 2,) + outgoing.shape[1:]), ('x',...  10.1 us
    ppermute x1, starting transfers between devices, body(): partner = lax.ppermute(sent, 'core', swap)  4.81 us
    all_to_all x1, starting transfers between devices, body(): lax.all_to_all(everyone.reshape((chips * 2,) + outgoing.shape[1:]), ('x',...  4.67 us
    all_to_all x1, starting transfers between devices, body(): lax.all_to_all(paired.reshape(levels - 1, chips, share, width), 'x', 1, 1...  3.55 us
  transfers between devices with their start and end apart: 6, of which 3 were waited for; matrix products, arithmetic and copies ran while one was open for 5% of the time, Pallas kernels for 0%

profile of v7, /device:TPU:1, one launch (start us, length us, event | category | flops | bytes accessed | tf_op | source)
XLA Modules:
  0.0 97.2 jit_solution(14400002661944667558)
XLA Ops:
  0.0 1.9 %fusion.10 = f32[10,128,128]{2,1,0:T(8,128)S(1)} fusion(bf16[10,512,128]{2,1,0:T(8,128)(2,1)} %param.7, bf16[512,128]{1,0:T(8,128)(2,1)} %param.4), kind=kOutput, calls=%fused_computation.21 | convolution fusion | flops 167772160 | bytes 2097152 | tf_op jit(solution)/shard_map/lpr,pq->lrq/dot_general | solution.py:12
  1.9 0.0 copy-start.5
  1.9 0.0 copy-start.1
  2.0 0.8 copy-done.1
  2.7 0.8 pad_maximum_fusion.1
  3.5 0.0 slice-start
  3.5 16.1 %collective-permute-start = (f32[704,128]{1,0:T(8,128)}, f32[704,128]{1,0:T(8,128)}, u32[]{:S(2)}, u32[]{:S(2)}) collective-permute-start(f32[704,128]{1,0:T(8,128)} %pad_maximum_fusion.1), channel_id=1, source_target_pairs={{0,1},{1,0},{2,3},{3,2},{4,5},{5,4},{6,7},{7,6},{8,9},{9,8},{10,11... | collective-permute-start | bytes 1081352 | tf_op jit(solution)/shard_map/ppermute | solution.py:25
  19.7 0.0 copy-done.5
  19.7 0.6 fusion.36
  22.2 0.0 slice-done
  22.2 0.6 copy.34
  22.8 0.0 copy-start.2
  22.8 0.1 copy.31
  23.0 0.0 collective-permute-done
  23.0 1.0 %slice.96 = f32[576,128]{1,0:T(8,128)S(1)} slice(f32[704,128]{1,0:T(8,128)} %collective-permute-done), slice={[128:704], [0:128]} | slice | bytes 589824 | tf_op jit(solution)/shard_map/slice | solution.py:29
  24.0 0.0 copy-done.2
  24.1 0.7 copy.26
  24.8 0.0 copy-start.4
  24.8 3.6 %all-to-all-start = ((f32[9,8,8,128]{3,2,0,1:T(8,128)}), f32[9,8,8,128]{3,2,0,1:T(8,128)S(1)}, u32[]{:S(2)}, u32[]{:S(2)}) async-start(f32[9,8,8,128]{3,2,0,1:T(8,128)} %copy.26), calls=%async_computation | async-start | bytes 589824 | tf_op jit(solution)/shard_map/all_to_all | solution.py:31
  28.4 12.9 %all-to-all-done = f32[9,8,8,128]{3,2,0,1:T(8,128)S(1)} async-done(((f32[9,8,8,128]{3,2,0,1:T(8,128)}), f32[9,8,8,128]{3,2,0,1:T(8,128)S(1)}, u32[]{:S(2)}, u32[]{:S(2)}) %all-to-all-start) | async-done | bytes 294944 | tf_op jit(solution)/shard_map/all_to_all | solution.py:31
  41.4 0.6 gather_fusion
  42.0 0.8 broadcast_select_fusion.1
  42.9 13.6 %all-to-all-start.1 = ((f32[64,8,128]{2,1,0:T(8,128)}), f32[64,8,128]{2,1,0:T(8,128)S(1)}, u32[]{:S(2)}, u32[]{:S(2)}) async-start(f32[64,8,128]{2,1,0:T(8,128)} %broadcast_select_fusion.1), calls=%async_computation.1 | async-start | bytes 524288 | tf_op jit(solution)/shard_map/all_to_all | solution.py:51
  56.6 12.9 %all-to-all-done.1 = f32[64,8,128]{2,1,0:T(8,128)S(1)} async-done(((f32[64,8,128]{2,1,0:T(8,128)}), f32[64,8,128]{2,1,0:T(8,128)S(1)}, u32[]{:S(2)}, u32[]{:S(2)}) %all-to-all-start.1) | async-done | bytes 262176 | tf_op jit(solution)/shard_map/all_to_all | solution.py:51
  69.4 0.0 copy-done.4
  69.4 4.8 %collective-permute-start.2 = (bf16[512,128]{1,0:T(8,128)(2,1)S(1)}, bf16[512,128]{1,0:T(8,128)(2,1)S(1)}, u32[]{:S(2)}, u32[]{:S(2)}) collective-permute-start(bf16[512,128]{1,0:T(8,128)(2,1)S(1)} %copy-done.4), channel_id=1, source_target_pairs={{0,1},{1,0},{2,3},{3,2},{4,5},{5,4},{6,7},{7,6},{8,9},{9,8},{10,11... | collective-permute-start | bytes 393224 | tf_op jit(solution)/shard_map/ppermute | solution.py:60
  74.3 1.9 %collective-permute-start.1 = (bf16[512,128]{1,0:T(8,128)(2,1)S(1)}, bf16[512,128]{1,0:T(8,128)(2,1)S(1)}, u32[]{:S(2)}, u32[]{:S(2)}) collective-permute-start(bf16[512,128]{1,0:T(8,128)(2,1)S(1)} %copy-done.4), channel_id=1, source_target_pairs={{1,2},{2,1},{3,4},{4,3},{5,6},{6,5},{7,8},{8,7},{9,10},{10,9},{11,... | collective-permute-start | bytes 393224 | tf_op jit(solution)/shard_map/ppermute | solution.py:65
  76.2 0.6 gather_fusion.1
  76.8 0.1 broadcast_select_fusion
  77.2 0.7 broadcast_in_dim.48
  78.0 4.7 %all-to-all-start.2 = ((bf16[16,9,8,128]{3,2,1,0:T(8,128)(2,1)}), bf16[16,9,8,128]{3,2,1,0:T(8,128)(2,1)S(1)}, u32[]{:S(2)}, u32[]{:S(2)}) async-start(bf16[16,9,8,128]{3,2,1,0:T(8,128)(2,1)} %bitcast.28), calls=%async_computation.2 | async-start | bytes 589824 | tf_op jit(solution)/shard_map/all_to_all | solution.py:91
  82.6 0.0 copy-start.3
  82.6 0.0 collective-permute-done.2
  82.6 0.0 collective-permute-done.1
  82.7 1.5 %fusion.3 = f32[128,512]{1,0:T(8,128)S(1)} fusion(bf16[1,3,512,512]{3,2,1,0:T(8,128)(2,1)} %param.5, bf16[1536,128]{1,0:T(8,128)(2,1)S(1)} %pad_maximum_fusion, s32[]{:T(128)S(6)} %select_n.75), kind=kOutput, calls=%fused_computation.8 | convolution fusion | flops 67108864 | bytes 917508 | tf_op jit(solution)/shard_map/dot_general | solution.py:78
  84.2 0.0 copy-done.3
  84.2 0.3 convolution_add_fusion.2
  84.5 0.0 copy-start
  84.5 0.3 convolution_add_fusion.1
  84.9 10.1 %all-to-all-done.2 = bf16[16,9,8,128]{3,2,1,0:T(8,128)(2,1)S(1)} async-done(((bf16[16,9,8,128]{3,2,1,0:T(8,128)(2,1)}), bf16[16,9,8,128]{3,2,1,0:T(8,128)(2,1)S(1)}, u32[]{:S(2)}, u32[]{:S(2)}) %all-to-all-start.2) | async-done | bytes 294944 | tf_op jit(solution)/shard_map/all_to_all | solution.py:91
  94.9 0.4 fusion.37
  95.3 0.0 copy-done
  95.3 1.1 %fusion.1 = f32[512,128]{0,1:T(8,128)S(1)} fusion(f32[128,512]{1,0:T(8,128)S(1)} %fusion.37, f32[128,512]{1,0:T(8,128)S(1)} %convolution_add_fusion.1, bf16[10,512,128]{2,1,0:T(8,128)(2,1)S(1)} %copy-done, f32[704,128]{1,0:T(8,128)} %collective-permute-done), kind=kOutput, calls=%fused_computation.4 | convolution fusion | flops 16908288 | bytes 950272 | tf_op jit(solution)/shard_map/dot_general | solution.py:100
  96.3 0.8 copy.32
  (34 shorter events, 0.4 us)
Async XLA Ops:
  1.9 17.8 %copy-start.5 = (s32[1,3]{1,0:T(1,128)S(1)}, s32[1,3]{1,0:T(1,128)}, u32[]{:S(2)}) copy-start(s32[1,3]{1,0:T(1,128)} %param.6) | copy-start | bytes 40
  1.9 0.8 copy-start.1
  3.5 18.7 %slice-start = ((bf16[10,512,128]{2,1,0:T(8,128)(2,1)}), bf16[9,512,128]{2,1,0:T(8,128)(2,1)S(1)}, s32[]{:S(2)}) async-start(bf16[10,512,128]{2,1,0:T(8,128)(2,1)} %param.7), calls=%async_computation.3 | async-start | bytes 2359296 | tf_op jit(solution)/shard_map/slice | solution.py:95
  3.5 19.5 %collective-permute-start = (f32[704,128]{1,0:T(8,128)}, f32[704,128]{1,0:T(8,128)}, u32[]{:S(2)}, u32[]{:S(2)}) collective-permute-start(f32[704,128]{1,0:T(8,128)} %pad_maximum_fusion.1), channel_id=1, source_target_pairs={{0,1},{1,0},{2,3},{3,2},{4,5},{5,4},{6,7},{7,6},{8,9},{9,8},{10,11... | collective-permute-start | bytes 1081352 | tf_op jit(solution)/shard_map/ppermute | solution.py:25
  22.8 1.2 %copy-start.2 = (f32[9,128,128]{2,1,0:T(8,128)S(1)}, f32[9,128,128]{2,1,0:T(8,128)}, u32[]{:S(2)}) copy-start(f32[9,128,128]{2,1,0:T(8,128)} %copy-done.1) | copy-start | bytes 1769476
  24.8 44.6 %copy-start.4 = (bf16[512,128]{1,0:T(8,128)(2,1)S(1)}, bf16[512,128]{1,0:T(8,128)(2,1)}, u32[]{:S(2)}) copy-start(bf16[512,128]{1,0:T(8,128)(2,1)} %param.4) | copy-start | bytes 393220
  24.8 16.6 %all-to-all-start = ((f32[9,8,8,128]{3,2,0,1:T(8,128)}), f32[9,8,8,128]{3,2,0,1:T(8,128)S(1)}, u32[]{:S(2)}, u32[]{:S(2)}) async-start(f32[9,8,8,128]{3,2,0,1:T(8,128)} %copy.26), calls=%async_computation | async-start | bytes 589824 | tf_op jit(solution)/shard_map/all_to_all | solution.py:31
  42.9 26.6 %all-to-all-start.1 = ((f32[64,8,128]{2,1,0:T(8,128)}), f32[64,8,128]{2,1,0:T(8,128)S(1)}, u32[]{:S(2)}, u32[]{:S(2)}) async-start(f32[64,8,128]{2,1,0:T(8,128)} %broadcast_select_fusion.1), calls=%async_computation.1 | async-start | bytes 524288 | tf_op jit(solution)/shard_map/all_to_all | solution.py:51
  69.4 13.2 %collective-permute-start.2 = (bf16[512,128]{1,0:T(8,128)(2,1)S(1)}, bf16[512,128]{1,0:T(8,128)(2,1)S(1)}, u32[]{:S(2)}, u32[]{:S(2)}) collective-permute-start(bf16[512,128]{1,0:T(8,128)(2,1)S(1)} %copy-done.4), channel_id=1, source_target_pairs={{0,1},{1,0},{2,3},{3,2},{4,5},{5,4},{6,7},{7,6},{8,9},{9,8},{10,11... | collective-permute-start | bytes 393224 | tf_op jit(solution)/shard_map/ppermute | solution.py:60
  74.3 8.4 %collective-permute-start.1 = (bf16[512,128]{1,0:T(8,128)(2,1)S(1)}, bf16[512,128]{1,0:T(8,128)(2,1)S(1)}, u32[]{:S(2)}, u32[]{:S(2)}) collective-permute-start(bf16[512,128]{1,0:T(8,128)(2,1)S(1)} %copy-done.4), channel_id=1, source_target_pairs={{1,2},{2,1},{3,4},{4,3},{5,6},{6,5},{7,8},{8,7},{9,10},{10,9},{11,... | collective-permute-start | bytes 393224 | tf_op jit(solution)/shard_map/ppermute | solution.py:65
  78.0 17.0 %all-to-all-start.2 = ((bf16[16,9,8,128]{3,2,1,0:T(8,128)(2,1)}), bf16[16,9,8,128]{3,2,1,0:T(8,128)(2,1)S(1)}, u32[]{:S(2)}, u32[]{:S(2)}) async-start(bf16[16,9,8,128]{3,2,1,0:T(8,128)(2,1)} %bitcast.28), calls=%async_computation.2 | async-start | bytes 589824 | tf_op jit(solution)/shard_map/all_to_all | solution.py:91
  82.6 1.6 %copy-start.3 = (bf16[1,3,512,512]{3,2,1,0:T(8,128)(2,1)S(1)}, bf16[1,3,512,512]{3,2,1,0:T(8,128)(2,1)}, u32[]{:S(2)}) copy-start(bf16[1,3,512,512]{3,2,1,0:T(8,128)(2,1)} %param.5) | copy-start | bytes 4718596
  84.5 10.8 %copy-start = (bf16[10,512,128]{2,1,0:T(8,128)(2,1)S(1)}, bf16[10,512,128]{2,1,0:T(8,128)(2,1)}, u32[]{:S(2)}) copy-start(bf16[10,512,128]{2,1,0:T(8,128)(2,1)} %param.7) | copy-start | bytes 3932164

commit v8 on v6

--- a/solution.py
+++ b/solution.py
@@ -94,14 +94,15 @@
     returned = lax.all_to_all(
         everyone.reshape((chips * 2,) + outgoing.shape[1:]), ("x", "core"), 0, 0, tiled=True
     )
-    coupling_rest = (
-        returned.reshape((chips, 2) + outgoing.shape[1:])
-        .transpose(2, 1, 0, 3, 4)
-        .reshape(levels - 1, rank, width)
+    far_rest = (
+        far_basis[1:]
+        .reshape(levels - 1, leaf_rows, 2, chips, share)
+        .transpose(1, 3, 2, 0, 4)
+        .reshape(leaf_rows, -1)
     )
     output = near_sum + jnp.dot(far_basis[0], coupling_first, preferred_element_type=jnp.float32)
-    output = output + jnp.einsum(
-        "lpr,lrq->pq", far_basis[1:], coupling_rest, preferred_element_type=jnp.float32
+    output = output + jnp.dot(
+        far_rest, returned.reshape(-1, width), preferred_element_type=jnp.float32
     )
     return output
 

time: 93.7 us -> 93.2 us (level)
  waiting for transfers between devices: 35.8 us -> 29.6 us
  matrix products: 4.29 us -> 7.34 us
  other arithmetic: 2.33 us -> 4.27 us
    all_to_all x1, waiting for transfers between devices: 11.7 us -> 8.39 us  [body(): lax.all_to_all(everyone.reshape((chips * 2,) + outgoing.shape[1:]), ('x',...]
    dot_general x3, matrix products: 0.94 us -> 4.16 us  [body(): jnp.dot(near_blocks[0, member], window, preferred_element_type=jnp.float32)]
    all_to_all x1, waiting for transfers between devices: 10.3 us -> 8.17 us  [body(): lax.all_to_all(paired.reshape(levels - 1, chips, share, width), 'x', 1, 1...]
    all_to_all x1, starting transfers between devices: 15.5 us -> 14.2 us  [body(): lax.all_to_all(jnp.take(totals, level_of, axis=0), 'slab', 0, 0, tiled=True)]
    select_n x1, other arithmetic: 0.02 us -> 1.04 us  [body(): jnp.where(core == 0, across, partner)]
  transfers between devices with their start and end apart: 5 -> 5, of which waited for: 4 -> 4; matrix products, arithmetic and copies ran while one was open for 6% -> 12% of each run, Pallas kernels for 0% -> 0%
where the time goes in v8:
time: 93.2 us; the launch traced here: 92.3 us
  starting transfers between devices  41.8 us (45%)
  waiting for transfers between devices  29.6 us (32%)
  matrix products  7.34 us (8%)
  local copies, waits for them, and re-layouts  6.85 us (7%)
  other arithmetic  4.27 us (5%)
  between operations  2.44 us (3%)
    all_to_all x1, starting transfers between devices, body(): lax.all_to_all(jnp.take(totals, level_of, axis=0), 'slab', 0, 0, tiled=True)  14.2 us
    ppermute x1, starting transfers between devices, body(): lax.ppermute(jnp.concatenate([projected[0], send.reshape(-1, width), prob...  12.8 us
    all_to_all x1, waiting for transfers between devices, body(): lax.all_to_all(jnp.take(totals, level_of, axis=0), 'slab', 0, 0, tiled=True)  12.1 us
    all_to_all x1, waiting for transfers between devices, body(): lax.all_to_all(everyone.reshape((chips * 2,) + outgoing.shape[1:]), ('x',...  8.39 us
    all_to_all x1, waiting for transfers between devices, body(): lax.all_to_all(paired.reshape(levels - 1, chips, share, width), 'x', 1, 1...  8.17 us
    all_to_all x1, starting transfers between devices, body(): lax.all_to_all(everyone.reshape((chips * 2,) + outgoing.shape[1:]), ('x',...  6.22 us
    ppermute x1, starting transfers between devices, body(): across = lax.ppermute(probes, PLACED, pairs)  4.49 us
    dot_general x3, matrix products, body(): jnp.dot(near_blocks[0, member], window, preferred_element_type=jnp.float32)  4.16 us
  transfers between devices with their start and end apart: 5, of which 4 were waited for; matrix products, arithmetic and copies ran while one was open for 12% of the time, Pallas kernels for 0%

profile of v8, /device:TPU:1, one launch (start us, length us, event | category | flops | bytes accessed | tf_op | source)
XLA Modules:
  0.0 92.3 jit_solution(506749646381007069)
XLA Ops:
  0.0 4.5 %collective-permute-start = (bf16[512,128]{1,0:T(8,128)(2,1)}, bf16[512,128]{1,0:T(8,128)(2,1)}, u32[]{:S(2)}, u32[]{:S(2)}) collective-permute-start(bf16[512,128]{1,0:T(8,128)(2,1)} %param.4), channel_id=1, source_target_pairs={{1,2},{2,1},{3,4},{4,3},{5,6},{6,5},{7,8},{8,7},{9,10},{10,9},{11,... | collective-permute-start | bytes 393224 | tf_op jit(solution)/shard_map/ppermute | solution.py:40
  4.5 0.9 %convert_element_type.185 = f32[512,128]{1,0:T(8,128)S(1)} convert(bf16[512,128]{1,0:T(8,128)(2,1)} %param.4) | non-fusion elementwise | flops 65536 | bytes 393216 | tf_op jit(solution)/shard_map/convert_element_type | solution.py:27
  5.4 1.9 %fusion.10 = f32[10,128,128]{2,1,0:T(8,128)S(1)} fusion(bf16[10,512,128]{2,1,0:T(8,128)(2,1)} %param.7, bf16[512,128]{1,0:T(8,128)(2,1)} %param.4), kind=kOutput, calls=%fused_computation.21 | convolution fusion | flops 167772160 | bytes 2097152 | tf_op jit(solution)/shard_map/lpr,pq->lrq/dot_general | solution.py:12
  7.3 0.0 copy-start.5
  7.5 12.8 %collective-permute-start.1 = (f32[1216,128]{1,0:T(8,128)S(1)}, f32[1216,128]{1,0:T(8,128)S(1)}, u32[]{:S(2)}, u32[]{:S(2)}) collective-permute-start(f32[1216,128]{1,0:T(8,128)S(1)} %pad_maximum_fusion), channel_id=1, source_target_pairs={{0,1},{1,0},{2,3},{3,2},{4,5},{5,4},{6,7},{7,6},{8,9},{9,8},{10,11... | collective-permute-start | bytes 1867784 | tf_op jit(solution)/shard_map/ppermute | solution.py:25
  20.4 0.0 copy-done.5
  20.4 0.6 fusion.37
  21.0 1.0 %collective-permute-done.1 = f32[1216,128]{1,0:T(8,128)S(1)} collective-permute-done((f32[1216,128]{1,0:T(8,128)S(1)}, f32[1216,128]{1,0:T(8,128)S(1)}, u32[]{:S(2)}, u32[]{:S(2)}) %collective-permute-start.1) | collective-permute-done | bytes 622624 | tf_op jit(solution)/shard_map/ppermute | solution.py:25
  22.0 0.0 copy-start.1
  22.0 0.8 copy.26
  22.8 0.0 copy-done.1
  22.9 4.1 %all-to-all-start = ((f32[9,8,8,128]{3,2,0,1:T(8,128)}), f32[9,8,8,128]{3,2,0,1:T(8,128)}, u32[]{:S(2)}, u32[]{:S(2)}) async-start(f32[9,8,8,128]{3,2,0,1:T(8,128)} %copy.26), calls=%async_computation | async-start | bytes 589824 | tf_op jit(solution)/shard_map/all_to_all | solution.py:57
  26.9 0.0 slice-start
  29.0 0.0 slice-done
  29.0 0.6 copy.34
  29.6 0.0 copy-start.2
  29.6 0.1 copy.31
  29.7 0.0 copy-start.3
  29.7 0.9 copy-done.2
  30.7 0.0 copy-start.4
  30.7 0.0 collective-permute-done
  30.7 1.0 %broadcast_select_fusion.3 = (bf16[512,128]{1,0:T(8,128)(2,1)S(1)}, bf16[512,128]{1,0:T(8,128)(2,1)S(1)}) fusion(bf16[512,128]{1,0:T(8,128)(2,1)} %collective-permute-done, pred[]{:T(512)S(6)} %eq.4, bf16[1216,128]{1,0:T(8,128)(2,1)S(1)} %convert.4), kind=kLoop, calls=%fused_computation.30 | loop fusion | flops 131072 | bytes 524289 | tf_op jit(solution)/shard_map/jit(_where)/select_n | solution.py:43
  31.7 0.0 copy-done.3
  31.8 8.2 %all-to-all-done = f32[9,8,8,128]{3,2,0,1:T(8,128)} async-done(((f32[9,8,8,128]{3,2,0,1:T(8,128)}), f32[9,8,8,128]{3,2,0,1:T(8,128)}, u32[]{:S(2)}, u32[]{:S(2)}) %all-to-all-start) | async-done | bytes 294944 | tf_op jit(solution)/shard_map/all_to_all | solution.py:57
  40.0 0.0 copy-done.4
  40.0 0.9 %slice_reduce_fusion = f32[6,8,128]{2,1,0:T(8,128)S(1)} fusion(f32[9,8,8,128]{3,2,0,1:T(8,128)} %all-to-all-done), kind=kLoop, calls=%fused_computation.17 | loop fusion | flops 43008 | bytes 221184 | tf_op jit(solution)/shard_map/reduce_sum | solution.py:69
  40.9 0.6 gather_fusion
  41.6 0.8 broadcast_select_fusion.1
  42.4 14.2 %all-to-all-start.1 = ((f32[64,8,128]{2,1,0:T(8,128)}), f32[64,8,128]{2,1,0:T(8,128)S(1)}, u32[]{:S(2)}, u32[]{:S(2)}) async-start(f32[64,8,128]{2,1,0:T(8,128)} %broadcast_select_fusion.1), calls=%async_computation.1 | async-start | bytes 524288 | tf_op jit(solution)/shard_map/all_to_all | solution.py:77
  56.6 0.8 fusion.36
  57.5 12.1 %all-to-all-done.1 = f32[64,8,128]{2,1,0:T(8,128)S(1)} async-done(((f32[64,8,128]{2,1,0:T(8,128)}), f32[64,8,128]{2,1,0:T(8,128)S(1)}, u32[]{:S(2)}, u32[]{:S(2)}) %all-to-all-start.1) | async-done | bytes 262176 | tf_op jit(solution)/shard_map/all_to_all | solution.py:77
  69.6 0.6 gather_fusion.1
  70.2 0.1 broadcast_select_fusion
  70.6 0.8 broadcast_in_dim.48
  71.4 6.2 %all-to-all-start.2 = ((bf16[16,9,8,128]{3,2,1,0:T(8,128)(2,1)}), bf16[16,9,8,128]{3,2,1,0:T(8,128)(2,1)S(1)}, u32[]{:S(2)}, u32[]{:S(2)}) async-start(bf16[16,9,8,128]{3,2,1,0:T(8,128)(2,1)} %bitcast.28), calls=%async_computation.2 | async-start | bytes 589824 | tf_op jit(solution)/shard_map/all_to_all | solution.py:94
  77.6 1.3 %fusion.3 = f32[128,512]{1,0:T(8,128)S(1)} fusion(bf16[1,3,512,512]{3,2,1,0:T(8,128)(2,1)} %param.5, bf16[1536,128]{1,0:T(8,128)(2,1)S(1)} %pad_maximum_fusion.1, s32[]{:T(128)S(6)} %select_n.71), kind=kOutput, calls=%fused_computation.9 | convolution fusion | flops 67108864 | bytes 917508 | tf_op jit(solution)/shard_map/dot_general | solution.py:53
  78.9 1.4 %convolution_add_fusion.2 = f32[128,512]{1,0:T(8,128)S(1)} fusion(f32[128,512]{1,0:T(8,128)S(1)} %fusion.3, bf16[1,3,512,512]{3,2,1,0:T(8,128)(2,1)} %param.5, bf16[1536,128]{1,0:T(8,128)(2,1)S(1)} %pad_maximum_fusion.1, s32[]{:T(128)S(6)} %select_n.70), kind=kOutput, calls=%fused_computation.6 | convolution fusion | flops 67174400 | bytes 1179652 | tf_op jit(solution)/shard_map/dot_general | solution.py:53
  80.3 0.0 copy-start
  80.3 1.5 %convolution_add_fusion.1 = f32[128,512]{1,0:T(8,128)S(1)} fusion(f32[128,512]{1,0:T(8,128)S(1)} %convolution_add_fusion.2, bf16[1,3,512,512]{3,2,1,0:T(8,128)(2,1)} %param.5, bf16[1536,128]{1,0:T(8,128)(2,1)S(1)} %pad_maximum_fusion.1, s32[]{:T(128)S(6)} %select_n.72), kind=kOutput, calls=%fused_computation.5 | convolution fusion | flops 67174400 | bytes 1179652 | tf_op jit(solution)/shard_map/dot_general | solution.py:53
  81.8 8.4 %all-to-all-done.2 = bf16[16,9,8,128]{3,2,1,0:T(8,128)(2,1)S(1)} async-done(((bf16[16,9,8,128]{3,2,1,0:T(8,128)(2,1)}), bf16[16,9,8,128]{3,2,1,0:T(8,128)(2,1)S(1)}, u32[]{:S(2)}, u32[]{:S(2)}) %all-to-all-start.2) | async-done | bytes 294944 | tf_op jit(solution)/shard_map/all_to_all | solution.py:94
  90.2 0.4 fusion.38
  90.5 0.0 copy-done
  90.5 1.0 %fusion.1 = f32[512,128]{0,1:T(8,128)S(1)} fusion(f32[128,512]{1,0:T(8,128)S(1)} %fusion.38, f32[128,512]{1,0:T(8,128)S(1)} %convolution_add_fusion.1, bf16[10,512,128]{2,1,0:T(8,128)(2,1)S(1)} %copy-done, bf16[1216,128]{1,0:T(8,128)(2,1)} %copy-done.4), kind=kOutput, calls=%fused_computation.4 | convolution fusion | flops 16908288 | bytes 950272 | tf_op jit(solution)/shard_map/dot_general | solution.py:103
  91.5 0.8 copy.32
  (34 shorter events, 0.5 us)
Async XLA Ops:
  0.0 30.7 %collective-permute-start = (bf16[512,128]{1,0:T(8,128)(2,1)}, bf16[512,128]{1,0:T(8,128)(2,1)}, u32[]{:S(2)}, u32[]{:S(2)}) collective-permute-start(bf16[512,128]{1,0:T(8,128)(2,1)} %param.4), channel_id=1, source_target_pairs={{1,2},{2,1},{3,4},{4,3},{5,6},{6,5},{7,8},{8,7},{9,10},{10,9},{11,... | collective-permute-start | bytes 393224 | tf_op jit(solution)/shard_map/ppermute | solution.py:40
  7.3 13.1 %copy-start.5 = (s32[1,3]{1,0:T(1,128)S(1)}, s32[1,3]{1,0:T(1,128)}, u32[]{:S(2)}) copy-start(s32[1,3]{1,0:T(1,128)} %param.6) | copy-start | bytes 40
  7.5 14.5 %collective-permute-start.1 = (f32[1216,128]{1,0:T(8,128)S(1)}, f32[1216,128]{1,0:T(8,128)S(1)}, u32[]{:S(2)}, u32[]{:S(2)}) collective-permute-start(f32[1216,128]{1,0:T(8,128)S(1)} %pad_maximum_fusion), channel_id=1, source_target_pairs={{0,1},{1,0},{2,3},{3,2},{4,5},{5,4},{6,7},{7,6},{8,9},{9,8},{10,11... | collective-permute-start | bytes 1867784 | tf_op jit(solution)/shard_map/ppermute | solution.py:25
  22.0 0.9 copy-start.1
  22.9 17.1 %all-to-all-start = ((f32[9,8,8,128]{3,2,0,1:T(8,128)}), f32[9,8,8,128]{3,2,0,1:T(8,128)}, u32[]{:S(2)}, u32[]{:S(2)}) async-start(f32[9,8,8,128]{3,2,0,1:T(8,128)} %copy.26), calls=%async_computation | async-start | bytes 589824 | tf_op jit(solution)/shard_map/all_to_all | solution.py:57
  26.9 2.0 %slice-start = ((bf16[10,512,128]{2,1,0:T(8,128)(2,1)}), bf16[9,512,128]{2,1,0:T(8,128)(2,1)S(1)}, s32[]{:S(2)}) async-start(bf16[10,512,128]{2,1,0:T(8,128)(2,1)} %param.7), calls=%async_computation.3 | async-start | bytes 2359296 | tf_op jit(solution)/shard_map/slice | solution.py:98
  29.6 1.1 %copy-start.2 = (f32[1216,128]{1,0:T(8,128)S(1)}, f32[1216,128]{1,0:T(8,128)}, u32[]{:S(2)}) copy-start(f32[1216,128]{1,0:T(8,128)} %copy-done.1) | copy-start | bytes 1867780
  29.7 2.0 %copy-start.3 = (bf16[512,128]{1,0:T(8,128)(2,1)S(1)}, bf16[512,128]{1,0:T(8,128)(2,1)}, u32[]{:S(2)}) copy-start(bf16[512,128]{1,0:T(8,128)(2,1)} %param.4) | copy-start | bytes 393220
  30.7 9.3 %copy-start.4 = (bf16[1216,128]{1,0:T(8,128)(2,1)}, bf16[1216,128]{1,0:T(8,128)(2,1)S(1)}, u32[]{:S(2)}) copy-start(bf16[1216,128]{1,0:T(8,128)(2,1)S(1)} %convert.4) | copy-start | bytes 933892
  42.4 27.2 %all-to-all-start.1 = ((f32[64,8,128]{2,1,0:T(8,128)}), f32[64,8,128]{2,1,0:T(8,128)S(1)}, u32[]{:S(2)}, u32[]{:S(2)}) async-start(f32[64,8,128]{2,1,0:T(8,128)} %broadcast_select_fusion.1), calls=%async_computation.1 | async-start | bytes 524288 | tf_op jit(solution)/shard_map/all_to_all | solution.py:77
  71.4 18.8 %all-to-all-start.2 = ((bf16[16,9,8,128]{3,2,1,0:T(8,128)(2,1)}), bf16[16,9,8,128]{3,2,1,0:T(8,128)(2,1)S(1)}, u32[]{:S(2)}, u32[]{:S(2)}) async-start(bf16[16,9,8,128]{3,2,1,0:T(8,128)(2,1)} %bitcast.28), calls=%async_computation.2 | async-start | bytes 589824 | tf_op jit(solution)/shard_map/all_to_all | solution.py:94
  80.3 10.2 %copy-start = (bf16[10,512,128]{2,1,0:T(8,128)(2,1)S(1)}, bf16[10,512,128]{2,1,0:T(8,128)(2,1)}, u32[]{:S(2)}) copy-start(bf16[10,512,128]{2,1,0:T(8,128)(2,1)} %param.7) | copy-start | bytes 3932164

commit v9 on v8

--- a/solution.py
+++ b/solution.py
@@ -69,17 +69,18 @@
     totals = parts[leaf_bits - 1 :].sum(axis=1)
 
     slab_index = lax.axis_index("slab")
-    relative = jnp.arange(slabs, dtype=jnp.int32)
-    distance = jnp.bitwise_xor(relative, slab_index)
-    level_of = jnp.zeros_like(distance)
-    for bit in range(1, slab_bits):
-        level_of = level_of + (distance >= 2**bit).astype(jnp.int32)
-    received = lax.all_to_all(jnp.take(totals, level_of, axis=0), "slab", 0, 0, tiled=True)
-    by_distance = jnp.take(received, distance, axis=0)
+    outgoing = jnp.zeros((slabs,) + totals.shape[1:], totals.dtype)
+    starts = []
+    for step in range(slab_bits):
+        begin = jnp.bitwise_xor(slab_index >> step, 1) << step
+        starts.append(begin)
+        run = jnp.broadcast_to(totals[step][None], (2**step,) + totals.shape[1:])
+        outgoing = lax.dynamic_update_slice_in_dim(outgoing, run, begin, 0)
+    received = lax.all_to_all(outgoing, "slab", 0, 0, tiled=True)
     couplings_high = []
     for step in range(slab_bits):
         level = leaf_bits + step
-        sibling = by_distance[2**step : 2 ** (step + 1)].sum(axis=0)
+        sibling = lax.dynamic_slice_in_dim(received, starts[step], 2**step, 0).sum(axis=0)
         couplings_high.append((sibling * 2.0 ** (-0.5 * level)).astype(jnp.bfloat16))
 
     high = jnp.stack(couplings_high)

time: 93.2 us -> 92.2 us (0.989)
  local copies, waits for them, and re-layouts: 6.85 us -> 9.99 us
  waiting for transfers between devices: 29.6 us -> 27 us
  starting transfers between devices: 41.8 us -> 40.6 us
    ppermute x1, starting transfers between devices: 12.8 us -> 16 us  [body(): lax.ppermute(jnp.concatenate([projected[0], send.reshape(-1, width), prob...]
    dynamic_update_slice x0 -> x5, local copies, waits for them, and re-layouts: none -> 3.12 us  [body(): outgoing = lax.dynamic_update_slice_in_dim(outgoing, run, begin, 0)]
    ppermute x1, starting transfers between devices: 4.49 us -> 1.92 us  [body(): across = lax.ppermute(probes, PLACED, pairs)]
    all_to_all x1, starting transfers between devices: 14.2 us -> 12 us  [body(): received = lax.all_to_all(outgoing, 'slab', 0, 0, tiled=True)]
    all_to_all x1, waiting for transfers between devices: 8.17 us -> 6.82 us  [body(): lax.all_to_all(paired.reshape(levels - 1, chips, share, width), 'x', 1, 1...]
    broadcast_in_dim x0 -> x2, local copies, waits for them, and re-layouts: none -> 1.32 us  [the longest x1 0.72 us: body(): outgoing = jnp.zeros((slabs,) + totals.shape[1:], totals.dtype)]
    gather x2 -> x0, local copies, waits for them, and re-layouts: 1.26 us -> none  [the longest x1 0.63 us: body(): jnp.take(totals, level_of, axis=0)]
    select_n x4 -> x0, other arithmetic: 0.99 us -> none  [the longest x2 0.85 us: body(): jnp.take(totals, level_of, axis=0)]
  transfers between devices with their start and end apart: 5 -> 5, of which waited for: 4 -> 3; matrix products, arithmetic and copies ran while one was open for 12% -> 10% of each run, Pallas kernels for 0% -> 0%
where the time goes in v9:
time: 92.2 us; the launch traced here: 91.4 us
  starting transfers between devices  40.6 us (44%)
  waiting for transfers between devices  27 us (29%)
  local copies, waits for them, and re-layouts  9.99 us (11%)
  matrix products  7.34 us (8%)
  other arithmetic  4.17 us (5%)
  between operations  2.29 us (2%)
    ppermute x1, starting transfers between devices, body(): lax.ppermute(jnp.concatenate([projected[0], send.reshape(-1, width), prob...  16 us
    all_to_all x1, starting transfers between devices, body(): received = lax.all_to_all(outgoing, 'slab', 0, 0, tiled=True)  12 us
    all_to_all x1, waiting for transfers between devices, body(): received = lax.all_to_all(outgoing, 'slab', 0, 0, tiled=True)  11.8 us
    all_to_all x1, waiting for transfers between devices, body(): lax.all_to_all(everyone.reshape((chips * 2,) + outgoing.shape[1:]), ('x',...  8.38 us
    all_to_all x1, waiting for transfers between devices, body(): lax.all_to_all(paired.reshape(levels - 1, chips, share, width), 'x', 1, 1...  6.82 us
    all_to_all x1, starting transfers between devices, body(): lax.all_to_all(everyone.reshape((chips * 2,) + outgoing.shape[1:]), ('x',...  6.63 us
    dot_general x3, matrix products, body(): jnp.dot(near_blocks[0, member], window, preferred_element_type=jnp.float32)  4.16 us
    all_to_all x1, starting transfers between devices, body(): lax.all_to_all(paired.reshape(levels - 1, chips, share, width), 'x', 1, 1...  4.05 us
  transfers between devices with their start and end apart: 5, of which 3 were waited for; matrix products, arithmetic and copies ran while one was open for 10% of the time, Pallas kernels for 0%

profile of v9, /device:TPU:1, one launch (start us, length us, event | category | flops | bytes accessed | tf_op | source)
XLA Modules:
  0.0 91.4 jit_solution(15839913299802006954)
XLA Ops:
  0.0 0.9 %convert_element_type.115 = f32[512,128]{1,0:T(8,128)S(1)} convert(bf16[512,128]{1,0:T(8,128)(2,1)} %param.4) | non-fusion elementwise | flops 65536 | bytes 393216 | tf_op jit(solution)/shard_map/convert_element_type | solution.py:27
  0.9 1.9 %fusion.10 = f32[10,128,128]{2,1,0:T(8,128)S(1)} fusion(bf16[10,512,128]{2,1,0:T(8,128)(2,1)} %param.7, bf16[512,128]{1,0:T(8,128)(2,1)} %param.4), kind=kOutput, calls=%fused_computation.18 | convolution fusion | flops 167772160 | bytes 2097152 | tf_op jit(solution)/shard_map/lpr,pq->lrq/dot_general | solution.py:12
  2.9 16.0 %collective-permute-start.1 = (f32[1216,128]{1,0:T(8,128)S(1)}, f32[1216,128]{1,0:T(8,128)S(1)}, u32[]{:S(2)}, u32[]{:S(2)}) collective-permute-start(f32[1216,128]{1,0:T(8,128)S(1)} %pad_maximum_fusion), channel_id=1, source_target_pairs={{0,1},{1,0},{2,3},{3,2},{4,5},{5,4},{6,7},{7,6},{8,9},{9,8},{10,11... | collective-permute-start | bytes 1867784 | tf_op jit(solution)/shard_map/ppermute | solution.py:25
  19.0 1.9 %collective-permute-start = (bf16[512,128]{1,0:T(8,128)(2,1)}, bf16[512,128]{1,0:T(8,128)(2,1)}, u32[]{:S(2)}, u32[]{:S(2)}) collective-permute-start(bf16[512,128]{1,0:T(8,128)(2,1)} %param.4), channel_id=1, source_target_pairs={{1,2},{2,1},{3,4},{4,3},{5,6},{6,5},{7,8},{8,7},{9,10},{10,9},{11,... | collective-permute-start | bytes 393224 | tf_op jit(solution)/shard_map/ppermute | solution.py:40
  20.9 0.0 copy-start.4
  20.9 0.0 collective-permute-done.1
  20.9 0.0 copy-start.1
  21.0 0.8 copy.26
  21.8 0.0 copy-done.1
  21.8 4.1 %all-to-all-start = ((f32[9,8,8,128]{3,2,0,1:T(8,128)}), f32[9,8,8,128]{3,2,0,1:T(8,128)}, u32[]{:S(2)}, u32[]{:S(2)}) async-start(f32[9,8,8,128]{3,2,0,1:T(8,128)} %copy.26), calls=%async_computation | async-start | bytes 589824 | tf_op jit(solution)/shard_map/all_to_all | solution.py:57
  25.9 0.0 copy-done.4
  25.9 0.0 slice-start
  25.9 0.6 fusion.28
  28.4 0.0 slice-done
  28.4 0.6 copy.34
  29.1 0.0 copy-start.2
  29.1 0.1 copy.31
  29.2 0.9 copy-done.2
  30.2 0.0 copy-start.3
  30.2 0.0 collective-permute-done
  30.2 1.0 %broadcast_select_fusion.1 = (bf16[512,128]{1,0:T(8,128)(2,1)S(1)}, bf16[512,128]{1,0:T(8,128)(2,1)S(1)}) fusion(bf16[512,128]{1,0:T(8,128)(2,1)} %collective-permute-done, pred[]{:T(512)S(6)} %eq.4, bf16[1216,128]{1,0:T(8,128)(2,1)S(1)} %convert.4), kind=kLoop, calls=%fused_computation.26 | loop fusion | flops 131072 | bytes 524289 | tf_op jit(solution)/shard_map/jit(_where)/select_n | solution.py:43
  31.2 0.9 %pad_maximum_fusion.1 = bf16[1536,128]{1,0:T(8,128)(2,1)S(1)} fusion(bf16[512,128]{1,0:T(8,128)(2,1)S(1)} %get-tuple-element.6, bf16[512,128]{1,0:T(8,128)(2,1)} %param.4, bf16[512,128]{1,0:T(8,128)(2,1)S(1)} %get-tuple-element.5), kind=kLoop, calls=%fused_computation.13 | loop fusion | flops 1179648 | bytes 786432 | tf_op jit(solution)/shard_map/concatenate | solution.py:41
  32.2 6.8 %all-to-all-done = f32[9,8,8,128]{3,2,0,1:T(8,128)} async-done(((f32[9,8,8,128]{3,2,0,1:T(8,128)}), f32[9,8,8,128]{3,2,0,1:T(8,128)}, u32[]{:S(2)}, u32[]{:S(2)}) %all-to-all-start) | async-done | bytes 294944 | tf_op jit(solution)/shard_map/all_to_all | solution.py:57
  39.0 0.9 %slice_reduce_fusion = f32[6,8,128]{2,1,0:T(8,128)S(1)} fusion(f32[9,8,8,128]{3,2,0,1:T(8,128)} %all-to-all-done), kind=kLoop, calls=%fused_computation.15 | loop fusion | flops 43008 | bytes 221184 | tf_op jit(solution)/shard_map/reduce_sum | solution.py:69
  39.9 0.7 broadcast_in_dim.64
  40.7 0.6 slice_bitcast_fusion.1
  41.2 0.6 constant_dynamic-update-slice_fusion.6
  41.8 0.6 broadcast_dynamic-update-slice_fusion.3
  42.5 0.6 broadcast_dynamic-update-slice_fusion.2
  43.1 0.6 broadcast_dynamic-update-slice_fusion.1
  43.7 0.7 broadcast_dynamic-update-slice_fusion
  44.4 0.0 copy-done.3
  44.4 12.0 %all-to-all-start.1 = ((f32[64,8,128]{2,1,0:T(8,128)}), f32[64,8,128]{2,1,0:T(8,128)S(1)}, u32[]{:S(2)}, u32[]{:S(2)}) async-start(f32[64,8,128]{2,1,0:T(8,128)} %broadcast_dynamic-update-slice_fusion), calls=%async_computation.1 | async-start | bytes 524288 | tf_op jit(solution)/shard_map/all_to_all | solution.py:79
  56.4 0.8 fusion.27
  57.2 11.8 %all-to-all-done.1 = f32[64,8,128]{2,1,0:T(8,128)S(1)} async-done(((f32[64,8,128]{2,1,0:T(8,128)}), f32[64,8,128]{2,1,0:T(8,128)S(1)}, u32[]{:S(2)}, u32[]{:S(2)}) %all-to-all-start.1) | async-done | bytes 262176 | tf_op jit(solution)/shard_map/all_to_all | solution.py:79
  69.2 0.8 broadcast_in_dim.76
  70.0 6.6 %all-to-all-start.2 = ((bf16[16,9,8,128]{3,2,1,0:T(8,128)(2,1)}), bf16[16,9,8,128]{3,2,1,0:T(8,128)(2,1)S(1)}, u32[]{:S(2)}, u32[]{:S(2)}) async-start(bf16[16,9,8,128]{3,2,1,0:T(8,128)(2,1)} %bitcast.31), calls=%async_computation.2 | async-start | bytes 589824 | tf_op jit(solution)/shard_map/all_to_all | solution.py:95
  76.6 1.3 %fusion.3 = f32[128,512]{1,0:T(8,128)S(1)} fusion(bf16[1,3,512,512]{3,2,1,0:T(8,128)(2,1)} %param.5, bf16[1536,128]{1,0:T(8,128)(2,1)S(1)} %pad_maximum_fusion.1, s32[]{:T(128)S(6)} %select_n.56), kind=kOutput, calls=%fused_computation.7 | convolution fusion | flops 67108864 | bytes 917508 | tf_op jit(solution)/shard_map/dot_general | solution.py:53
  78.0 1.4 %convolution_add_fusion.2 = f32[128,512]{1,0:T(8,128)S(1)} fusion(f32[128,512]{1,0:T(8,128)S(1)} %fusion.3, bf16[1,3,512,512]{3,2,1,0:T(8,128)(2,1)} %param.5, bf16[1536,128]{1,0:T(8,128)(2,1)S(1)} %pad_maximum_fusion.1, s32[]{:T(128)S(6)} %select_n.55), kind=kOutput, calls=%fused_computation.4 | convolution fusion | flops 67174400 | bytes 1179652 | tf_op jit(solution)/shard_map/dot_general | solution.py:53
  79.3 0.0 copy-start
  79.3 1.5 %convolution_add_fusion.1 = f32[128,512]{1,0:T(8,128)S(1)} fusion(f32[128,512]{1,0:T(8,128)S(1)} %convolution_add_fusion.2, bf16[1,3,512,512]{3,2,1,0:T(8,128)(2,1)} %param.5, bf16[1536,128]{1,0:T(8,128)(2,1)S(1)} %pad_maximum_fusion.1, s32[]{:T(128)S(6)} %select_n.57), kind=kOutput, calls=%fused_computation.3 | convolution fusion | flops 67174400 | bytes 1179652 | tf_op jit(solution)/shard_map/dot_general | solution.py:53
  80.8 8.4 %all-to-all-done.2 = bf16[16,9,8,128]{3,2,1,0:T(8,128)(2,1)S(1)} async-done(((bf16[16,9,8,128]{3,2,1,0:T(8,128)(2,1)}), bf16[16,9,8,128]{3,2,1,0:T(8,128)(2,1)S(1)}, u32[]{:S(2)}, u32[]{:S(2)}) %all-to-all-start.2) | async-done | bytes 294944 | tf_op jit(solution)/shard_map/all_to_all | solution.py:95
  89.2 0.4 fusion.29
  89.6 0.0 copy-done
  89.6 1.0 %fusion.1 = f32[512,128]{0,1:T(8,128)S(1)} fusion(f32[128,512]{1,0:T(8,128)S(1)} %fusion.29, f32[128,512]{1,0:T(8,128)S(1)} %convolution_add_fusion.1, bf16[10,512,128]{2,1,0:T(8,128)(2,1)S(1)} %copy-done, bf16[1216,128]{1,0:T(8,128)(2,1)} %copy-done.3), kind=kOutput, calls=%fused_computation.2 | convolution fusion | flops 16908288 | bytes 950272 | tf_op jit(solution)/shard_map/dot_general | solution.py:104
  90.6 0.8 copy.32
  (27 shorter events, 0.4 us)
Async XLA Ops:
  2.9 18.0 %collective-permute-start.1 = (f32[1216,128]{1,0:T(8,128)S(1)}, f32[1216,128]{1,0:T(8,128)S(1)}, u32[]{:S(2)}, u32[]{:S(2)}) collective-permute-start(f32[1216,128]{1,0:T(8,128)S(1)} %pad_maximum_fusion), channel_id=1, source_target_pairs={{0,1},{1,0},{2,3},{3,2},{4,5},{5,4},{6,7},{7,6},{8,9},{9,8},{10,11... | collective-permute-start | bytes 1867784 | tf_op jit(solution)/shard_map/ppermute | solution.py:25
  19.0 11.2 %collective-permute-start = (bf16[512,128]{1,0:T(8,128)(2,1)}, bf16[512,128]{1,0:T(8,128)(2,1)}, u32[]{:S(2)}, u32[]{:S(2)}) collective-permute-start(bf16[512,128]{1,0:T(8,128)(2,1)} %param.4), channel_id=1, source_target_pairs={{1,2},{2,1},{3,4},{4,3},{5,6},{6,5},{7,8},{8,7},{9,10},{10,9},{11,... | collective-permute-start | bytes 393224 | tf_op jit(solution)/shard_map/ppermute | solution.py:40
  20.9 5.0 %copy-start.4 = (s32[1,3]{1,0:T(1,128)S(1)}, s32[1,3]{1,0:T(1,128)}, u32[]{:S(2)}) copy-start(s32[1,3]{1,0:T(1,128)} %param.6) | copy-start | bytes 40
  20.9 0.9 %copy-start.1 = (f32[1216,128]{1,0:T(8,128)}, f32[1216,128]{1,0:T(8,128)S(1)}, u32[]{:S(2)}) copy-start(f32[1216,128]{1,0:T(8,128)S(1)} %collective-permute-done.1) | copy-start | bytes 1867780
  21.8 17.1 %all-to-all-start = ((f32[9,8,8,128]{3,2,0,1:T(8,128)}), f32[9,8,8,128]{3,2,0,1:T(8,128)}, u32[]{:S(2)}, u32[]{:S(2)}) async-start(f32[9,8,8,128]{3,2,0,1:T(8,128)} %copy.26), calls=%async_computation | async-start | bytes 589824 | tf_op jit(solution)/shard_map/all_to_all | solution.py:57
  25.9 2.5 %slice-start = ((bf16[10,512,128]{2,1,0:T(8,128)(2,1)}), bf16[9,512,128]{2,1,0:T(8,128)(2,1)S(1)}, s32[]{:S(2)}) async-start(bf16[10,512,128]{2,1,0:T(8,128)(2,1)} %param.7), calls=%async_computation.3 | async-start | bytes 2359296 | tf_op jit(solution)/shard_map/slice | solution.py:99
  29.1 1.1 %copy-start.2 = (f32[1216,128]{1,0:T(8,128)S(1)}, f32[1216,128]{1,0:T(8,128)}, u32[]{:S(2)}) copy-start(f32[1216,128]{1,0:T(8,128)} %copy-done.1) | copy-start | bytes 1867780
  30.2 14.2 %copy-start.3 = (bf16[1216,128]{1,0:T(8,128)(2,1)}, bf16[1216,128]{1,0:T(8,128)(2,1)S(1)}, u32[]{:S(2)}) copy-start(bf16[1216,128]{1,0:T(8,128)(2,1)S(1)} %convert.4) | copy-start | bytes 933892
  44.4 24.6 %all-to-all-start.1 = ((f32[64,8,128]{2,1,0:T(8,128)}), f32[64,8,128]{2,1,0:T(8,128)S(1)}, u32[]{:S(2)}, u32[]{:S(2)}) async-start(f32[64,8,128]{2,1,0:T(8,128)} %broadcast_dynamic-update-slice_fusion), calls=%async_computation.1 | async-start | bytes 524288 | tf_op jit(solution)/shard_map/all_to_all | solution.py:79
  70.0 19.2 %all-to-all-start.2 = ((bf16[16,9,8,128]{3,2,1,0:T(8,128)(2,1)}), bf16[16,9,8,128]{3,2,1,0:T(8,128)(2,1)S(1)}, u32[]{:S(2)}, u32[]{:S(2)}) async-start(bf16[16,9,8,128]{3,2,1,0:T(8,128)(2,1)} %bitcast.31), calls=%async_computation.2 | async-start | bytes 589824 | tf_op jit(solution)/shard_map/all_to_all | solution.py:95
  79.3 10.2 %copy-start = (bf16[10,512,128]{2,1,0:T(8,128)(2,1)S(1)}, bf16[10,512,128]{2,1,0:T(8,128)(2,1)}, u32[]{:S(2)}) copy-start(bf16[10,512,128]{2,1,0:T(8,128)(2,1)} %param.7) | copy-start | bytes 3932164

commit v10 on v9

--- a/solution.py
+++ b/solution.py
@@ -69,13 +69,15 @@
     totals = parts[leaf_bits - 1 :].sum(axis=1)
 
     slab_index = lax.axis_index("slab")
-    outgoing = jnp.zeros((slabs,) + totals.shape[1:], totals.dtype)
+    distance = jnp.bitwise_xor(jnp.arange(slabs, dtype=jnp.int32), slab_index)
+    outgoing = jnp.broadcast_to(totals[0][None], (slabs,) + totals.shape[1:])
     starts = []
     for step in range(slab_bits):
-        begin = jnp.bitwise_xor(slab_index >> step, 1) << step
-        starts.append(begin)
-        run = jnp.broadcast_to(totals[step][None], (2**step,) + totals.shape[1:])
-        outgoing = lax.dynamic_update_slice_in_dim(outgoing, run, begin, 0)
+        starts.append(jnp.bitwise_xor(slab_index >> step, 1) << step)
+        if step:
+            outgoing = jnp.where(
+                (distance >= 2**step)[:, None, None], totals[step][None], outgoing
+            )
     received = lax.all_to_all(outgoing, "slab", 0, 0, tiled=True)
     couplings_high = []
     for step in range(slab_bits):

time: 92.2 us -> 89.7 us (0.973)
  local copies, waits for them, and re-layouts: 9.99 us -> 5.62 us
  other arithmetic: 4.17 us -> 5.9 us
    dynamic_update_slice x5 -> x0, local copies, waits for them, and re-layouts: 3.12 us -> none  [body(): outgoing = lax.dynamic_update_slice_in_dim(outgoing, run, begin, 0)]
    broadcast_in_dim x2 -> x1, local copies, waits for them, and re-layouts: 1.32 us -> 0.01 us  [body(): jnp.where((distance >= 2 ** step)[:, None, None], totals[step][None], out...]
    select_n x0 -> x1, other arithmetic: none -> 1.2 us  [body(): jnp.where((distance >= 2 ** step)[:, None, None], totals[step][None], out...]
  transfers between devices with their start and end apart: 5 -> 5, of which waited for: 3 -> 3; matrix products, arithmetic and copies ran while one was open for 10% -> 11% of each run, Pallas kernels for 0% -> 0%
where the time goes in v10:
time: 89.7 us; the launch traced here: 88.8 us
  starting transfers between devices  40.7 us (45%)
  waiting for transfers between devices  27 us (30%)
  matrix products  7.35 us (8%)
  other arithmetic  5.9 us (7%)
  local copies, waits for them, and re-layouts  5.62 us (6%)
  between operations  2.31 us (3%)
    ppermute x1, starting transfers between devices, body(): lax.ppermute(jnp.concatenate([projected[0], send.reshape(-1, width), prob...  16 us
    all_to_all x1, starting transfers between devices, body(): received = lax.all_to_all(outgoing, 'slab', 0, 0, tiled=True)  12 us
    all_to_all x1, waiting for transfers between devices, body(): received = lax.all_to_all(outgoing, 'slab', 0, 0, tiled=True)  11.7 us
    all_to_all x1, waiting for transfers between devices, body(): lax.all_to_all(everyone.reshape((chips * 2,) + outgoing.shape[1:]), ('x',...  8.38 us
    all_to_all x1, waiting for transfers between devices, body(): lax.all_to_all(paired.reshape(levels - 1, chips, share, width), 'x', 1, 1...  6.88 us
    all_to_all x1, starting transfers between devices, body(): lax.all_to_all(everyone.reshape((chips * 2,) + outgoing.shape[1:]), ('x',...  6.71 us
    dot_general x3, matrix products, body(): jnp.dot(near_blocks[0, member], window, preferred_element_type=jnp.float32)  4.16 us
    all_to_all x1, starting transfers between devices, body(): lax.all_to_all(paired.reshape(levels - 1, chips, share, width), 'x', 1, 1...  4.05 us
  transfers between devices with their start and end apart: 5, of which 3 were waited for; matrix products, arithmetic and copies ran while one was open for 11% of the time, Pallas kernels for 0%

profile of v10, /device:TPU:1, one launch (start us, length us, event | category | flops | bytes accessed | tf_op | source)
XLA Modules:
  0.0 88.8 jit_solution(8419881104918761155)
XLA Ops:
  0.0 0.9 %convert_element_type.115 = f32[512,128]{1,0:T(8,128)S(1)} convert(bf16[512,128]{1,0:T(8,128)(2,1)} %param.4) | non-fusion elementwise | flops 65536 | bytes 393216 | tf_op jit(solution)/shard_map/convert_element_type | solution.py:27
  0.9 1.9 %fusion.10 = f32[10,128,128]{2,1,0:T(8,128)S(1)} fusion(bf16[10,512,128]{2,1,0:T(8,128)(2,1)} %param.7, bf16[512,128]{1,0:T(8,128)(2,1)} %param.4), kind=kOutput, calls=%fused_computation.19 | convolution fusion | flops 167772160 | bytes 2097152 | tf_op jit(solution)/shard_map/lpr,pq->lrq/dot_general | solution.py:12
  2.8 0.0 copy-start.4
  3.0 16.0 %collective-permute-start.1 = (f32[1216,128]{1,0:T(8,128)S(1)}, f32[1216,128]{1,0:T(8,128)S(1)}, u32[]{:S(2)}, u32[]{:S(2)}) collective-permute-start(f32[1216,128]{1,0:T(8,128)S(1)} %pad_maximum_fusion), channel_id=1, source_target_pairs={{0,1},{1,0},{2,3},{3,2},{4,5},{5,4},{6,7},{7,6},{8,9},{9,8},{10,11... | collective-permute-start | bytes 1867784 | tf_op jit(solution)/shard_map/ppermute | solution.py:25
  19.0 1.9 %collective-permute-start = (bf16[512,128]{1,0:T(8,128)(2,1)}, bf16[512,128]{1,0:T(8,128)(2,1)}, u32[]{:S(2)}, u32[]{:S(2)}) collective-permute-start(bf16[512,128]{1,0:T(8,128)(2,1)} %param.4), channel_id=1, source_target_pairs={{1,2},{2,1},{3,4},{4,3},{5,6},{6,5},{7,8},{8,7},{9,10},{10,9},{11,... | collective-permute-start | bytes 393224 | tf_op jit(solution)/shard_map/ppermute | solution.py:40
  20.9 0.0 copy-done.4
  21.0 0.6 fusion.31
  21.6 0.0 collective-permute-done.1
  21.6 0.0 copy-start.1
  21.7 0.8 copy.26
  22.5 0.0 copy-done.1
  22.5 4.1 %all-to-all-start = ((f32[9,8,8,128]{3,2,0,1:T(8,128)}), f32[9,8,8,128]{3,2,0,1:T(8,128)}, u32[]{:S(2)}, u32[]{:S(2)}) async-start(f32[9,8,8,128]{3,2,0,1:T(8,128)} %copy.26), calls=%async_computation | async-start | bytes 589824 | tf_op jit(solution)/shard_map/all_to_all | solution.py:57
  26.6 0.0 slice-start
  26.6 0.5 fusion.29
  29.0 0.0 slice-done
  29.0 0.6 copy.34
  29.6 0.0 copy-start.2
  29.6 0.1 copy.31
  29.8 0.0 copy-start.5
  29.8 0.9 copy-done.2
  30.7 0.0 copy-start.3
  30.8 0.0 collective-permute-done
  30.8 1.0 %broadcast_select_fusion.1 = (bf16[512,128]{1,0:T(8,128)(2,1)S(1)}, bf16[512,128]{1,0:T(8,128)(2,1)S(1)}) fusion(bf16[512,128]{1,0:T(8,128)(2,1)} %collective-permute-done, pred[]{:T(512)S(6)} %eq.4, bf16[1216,128]{1,0:T(8,128)(2,1)S(1)} %convert.4), kind=kLoop, calls=%fused_computation.27 | loop fusion | flops 131072 | bytes 524289 | tf_op jit(solution)/shard_map/jit(_where)/select_n | solution.py:43
  31.8 0.9 %pad_maximum_fusion.1 = bf16[1536,128]{1,0:T(8,128)(2,1)S(1)} fusion(bf16[512,128]{1,0:T(8,128)(2,1)S(1)} %get-tuple-element.6, bf16[512,128]{1,0:T(8,128)(2,1)} %param.4, bf16[512,128]{1,0:T(8,128)(2,1)S(1)} %get-tuple-element.5), kind=kLoop, calls=%fused_computation.13 | loop fusion | flops 1179648 | bytes 786432 | tf_op jit(solution)/shard_map/concatenate | solution.py:41
  32.7 6.9 %all-to-all-done = f32[9,8,8,128]{3,2,0,1:T(8,128)} async-done(((f32[9,8,8,128]{3,2,0,1:T(8,128)}), f32[9,8,8,128]{3,2,0,1:T(8,128)}, u32[]{:S(2)}, u32[]{:S(2)}) %all-to-all-start) | async-done | bytes 294944 | tf_op jit(solution)/shard_map/all_to_all | solution.py:57
  39.6 0.9 %slice_reduce_fusion = f32[6,8,128]{2,1,0:T(8,128)S(1)} fusion(f32[9,8,8,128]{3,2,0,1:T(8,128)} %all-to-all-done), kind=kLoop, calls=%fused_computation.16 | loop fusion | flops 43008 | bytes 221184 | tf_op jit(solution)/shard_map/reduce_sum | solution.py:69
  40.6 0.0 copy-done.5
  40.6 1.2 %select_select_fusion = f32[64,8,128]{2,1,0:T(8,128)} fusion(f32[8,128]{1,0:T(8,128)S(1)} %get-tuple-element.11, f32[8,128]{1,0:T(8,128)S(1)} %get-tuple-element.12, f32[8,128]{1,0:T(8,128)S(1)} %get-tuple-element.13, f32[8,128]{1,0:T(8,128)S(1)} %get-tuple-element.14, f32[8,128]{1,0:T(8,128)S(1)} %get-tuple-element.15, f32[8,128]{1,0:T(8,128)S(1)} %get-tuple-element.10, ...), kind=kLoop, calls=%fused_computation.15 | loop fusion | flops 327680 | bytes 287040 | tf_op jit(solution)/shard_map/jit(_where)/select_n | solution.py:78
  41.8 12.0 %all-to-all-start.1 = ((f32[64,8,128]{2,1,0:T(8,128)}), f32[64,8,128]{2,1,0:T(8,128)S(1)}, u32[]{:S(2)}, u32[]{:S(2)}) async-start(f32[64,8,128]{2,1,0:T(8,128)} %select_select_fusion), calls=%async_computation.1 | async-start | bytes 524288 | tf_op jit(solution)/shard_map/all_to_all | solution.py:81
  53.8 0.8 fusion.30
  54.6 0.0 copy-done.3
  54.7 11.7 %all-to-all-done.1 = f32[64,8,128]{2,1,0:T(8,128)S(1)} async-done(((f32[64,8,128]{2,1,0:T(8,128)}), f32[64,8,128]{2,1,0:T(8,128)S(1)}, u32[]{:S(2)}, u32[]{:S(2)}) %all-to-all-start.1) | async-done | bytes 262176 | tf_op jit(solution)/shard_map/all_to_all | solution.py:81
  66.6 0.8 broadcast_in_dim.122
  67.3 6.7 %all-to-all-start.2 = ((bf16[16,9,8,128]{3,2,1,0:T(8,128)(2,1)}), bf16[16,9,8,128]{3,2,1,0:T(8,128)(2,1)S(1)}, u32[]{:S(2)}, u32[]{:S(2)}) async-start(bf16[16,9,8,128]{3,2,1,0:T(8,128)(2,1)} %bitcast.32), calls=%async_computation.2 | async-start | bytes 589824 | tf_op jit(solution)/shard_map/all_to_all | solution.py:97
  74.1 1.3 %fusion.3 = f32[128,512]{1,0:T(8,128)S(1)} fusion(bf16[1,3,512,512]{3,2,1,0:T(8,128)(2,1)} %param.5, bf16[1536,128]{1,0:T(8,128)(2,1)S(1)} %pad_maximum_fusion.1, s32[]{:T(128)S(6)} %select_n.66), kind=kOutput, calls=%fused_computation.7 | convolution fusion | flops 67108864 | bytes 917508 | tf_op jit(solution)/shard_map/dot_general | solution.py:53
  75.4 1.4 %convolution_add_fusion.2 = f32[128,512]{1,0:T(8,128)S(1)} fusion(f32[128,512]{1,0:T(8,128)S(1)} %fusion.3, bf16[1,3,512,512]{3,2,1,0:T(8,128)(2,1)} %param.5, bf16[1536,128]{1,0:T(8,128)(2,1)S(1)} %pad_maximum_fusion.1, s32[]{:T(128)S(6)} %select_n.65), kind=kOutput, calls=%fused_computation.4 | convolution fusion | flops 67174400 | bytes 1179652 | tf_op jit(solution)/shard_map/dot_general | solution.py:53
  76.8 0.0 copy-start
  76.8 1.5 %convolution_add_fusion.1 = f32[128,512]{1,0:T(8,128)S(1)} fusion(f32[128,512]{1,0:T(8,128)S(1)} %convolution_add_fusion.2, bf16[1,3,512,512]{3,2,1,0:T(8,128)(2,1)} %param.5, bf16[1536,128]{1,0:T(8,128)(2,1)S(1)} %pad_maximum_fusion.1, s32[]{:T(128)S(6)} %select_n.67), kind=kOutput, calls=%fused_computation.3 | convolution fusion | flops 67174400 | bytes 1179652 | tf_op jit(solution)/shard_map/dot_general | solution.py:53
  78.3 8.4 %all-to-all-done.2 = bf16[16,9,8,128]{3,2,1,0:T(8,128)(2,1)S(1)} async-done(((bf16[16,9,8,128]{3,2,1,0:T(8,128)(2,1)}), bf16[16,9,8,128]{3,2,1,0:T(8,128)(2,1)S(1)}, u32[]{:S(2)}, u32[]{:S(2)}) %all-to-all-start.2) | async-done | bytes 294944 | tf_op jit(solution)/shard_map/all_to_all | solution.py:97
  86.6 0.4 fusion.32
  87.0 0.0 copy-done
  87.0 1.0 %fusion.1 = f32[512,128]{0,1:T(8,128)S(1)} fusion(f32[128,512]{1,0:T(8,128)S(1)} %fusion.32, f32[128,512]{1,0:T(8,128)S(1)} %convolution_add_fusion.1, bf16[10,512,128]{2,1,0:T(8,128)(2,1)S(1)} %copy-done, bf16[1216,128]{1,0:T(8,128)(2,1)} %copy-done.3), kind=kOutput, calls=%fused_computation.2 | convolution fusion | flops 16908288 | bytes 950272 | tf_op jit(solution)/shard_map/dot_general | solution.py:106
  88.0 0.8 copy.32
  (30 shorter events, 0.5 us)
Async XLA Ops:
  2.8 18.1 %copy-start.4 = (s32[1,3]{1,0:T(1,128)S(1)}, s32[1,3]{1,0:T(1,128)}, u32[]{:S(2)}) copy-start(s32[1,3]{1,0:T(1,128)} %param.6) | copy-start | bytes 40
  3.0 18.7 %collective-permute-start.1 = (f32[1216,128]{1,0:T(8,128)S(1)}, f32[1216,128]{1,0:T(8,128)S(1)}, u32[]{:S(2)}, u32[]{:S(2)}) collective-permute-start(f32[1216,128]{1,0:T(8,128)S(1)} %pad_maximum_fusion), channel_id=1, source_target_pairs={{0,1},{1,0},{2,3},{3,2},{4,5},{5,4},{6,7},{7,6},{8,9},{9,8},{10,11... | collective-permute-start | bytes 1867784 | tf_op jit(solution)/shard_map/ppermute | solution.py:25
  19.0 11.8 %collective-permute-start = (bf16[512,128]{1,0:T(8,128)(2,1)}, bf16[512,128]{1,0:T(8,128)(2,1)}, u32[]{:S(2)}, u32[]{:S(2)}) collective-permute-start(bf16[512,128]{1,0:T(8,128)(2,1)} %param.4), channel_id=1, source_target_pairs={{1,2},{2,1},{3,4},{4,3},{5,6},{6,5},{7,8},{8,7},{9,10},{10,9},{11,... | collective-permute-start | bytes 393224 | tf_op jit(solution)/shard_map/ppermute | solution.py:40
  21.6 0.9 %copy-start.1 = (f32[1216,128]{1,0:T(8,128)}, f32[1216,128]{1,0:T(8,128)S(1)}, u32[]{:S(2)}) copy-start(f32[1216,128]{1,0:T(8,128)S(1)} %collective-permute-done.1) | copy-start | bytes 1867780
  22.5 17.1 %all-to-all-start = ((f32[9,8,8,128]{3,2,0,1:T(8,128)}), f32[9,8,8,128]{3,2,0,1:T(8,128)}, u32[]{:S(2)}, u32[]{:S(2)}) async-start(f32[9,8,8,128]{3,2,0,1:T(8,128)} %copy.26), calls=%async_computation | async-start | bytes 589824 | tf_op jit(solution)/shard_map/all_to_all | solution.py:57
  26.6 2.4 %slice-start = ((bf16[10,512,128]{2,1,0:T(8,128)(2,1)}), bf16[9,512,128]{2,1,0:T(8,128)(2,1)S(1)}, s32[]{:S(2)}) async-start(bf16[10,512,128]{2,1,0:T(8,128)(2,1)} %param.7), calls=%async_computation.3 | async-start | bytes 2359296 | tf_op jit(solution)/shard_map/slice | solution.py:101
  29.6 1.1 %copy-start.2 = (f32[1216,128]{1,0:T(8,128)S(1)}, f32[1216,128]{1,0:T(8,128)}, u32[]{:S(2)}) copy-start(f32[1216,128]{1,0:T(8,128)} %copy-done.1) | copy-start | bytes 1867780
  29.8 10.8 %copy-start.5 = (pred[64]{0:T(512)(128)(4,1)S(1)}, pred[64]{0:T(512)(128)(4,1)}, u32[]{:S(2)}) copy-start(pred[64]{0:T(512)(128)(4,1)} %fusion.29) | copy-start | bytes 196
  30.7 23.9 %copy-start.3 = (bf16[1216,128]{1,0:T(8,128)(2,1)}, bf16[1216,128]{1,0:T(8,128)(2,1)S(1)}, u32[]{:S(2)}) copy-start(bf16[1216,128]{1,0:T(8,128)(2,1)S(1)} %convert.4) | copy-start | bytes 933892
  41.8 24.6 %all-to-all-start.1 = ((f32[64,8,128]{2,1,0:T(8,128)}), f32[64,8,128]{2,1,0:T(8,128)S(1)}, u32[]{:S(2)}, u32[]{:S(2)}) async-start(f32[64,8,128]{2,1,0:T(8,128)} %select_select_fusion), calls=%async_computation.1 | async-start | bytes 524288 | tf_op jit(solution)/shard_map/all_to_all | solution.py:81
  67.3 19.3 %all-to-all-start.2 = ((bf16[16,9,8,128]{3,2,1,0:T(8,128)(2,1)}), bf16[16,9,8,128]{3,2,1,0:T(8,128)(2,1)S(1)}, u32[]{:S(2)}, u32[]{:S(2)}) async-start(bf16[16,9,8,128]{3,2,1,0:T(8,128)(2,1)} %bitcast.32), calls=%async_computation.2 | async-start | bytes 589824 | tf_op jit(solution)/shard_map/all_to_all | solution.py:97
  76.8 10.2 %copy-start = (bf16[10,512,128]{2,1,0:T(8,128)(2,1)S(1)}, bf16[10,512,128]{2,1,0:T(8,128)(2,1)}, u32[]{:S(2)}) copy-start(bf16[10,512,128]{2,1,0:T(8,128)(2,1)} %param.7) | copy-start | bytes 3932164

commit v11 on v10

--- a/solution.py
+++ b/solution.py
@@ -103,10 +103,9 @@
         .transpose(1, 3, 2, 0, 4)
         .reshape(leaf_rows, -1)
     )
-    output = near_sum + jnp.dot(far_basis[0], coupling_first, preferred_element_type=jnp.float32)
-    output = output + jnp.dot(
-        far_rest, returned.reshape(-1, width), preferred_element_type=jnp.float32
-    )
+    far_all = jnp.concatenate([far_basis[0], far_rest], axis=1)
+    coupling_all = jnp.concatenate([coupling_first, returned.reshape(-1, width)], axis=0)
+    output = near_sum + jnp.dot(far_all, coupling_all, preferred_element_type=jnp.float32)
     return output
 
 

time: 89.7 us -> 87.6 us (0.977)
  other arithmetic: 5.9 us -> 2.17 us
  matrix products: 7.35 us -> 4.94 us
  waiting for transfers between devices: 27 us -> 29.4 us
  local copies, waits for them, and re-layouts: 5.62 us -> 7.6 us
    dot_general x3, matrix products: 4.16 us -> 1.65 us  [body(): jnp.dot(near_blocks[0, member], window, preferred_element_type=jnp.float32)]
    all_to_all x1, waiting for transfers between devices: 8.38 us -> 10.9 us  [body(): lax.all_to_all(everyone.reshape((chips * 2,) + outgoing.shape[1:]), ('x',...]
    slice x2, local copies, waits for them, and re-layouts: 0.01 us -> 1.27 us  [body(): far_basis[1:].reshape(levels - 1, leaf_rows, 2, chips, share)]
    transpose x1, local copies, waits for them, and re-layouts: 0.11 us -> 1.14 us  [body(): far_rest = far_basis[1:].reshape(levels - 1, leaf_rows, 2, chips, share)....]
    select_n x1, other arithmetic: 1.04 us -> 0.02 us  [body(): jnp.where(core == 0, across, partner)]
    all_to_all x1, waiting for transfers between devices: 6.88 us -> 5.93 us  [body(): lax.all_to_all(paired.reshape(levels - 1, chips, share, width), 'x', 1, 1...]
    reduce_sum x1, other arithmetic: 0.95 us -> 0.01 us  [body(): totals = parts[leaf_bits - 1:].sum(axis=1)]
    concatenate x1, other arithmetic: 0.93 us -> 0.03 us  [body(): jnp.concatenate([jnp.where(core == 0, across, partner), probes, jnp.where...]
  transfers between devices with their start and end apart: 5 -> 5, of which waited for: 3 -> 3; matrix products, arithmetic and copies ran while one was open for 11% -> 7% of each run, Pallas kernels for 0% -> 0%
where the time goes in v11:
time: 87.6 us; the launch traced here: 87.1 us
  starting transfers between devices  40.7 us (46%)
  waiting for transfers between devices  29.4 us (34%)
  local copies, waits for them, and re-layouts  7.6 us (9%)
  matrix products  4.94 us (6%)
  between operations  2.28 us (3%)
  other arithmetic  2.17 us (2%)
    ppermute x1, starting transfers between devices, body(): lax.ppermute(jnp.concatenate([projected[0], send.reshape(-1, width), prob...  16 us
    all_to_all x1, starting transfers between devices, body(): received = lax.all_to_all(outgoing, 'slab', 0, 0, tiled=True)  12.7 us
    all_to_all x1, waiting for transfers between devices, body(): received = lax.all_to_all(outgoing, 'slab', 0, 0, tiled=True)  12.6 us
    all_to_all x1, waiting for transfers between devices, body(): lax.all_to_all(everyone.reshape((chips * 2,) + outgoing.shape[1:]), ('x',...  10.9 us
    all_to_all x1, starting transfers between devices, body(): lax.all_to_all(everyone.reshape((chips * 2,) + outgoing.shape[1:]), ('x',...  6.63 us
    all_to_all x1, waiting for transfers between devices, body(): lax.all_to_all(paired.reshape(levels - 1, chips, share, width), 'x', 1, 1...  5.93 us
    all_to_all x1, starting transfers between devices, body(): lax.all_to_all(paired.reshape(levels - 1, chips, share, width), 'x', 1, 1...  3.42 us
    unnamed x14, local copies, waits for them, and re-layouts  2.06 us
  transfers between devices with their start and end apart: 5, of which 3 were waited for; matrix products, arithmetic and copies ran while one was open for 7% of the time, Pallas kernels for 0%

profile of v11, /device:TPU:1, one launch (start us, length us, event | category | flops | bytes accessed | tf_op | source)
XLA Modules:
  0.0 87.1 jit_solution(5111691234453882731)
XLA Ops:
  0.0 0.0 copy-start.1
  0.0 1.9 %fusion.18 = f32[10,128,128]{2,1,0:T(8,128)S(1)} fusion(bf16[10,512,128]{2,1,0:T(8,128)(2,1)} %param.7, bf16[512,128]{1,0:T(8,128)(2,1)} %param.4), kind=kOutput, calls=%fused_computation.24 | convolution fusion | flops 167772160 | bytes 2097152 | tf_op jit(solution)/shard_map/lpr,pq->lrq/dot_general | solution.py:12
  1.9 0.0 copy-start.4
  2.0 0.0 copy-done.1
  2.1 16.0 %collective-permute-start.1 = (f32[1216,128]{1,0:T(8,128)S(1)}, f32[1216,128]{1,0:T(8,128)S(1)}, u32[]{:S(2)}, u32[]{:S(2)}) collective-permute-start(f32[1216,128]{1,0:T(8,128)S(1)} %pad_maximum_fusion), channel_id=1, source_target_pairs={{0,1},{1,0},{2,3},{3,2},{4,5},{5,4},{6,7},{7,6},{8,9},{9,8},{10,11... | collective-permute-start | bytes 1867784 | tf_op jit(solution)/shard_map/ppermute | solution.py:25
  18.1 1.9 %collective-permute-start = (bf16[512,128]{1,0:T(8,128)(2,1)S(1)}, bf16[512,128]{1,0:T(8,128)(2,1)S(1)}, u32[]{:S(2)}, u32[]{:S(2)}) collective-permute-start(bf16[512,128]{1,0:T(8,128)(2,1)S(1)} %copy-done.1), channel_id=1, source_target_pairs={{1,2},{2,1},{3,4},{4,3},{5,6},{6,5},{7,8},{8,7},{9,10},{10,9},{11,... | collective-permute-start | bytes 393224 | tf_op jit(solution)/shard_map/ppermute | solution.py:40
  20.1 0.0 copy-done.4
  20.1 0.7 fusion.38
  20.8 0.0 collective-permute-done.1
  20.8 0.7 copy.34
  21.6 3.4 %all-to-all-start = ((f32[9,8,8,128]{3,2,0,1:T(8,128)}), f32[9,8,8,128]{3,2,0,1:T(8,128)S(1)}, u32[]{:S(2)}, u32[]{:S(2)}) async-start(f32[9,8,8,128]{3,2,0,1:T(8,128)} %copy.34), calls=%async_computation | async-start | bytes 589824 | tf_op jit(solution)/shard_map/all_to_all | solution.py:57
  25.0 0.5 fusion.35
  27.5 0.0 slice-start
  27.5 1.3 %slice-done = bf16[9,512,128]{2,1,0:T(8,128)(2,1)S(1)} async-done(((bf16[10,512,128]{2,1,0:T(8,128)(2,1)}), bf16[9,512,128]{2,1,0:T(8,128)(2,1)S(1)}, s32[]{:S(2)}) %slice-start) | async-done | bytes 1179672 | tf_op jit(solution)/shard_map/slice | solution.py:101
  28.7 0.6 copy.43
  29.3 0.0 slice-start.1
  29.4 1.1 %copy.33 = bf16[512,8,2,9,8]{0,4,3,2,1:T(8,128)(2,1)} copy(bf16[512,8,2,9,8]{0,4,1,2,3:T(8,128)(2,1)S(1)} %bitcast.75) | data formatting | bytes 2359296 | tf_op jit(solution)/shard_map/transpose | solution.py:103
  30.5 0.0 slice-done.1
  30.5 0.8 copy.42
  31.3 0.0 copy-start.5
  31.3 0.0 copy-start.3
  31.3 0.0 collective-permute-done
  31.3 0.7 copy-done.3
  32.1 5.9 %all-to-all-done = f32[9,8,8,128]{3,2,0,1:T(8,128)S(1)} async-done(((f32[9,8,8,128]{3,2,0,1:T(8,128)}), f32[9,8,8,128]{3,2,0,1:T(8,128)S(1)}, u32[]{:S(2)}, u32[]{:S(2)}) %all-to-all-start) | async-done | bytes 294944 | tf_op jit(solution)/shard_map/all_to_all | solution.py:57
  38.0 0.0 copy-done.5
  38.0 1.2 %select_select_fusion = f32[64,8,128]{2,1,0:T(8,128)} fusion(f32[8,128]{1,0:T(8,128)S(1)} %get-tuple-element.11, f32[8,128]{1,0:T(8,128)S(1)} %get-tuple-element.12, f32[8,128]{1,0:T(8,128)S(1)} %get-tuple-element.13, f32[8,128]{1,0:T(8,128)S(1)} %get-tuple-element.14, f32[8,128]{1,0:T(8,128)S(1)} %get-tuple-element.15, f32[8,128]{1,0:T(8,128)S(1)} %get-tuple-element.10, ...), kind=kLoop, calls=%fused_computation.21 | loop fusion | flops 327680 | bytes 287040 | tf_op jit(solution)/shard_map/jit(_where)/select_n | solution.py:78
  39.2 0.0 copy-start
  39.2 12.7 %all-to-all-start.1 = ((f32[64,8,128]{2,1,0:T(8,128)}), f32[64,8,128]{2,1,0:T(8,128)S(1)}, u32[]{:S(2)}, u32[]{:S(2)}) async-start(f32[64,8,128]{2,1,0:T(8,128)} %select_select_fusion), calls=%async_computation.1 | async-start | bytes 524288 | tf_op jit(solution)/shard_map/all_to_all | solution.py:81
  52.1 12.6 %all-to-all-done.1 = f32[64,8,128]{2,1,0:T(8,128)S(1)} async-done(((f32[64,8,128]{2,1,0:T(8,128)}), f32[64,8,128]{2,1,0:T(8,128)S(1)}, u32[]{:S(2)}, u32[]{:S(2)}) %all-to-all-start.1) | async-done | bytes 262176 | tf_op jit(solution)/shard_map/all_to_all | solution.py:81
  64.9 0.8 broadcast_in_dim.122
  65.6 6.6 %all-to-all-start.2 = ((bf16[16,9,8,128]{3,2,1,0:T(8,128)(2,1)}), bf16[16,9,8,128]{3,2,1,0:T(8,128)(2,1)S(1)}, u32[]{:S(2)}, u32[]{:S(2)}) async-start(bf16[16,9,8,128]{3,2,1,0:T(8,128)(2,1)} %bitcast.36), calls=%async_computation.2 | async-start | bytes 589824 | tf_op jit(solution)/shard_map/all_to_all | solution.py:97
  72.2 0.0 copy-done
  72.2 0.3 fusion.9
  72.6 0.0 copy-start.2
  72.6 0.0 slice-start.2
  72.6 0.3 convolution_add_fusion.1
  72.9 1.0 %fusion.7 = f32[512,128]{0,1:T(8,128)} fusion(f32[128,512]{1,0:T(8,128)S(1)} %convolution_add_fusion.1, bf16[1,3,512,512]{3,2,1,0:T(8,128)(2,1)S(1)} %copy-done, bf16[1536,128]{1,0:T(8,128)(2,1)S(1)} %pad_maximum_fusion.1, s32[]{:T(128)S(6)} %select_n.67), kind=kOutput, calls=%fused_computation.6 | convolution fusion | flops 67174400 | bytes 1179652 | tf_op jit(solution)/shard_map/dot_general | solution.py:53
  73.9 10.9 %all-to-all-done.2 = bf16[16,9,8,128]{3,2,1,0:T(8,128)(2,1)S(1)} async-done(((bf16[16,9,8,128]{3,2,1,0:T(8,128)(2,1)}), bf16[16,9,8,128]{3,2,1,0:T(8,128)(2,1)S(1)}, u32[]{:S(2)}, u32[]{:S(2)}) %all-to-all-start.2) | async-done | bytes 294944 | tf_op jit(solution)/shard_map/all_to_all | solution.py:97
  84.8 0.0 copy-done.2
  84.8 0.0 slice-done.2
  84.8 1.4 %fusion.4 = f32[512,128]{0,1:T(8,128)S(1)} fusion(f32[512,128]{0,1:T(8,128)} %fusion.7, bf16[512,1152]{0,1:T(8,128)(2,1)S(1)} %bitcast.78, bf16[512,128]{0,1:T(8,128)(2,1)} %bitcast.80, bf16[1152,128]{1,0:T(8,128)(2,1)S(1)} %bitcast.79, bf16[128,128]{1,0:T(8,128)(2,1)S(1)} %slice-done.2), kind=kOutput, calls=%fused_computation.4 | convolution fusion | flops 171114496 | bytes 2162688 | tf_op jit(solution)/shard_map/dot_general | solution.py:108
  86.2 0.8 copy.39
  (35 shorter events, 0.6 us)
Async XLA Ops:
  0.0 2.0 %copy-start.1 = (bf16[512,128]{1,0:T(8,128)(2,1)S(1)}, bf16[512,128]{1,0:T(8,128)(2,1)}, u32[]{:S(2)}) copy-start(bf16[512,128]{1,0:T(8,128)(2,1)} %param.4) | copy-start | bytes 393220
  1.9 18.1 %copy-start.4 = (s32[1,3]{1,0:T(1,128)S(1)}, s32[1,3]{1,0:T(1,128)}, u32[]{:S(2)}) copy-start(s32[1,3]{1,0:T(1,128)} %param.6) | copy-start | bytes 40
  2.1 18.7 %collective-permute-start.1 = (f32[1216,128]{1,0:T(8,128)S(1)}, f32[1216,128]{1,0:T(8,128)S(1)}, u32[]{:S(2)}, u32[]{:S(2)}) collective-permute-start(f32[1216,128]{1,0:T(8,128)S(1)} %pad_maximum_fusion), channel_id=1, source_target_pairs={{0,1},{1,0},{2,3},{3,2},{4,5},{5,4},{6,7},{7,6},{8,9},{9,8},{10,11... | collective-permute-start | bytes 1867784 | tf_op jit(solution)/shard_map/ppermute | solution.py:25
  18.1 13.2 %collective-permute-start = (bf16[512,128]{1,0:T(8,128)(2,1)S(1)}, bf16[512,128]{1,0:T(8,128)(2,1)S(1)}, u32[]{:S(2)}, u32[]{:S(2)}) collective-permute-start(bf16[512,128]{1,0:T(8,128)(2,1)S(1)} %copy-done.1), channel_id=1, source_target_pairs={{1,2},{2,1},{3,4},{4,3},{5,6},{6,5},{7,8},{8,7},{9,10},{10,9},{11,... | collective-permute-start | bytes 393224 | tf_op jit(solution)/shard_map/ppermute | solution.py:40
  21.6 16.4 %all-to-all-start = ((f32[9,8,8,128]{3,2,0,1:T(8,128)}), f32[9,8,8,128]{3,2,0,1:T(8,128)S(1)}, u32[]{:S(2)}, u32[]{:S(2)}) async-start(f32[9,8,8,128]{3,2,0,1:T(8,128)} %copy.34), calls=%async_computation | async-start | bytes 589824 | tf_op jit(solution)/shard_map/all_to_all | solution.py:57
  27.5 1.3 %slice-start = ((bf16[10,512,128]{2,1,0:T(8,128)(2,1)}), bf16[9,512,128]{2,1,0:T(8,128)(2,1)S(1)}, s32[]{:S(2)}) async-start(bf16[10,512,128]{2,1,0:T(8,128)(2,1)} %param.7), calls=%async_computation.3 | async-start | bytes 2359296 | tf_op jit(solution)/shard_map/slice | solution.py:101
  29.3 1.2 %slice-start.1 = ((bf16[10,512,128]{2,1,0:T(8,128)(2,1)}), bf16[1,512,128]{2,1,0:T(8,128)(2,1)S(1)}, s32[]{:S(2)}) async-start(bf16[10,512,128]{2,1,0:T(8,128)(2,1)} %param.7), calls=%async_computation.4 | async-start | bytes 262144 | tf_op jit(solution)/shard_map/slice | solution.py:106
  31.3 6.8 %copy-start.5 = (pred[64]{0:T(512)(128)(4,1)S(1)}, pred[64]{0:T(512)(128)(4,1)}, u32[]{:S(2)}) copy-start(pred[64]{0:T(512)(128)(4,1)} %fusion.35) | copy-start | bytes 196
  31.3 0.7 copy-start.3
  39.2 33.0 %copy-start = (bf16[1,3,512,512]{3,2,1,0:T(8,128)(2,1)S(1)}, bf16[1,3,512,512]{3,2,1,0:T(8,128)(2,1)}, u32[]{:S(2)}) copy-start(bf16[1,3,512,512]{3,2,1,0:T(8,128)(2,1)} %param.5) | copy-start | bytes 4718596
  39.2 25.4 %all-to-all-start.1 = ((f32[64,8,128]{2,1,0:T(8,128)}), f32[64,8,128]{2,1,0:T(8,128)S(1)}, u32[]{:S(2)}, u32[]{:S(2)}) async-start(f32[64,8,128]{2,1,0:T(8,128)} %select_select_fusion), calls=%async_computation.1 | async-start | bytes 524288 | tf_op jit(solution)/shard_map/all_to_all | solution.py:81
  65.6 19.2 %all-to-all-start.2 = ((bf16[16,9,8,128]{3,2,1,0:T(8,128)(2,1)}), bf16[16,9,8,128]{3,2,1,0:T(8,128)(2,1)S(1)}, u32[]{:S(2)}, u32[]{:S(2)}) async-start(bf16[16,9,8,128]{3,2,1,0:T(8,128)(2,1)} %bitcast.36), calls=%async_computation.2 | async-start | bytes 589824 | tf_op jit(solution)/shard_map/all_to_all | solution.py:97
  72.6 12.3 %copy-start.2 = (bf16[512,8,2,9,8]{0,4,3,2,1:T(8,128)(2,1)S(1)}, bf16[512,8,2,9,8]{0,4,3,2,1:T(8,128)(2,1)}, u32[]{:S(2)}) copy-start(bf16[512,8,2,9,8]{0,4,3,2,1:T(8,128)(2,1)} %copy.33) | copy-start | bytes 3538948
  72.6 12.3 %slice-start.2 = ((bf16[1216,128]{1,0:T(8,128)(2,1)}), bf16[128,128]{1,0:T(8,128)(2,1)S(1)}, s32[]{:S(2)}) async-start(bf16[1216,128]{1,0:T(8,128)(2,1)} %copy-done.3), calls=%async_computation.5 | async-start | bytes 65536 | tf_op jit(solution)/shard_map/slice | solution.py:32

commit v12 on v11

--- a/solution.py
+++ b/solution.py
@@ -85,17 +85,17 @@
         sibling = lax.dynamic_slice_in_dim(received, starts[step], 2**step, 0).sum(axis=0)
         couplings_high.append((sibling * 2.0 ** (-0.5 * level)).astype(jnp.bfloat16))
 
+    low = jnp.stack(couplings_low, axis=1)
     high = jnp.stack(couplings_high)
-    outgoing = jnp.concatenate(
+    everyone = jnp.concatenate(
         [
-            jnp.stack(couplings_low, axis=1),
-            jnp.broadcast_to(high[None], (chips,) + high.shape),
+            jnp.broadcast_to(low[:, None], (chips, 2) + low.shape[1:]),
+            jnp.broadcast_to(high[None, None], (chips, 2) + high.shape),
         ],
-        axis=1,
+        axis=2,
     )
-    everyone = jnp.broadcast_to(outgoing[:, None], (chips, 2) + outgoing.shape[1:])
     returned = lax.all_to_all(
-        everyone.reshape((chips * 2,) + outgoing.shape[1:]), ("x", "core"), 0, 0, tiled=True
+        everyone.reshape((chips * 2,) + everyone.shape[2:]), ("x", "core"), 0, 0, tiled=True
     )
     far_rest = (
         far_basis[1:]

time: 87.6 us -> 87.4 us (level)
  no operation moved by 1% of the time
where the time goes in v12:
time: 87.4 us; the launch traced here: 86.9 us
  starting transfers between devices  40.6 us (46%)
  waiting for transfers between devices  29.3 us (34%)
  local copies, waits for them, and re-layouts  6.89 us (8%)
  matrix products  4.94 us (6%)
  other arithmetic  2.9 us (3%)
  between operations  2.3 us (3%)
    ppermute x1, starting transfers between devices, body(): lax.ppermute(jnp.concatenate([projected[0], send.reshape(-1, width), prob...  16 us
    all_to_all x1, starting transfers between devices, body(): received = lax.all_to_all(outgoing, 'slab', 0, 0, tiled=True)  12.6 us
    all_to_all x1, waiting for transfers between devices, body(): received = lax.all_to_all(outgoing, 'slab', 0, 0, tiled=True)  12.5 us
    all_to_all x1, waiting for transfers between devices, body(): lax.all_to_all(everyone.reshape((chips * 2,) + everyone.shape[2:]), ('x',...  10.9 us
    all_to_all x1, starting transfers between devices, body(): lax.all_to_all(everyone.reshape((chips * 2,) + everyone.shape[2:]), ('x',...  6.63 us
    all_to_all x1, waiting for transfers between devices, body(): lax.all_to_all(paired.reshape(levels - 1, chips, share, width), 'x', 1, 1...  5.93 us
    all_to_all x1, starting transfers between devices, body(): lax.all_to_all(paired.reshape(levels - 1, chips, share, width), 'x', 1, 1...  3.42 us
    unnamed x14, local copies, waits for them, and re-layouts  2.07 us
  transfers between devices with their start and end apart: 5, of which 3 were waited for; matrix products, arithmetic and copies ran while one was open for 7% of the time, Pallas kernels for 0%

profile of v12, /device:TPU:1, one launch (start us, length us, event | category | flops | bytes accessed | tf_op | source)
XLA Modules:
  0.0 86.9 jit_solution(1646250157470858442)
XLA Ops:
  0.0 0.0 copy-start.1
  0.0 1.9 %fusion.18 = f32[10,128,128]{2,1,0:T(8,128)S(1)} fusion(bf16[10,512,128]{2,1,0:T(8,128)(2,1)} %param.7, bf16[512,128]{1,0:T(8,128)(2,1)} %param.4), kind=kOutput, calls=%fused_computation.24 | convolution fusion | flops 167772160 | bytes 2097152 | tf_op jit(solution)/shard_map/lpr,pq->lrq/dot_general | solution.py:12
  1.9 0.0 copy-start.4
  2.0 0.0 copy-done.1
  2.1 16.0 %collective-permute-start.1 = (f32[1216,128]{1,0:T(8,128)S(1)}, f32[1216,128]{1,0:T(8,128)S(1)}, u32[]{:S(2)}, u32[]{:S(2)}) collective-permute-start(f32[1216,128]{1,0:T(8,128)S(1)} %pad_maximum_fusion), channel_id=1, source_target_pairs={{0,1},{1,0},{2,3},{3,2},{4,5},{5,4},{6,7},{7,6},{8,9},{9,8},{10,11... | collective-permute-start | bytes 1867784 | tf_op jit(solution)/shard_map/ppermute | solution.py:25
  18.1 1.9 %collective-permute-start = (bf16[512,128]{1,0:T(8,128)(2,1)S(1)}, bf16[512,128]{1,0:T(8,128)(2,1)S(1)}, u32[]{:S(2)}, u32[]{:S(2)}) collective-permute-start(bf16[512,128]{1,0:T(8,128)(2,1)S(1)} %copy-done.1), channel_id=1, source_target_pairs={{1,2},{2,1},{3,4},{4,3},{5,6},{6,5},{7,8},{8,7},{9,10},{10,9},{11,... | collective-permute-start | bytes 393224 | tf_op jit(solution)/shard_map/ppermute | solution.py:40
  20.1 0.0 copy-done.4
  20.1 0.7 fusion.38
  20.8 0.0 collective-permute-done.1
  20.8 0.7 copy.28
  21.6 3.4 %all-to-all-start = ((f32[9,8,8,128]{3,2,0,1:T(8,128)}), f32[9,8,8,128]{3,2,0,1:T(8,128)S(1)}, u32[]{:S(2)}, u32[]{:S(2)}) async-start(f32[9,8,8,128]{3,2,0,1:T(8,128)} %copy.28), calls=%async_computation | async-start | bytes 589824 | tf_op jit(solution)/shard_map/all_to_all | solution.py:57
  25.0 0.5 fusion.35
  27.5 0.0 slice-start
  27.5 1.3 %slice-done = bf16[9,512,128]{2,1,0:T(8,128)(2,1)S(1)} async-done(((bf16[10,512,128]{2,1,0:T(8,128)(2,1)}), bf16[9,512,128]{2,1,0:T(8,128)(2,1)S(1)}, s32[]{:S(2)}) %slice-start) | async-done | bytes 1179672 | tf_op jit(solution)/shard_map/slice | solution.py:101
  28.7 0.6 copy.35
  29.3 0.0 slice-start.1
  29.4 1.1 %copy.27 = bf16[512,8,2,9,8]{0,4,3,2,1:T(8,128)(2,1)} copy(bf16[512,8,2,9,8]{0,4,1,2,3:T(8,128)(2,1)S(1)} %bitcast.69) | data formatting | bytes 2359296 | tf_op jit(solution)/shard_map/transpose | solution.py:103
  30.5 0.0 slice-done.1
  30.5 0.8 copy.34
  31.3 0.0 copy-start.5
  31.3 0.0 copy-start.3
  31.3 0.0 collective-permute-done
  31.3 0.7 copy-done.3
  32.1 5.9 %all-to-all-done = f32[9,8,8,128]{3,2,0,1:T(8,128)S(1)} async-done(((f32[9,8,8,128]{3,2,0,1:T(8,128)}), f32[9,8,8,128]{3,2,0,1:T(8,128)S(1)}, u32[]{:S(2)}, u32[]{:S(2)}) %all-to-all-start) | async-done | bytes 294944 | tf_op jit(solution)/shard_map/all_to_all | solution.py:57
  38.0 0.0 copy-done.5
  38.0 1.2 %select_select_fusion = f32[64,8,128]{2,1,0:T(8,128)} fusion(f32[8,128]{1,0:T(8,128)S(1)} %get-tuple-element.11, f32[8,128]{1,0:T(8,128)S(1)} %get-tuple-element.12, f32[8,128]{1,0:T(8,128)S(1)} %get-tuple-element.13, f32[8,128]{1,0:T(8,128)S(1)} %get-tuple-element.14, f32[8,128]{1,0:T(8,128)S(1)} %get-tuple-element.15, f32[8,128]{1,0:T(8,128)S(1)} %get-tuple-element.10, ...), kind=kLoop, calls=%fused_computation.22 | loop fusion | flops 327680 | bytes 287040 | tf_op jit(solution)/shard_map/jit(_where)/select_n | solution.py:78
  39.2 12.6 %all-to-all-start.1 = ((f32[64,8,128]{2,1,0:T(8,128)}), f32[64,8,128]{2,1,0:T(8,128)S(1)}, u32[]{:S(2)}, u32[]{:S(2)}) async-start(f32[64,8,128]{2,1,0:T(8,128)} %select_select_fusion), calls=%async_computation.1 | async-start | bytes 524288 | tf_op jit(solution)/shard_map/all_to_all | solution.py:81
  51.8 0.0 copy-start
  52.0 12.5 %all-to-all-done.1 = f32[64,8,128]{2,1,0:T(8,128)S(1)} async-done(((f32[64,8,128]{2,1,0:T(8,128)}), f32[64,8,128]{2,1,0:T(8,128)S(1)}, u32[]{:S(2)}, u32[]{:S(2)}) %all-to-all-start.1) | async-done | bytes 262176 | tf_op jit(solution)/shard_map/all_to_all | solution.py:81
  64.7 0.7 pad_maximum_fusion.2
  65.4 6.6 %all-to-all-start.2 = ((bf16[16,9,8,128]{3,2,1,0:T(8,128)(2,1)}), bf16[16,9,8,128]{3,2,1,0:T(8,128)(2,1)S(1)}, u32[]{:S(2)}, u32[]{:S(2)}) async-start(bf16[16,9,8,128]{3,2,1,0:T(8,128)(2,1)} %bitcast.33), calls=%async_computation.2 | async-start | bytes 589824 | tf_op jit(solution)/shard_map/all_to_all | solution.py:97
  72.1 0.0 copy-done
  72.1 0.3 fusion.9
  72.4 0.0 copy-start.2
  72.4 0.0 slice-start.2
  72.4 0.3 convolution_add_fusion.1
  72.7 1.0 %fusion.7 = f32[512,128]{0,1:T(8,128)} fusion(f32[128,512]{1,0:T(8,128)S(1)} %convolution_add_fusion.1, bf16[1,3,512,512]{3,2,1,0:T(8,128)(2,1)S(1)} %copy-done, bf16[1536,128]{1,0:T(8,128)(2,1)S(1)} %pad_maximum_fusion.1, s32[]{:T(128)S(6)} %select_n.67), kind=kOutput, calls=%fused_computation.6 | convolution fusion | flops 67174400 | bytes 1179652 | tf_op jit(solution)/shard_map/dot_general | solution.py:53
  73.8 10.9 %all-to-all-done.2 = bf16[16,9,8,128]{3,2,1,0:T(8,128)(2,1)S(1)} async-done(((bf16[16,9,8,128]{3,2,1,0:T(8,128)(2,1)}), bf16[16,9,8,128]{3,2,1,0:T(8,128)(2,1)S(1)}, u32[]{:S(2)}, u32[]{:S(2)}) %all-to-all-start.2) | async-done | bytes 294944 | tf_op jit(solution)/shard_map/all_to_all | solution.py:97
  84.7 0.0 copy-done.2
  84.7 0.0 slice-done.2
  84.7 1.4 %fusion.4 = f32[512,128]{0,1:T(8,128)S(1)} fusion(f32[512,128]{0,1:T(8,128)} %fusion.7, bf16[512,1152]{0,1:T(8,128)(2,1)S(1)} %bitcast.72, bf16[512,128]{0,1:T(8,128)(2,1)} %bitcast.74, bf16[1152,128]{1,0:T(8,128)(2,1)S(1)} %bitcast.73, bf16[128,128]{1,0:T(8,128)(2,1)S(1)} %slice-done.2), kind=kOutput, calls=%fused_computation.4 | convolution fusion | flops 171114496 | bytes 2162688 | tf_op jit(solution)/shard_map/dot_general | solution.py:108
  86.1 0.8 copy.31
  (37 shorter events, 0.6 us)
Async XLA Ops:
  0.0 2.0 %copy-start.1 = (bf16[512,128]{1,0:T(8,128)(2,1)S(1)}, bf16[512,128]{1,0:T(8,128)(2,1)}, u32[]{:S(2)}) copy-start(bf16[512,128]{1,0:T(8,128)(2,1)} %param.4) | copy-start | bytes 393220
  1.9 18.1 %copy-start.4 = (s32[1,3]{1,0:T(1,128)S(1)}, s32[1,3]{1,0:T(1,128)}, u32[]{:S(2)}) copy-start(s32[1,3]{1,0:T(1,128)} %param.6) | copy-start | bytes 40
  2.1 18.7 %collective-permute-start.1 = (f32[1216,128]{1,0:T(8,128)S(1)}, f32[1216,128]{1,0:T(8,128)S(1)}, u32[]{:S(2)}, u32[]{:S(2)}) collective-permute-start(f32[1216,128]{1,0:T(8,128)S(1)} %pad_maximum_fusion), channel_id=1, source_target_pairs={{0,1},{1,0},{2,3},{3,2},{4,5},{5,4},{6,7},{7,6},{8,9},{9,8},{10,11... | collective-permute-start | bytes 1867784 | tf_op jit(solution)/shard_map/ppermute | solution.py:25
  18.1 13.2 %collective-permute-start = (bf16[512,128]{1,0:T(8,128)(2,1)S(1)}, bf16[512,128]{1,0:T(8,128)(2,1)S(1)}, u32[]{:S(2)}, u32[]{:S(2)}) collective-permute-start(bf16[512,128]{1,0:T(8,128)(2,1)S(1)} %copy-done.1), channel_id=1, source_target_pairs={{1,2},{2,1},{3,4},{4,3},{5,6},{6,5},{7,8},{8,7},{9,10},{10,9},{11,... | collective-permute-start | bytes 393224 | tf_op jit(solution)/shard_map/ppermute | solution.py:40
  21.6 16.4 %all-to-all-start = ((f32[9,8,8,128]{3,2,0,1:T(8,128)}), f32[9,8,8,128]{3,2,0,1:T(8,128)S(1)}, u32[]{:S(2)}, u32[]{:S(2)}) async-start(f32[9,8,8,128]{3,2,0,1:T(8,128)} %copy.28), calls=%async_computation | async-start | bytes 589824 | tf_op jit(solution)/shard_map/all_to_all | solution.py:57
  27.5 1.3 %slice-start = ((bf16[10,512,128]{2,1,0:T(8,128)(2,1)}), bf16[9,512,128]{2,1,0:T(8,128)(2,1)S(1)}, s32[]{:S(2)}) async-start(bf16[10,512,128]{2,1,0:T(8,128)(2,1)} %param.7), calls=%async_computation.3 | async-start | bytes 2359296 | tf_op jit(solution)/shard_map/slice | solution.py:101
  29.3 1.2 %slice-start.1 = ((bf16[10,512,128]{2,1,0:T(8,128)(2,1)}), bf16[1,512,128]{2,1,0:T(8,128)(2,1)S(1)}, s32[]{:S(2)}) async-start(bf16[10,512,128]{2,1,0:T(8,128)(2,1)} %param.7), calls=%async_computation.4 | async-start | bytes 262144 | tf_op jit(solution)/shard_map/slice | solution.py:106
  31.3 6.8 %copy-start.5 = (pred[64]{0:T(512)(128)(4,1)S(1)}, pred[64]{0:T(512)(128)(4,1)}, u32[]{:S(2)}) copy-start(pred[64]{0:T(512)(128)(4,1)} %fusion.35) | copy-start | bytes 196
  31.3 0.7 copy-start.3
  39.2 25.2 %all-to-all-start.1 = ((f32[64,8,128]{2,1,0:T(8,128)}), f32[64,8,128]{2,1,0:T(8,128)S(1)}, u32[]{:S(2)}, u32[]{:S(2)}) async-start(f32[64,8,128]{2,1,0:T(8,128)} %select_select_fusion), calls=%async_computation.1 | async-start | bytes 524288 | tf_op jit(solution)/shard_map/all_to_all | solution.py:81
  51.8 20.2 %copy-start = (bf16[1,3,512,512]{3,2,1,0:T(8,128)(2,1)S(1)}, bf16[1,3,512,512]{3,2,1,0:T(8,128)(2,1)}, u32[]{:S(2)}) copy-start(bf16[1,3,512,512]{3,2,1,0:T(8,128)(2,1)} %param.5) | copy-start | bytes 4718596
  65.4 19.2 %all-to-all-start.2 = ((bf16[16,9,8,128]{3,2,1,0:T(8,128)(2,1)}), bf16[16,9,8,128]{3,2,1,0:T(8,128)(2,1)S(1)}, u32[]{:S(2)}, u32[]{:S(2)}) async-start(bf16[16,9,8,128]{3,2,1,0:T(8,128)(2,1)} %bitcast.33), calls=%async_computation.2 | async-start | bytes 589824 | tf_op jit(solution)/shard_map/all_to_all | solution.py:97
  72.4 12.3 %copy-start.2 = (bf16[512,8,2,9,8]{0,4,3,2,1:T(8,128)(2,1)S(1)}, bf16[512,8,2,9,8]{0,4,3,2,1:T(8,128)(2,1)}, u32[]{:S(2)}) copy-start(bf16[512,8,2,9,8]{0,4,3,2,1:T(8,128)(2,1)} %copy.27) | copy-start | bytes 3538948
  72.4 12.3 %slice-start.2 = ((bf16[1216,128]{1,0:T(8,128)(2,1)}), bf16[128,128]{1,0:T(8,128)(2,1)S(1)}, s32[]{:S(2)}) async-start(bf16[1216,128]{1,0:T(8,128)(2,1)} %copy-done.3), calls=%async_computation.5 | async-start | bytes 65536 | tf_op jit(solution)/shard_map/slice | solution.py:32

commit v13 on v12

--- a/solution.py
+++ b/solution.py
@@ -66,18 +66,19 @@
             grouped[:, :, None], (nodes, 2, 2**sub, share, width)
         ).reshape(chips, share, width)
         couplings_low.append((sibling * 2.0 ** (-0.5 * level)).astype(jnp.bfloat16))
-    totals = parts[leaf_bits - 1 :].sum(axis=1)
 
     slab_index = lax.axis_index("slab")
     distance = jnp.bitwise_xor(jnp.arange(slabs, dtype=jnp.int32), slab_index)
-    outgoing = jnp.broadcast_to(totals[0][None], (slabs,) + totals.shape[1:])
+    upper = parts[leaf_bits - 1 :]
+    outgoing = jnp.broadcast_to(upper[0][None], (slabs,) + upper.shape[1:])
     starts = []
     for step in range(slab_bits):
         starts.append(jnp.bitwise_xor(slab_index >> step, 1) << step)
         if step:
             outgoing = jnp.where(
-                (distance >= 2**step)[:, None, None], totals[step][None], outgoing
+                (distance >= 2**step)[:, None, None, None], upper[step][None], outgoing
             )
+    outgoing = outgoing.sum(axis=1)
     received = lax.all_to_all(outgoing, "slab", 0, 0, tiled=True)
     couplings_high = []
     for step in range(slab_bits):

time: 87.4 us -> 88.1 us (level)
  waiting for transfers between devices: 29.3 us -> 31.1 us
  local copies, waits for them, and re-layouts: 6.89 us -> 5.6 us
    reduce_sum x1, other arithmetic: 0.01 us -> 1.89 us  [body(): outgoing = outgoing.sum(axis=1)]
    all_to_all x1, waiting for transfers between devices: 5.93 us -> 7.72 us  [body(): lax.all_to_all(paired.reshape(levels - 1, chips, share, width), 'x', 1, 1...]
    slice x2, local copies, waits for them, and re-layouts: 1.27 us -> 0.01 us  [body(): far_basis[1:].reshape(levels - 1, leaf_rows, 2, chips, share)]
    select_n x1 -> x0, other arithmetic: 1.2 us -> none  [body(): jnp.where((distance >= 2 ** step)[:, None, None], totals[step][None], out...]
    unnamed x14 -> x12, local copies, waits for them, and re-layouts: 2.07 us -> 2.1 us
where the time goes in v13:
time: 88.1 us; the launch traced here: 87.6 us
  starting transfers between devices  40.7 us (46%)
  waiting for transfers between devices  31.1 us (35%)
  local copies, waits for them, and re-layouts  5.6 us (6%)
  matrix products  4.95 us (6%)
  other arithmetic  3.04 us (3%)
  between operations  2.29 us (3%)
    ppermute x1, starting transfers between devices, body(): lax.ppermute(jnp.concatenate([projected[0], send.reshape(-1, width), prob...  16 us
    all_to_all x1, starting transfers between devices, body(): received = lax.all_to_all(outgoing, 'slab', 0, 0, tiled=True)  12.6 us
    all_to_all x1, waiting for transfers between devices, body(): received = lax.all_to_all(outgoing, 'slab', 0, 0, tiled=True)  12.5 us
    all_to_all x1, waiting for transfers between devices, body(): lax.all_to_all(everyone.reshape((chips * 2,) + everyone.shape[2:]), ('x',...  10.9 us
    all_to_all x1, waiting for transfers between devices, body(): lax.all_to_all(paired.reshape(levels - 1, chips, share, width), 'x', 1, 1...  7.72 us
    all_to_all x1, starting transfers between devices, body(): lax.all_to_all(everyone.reshape((chips * 2,) + everyone.shape[2:]), ('x',...  6.63 us
    all_to_all x1, starting transfers between devices, body(): lax.all_to_all(paired.reshape(levels - 1, chips, share, width), 'x', 1, 1...  3.55 us
    unnamed x12, local copies, waits for them, and re-layouts  2.1 us
  transfers between devices with their start and end apart: 5, of which 3 were waited for; matrix products, arithmetic and copies ran while one was open for 7% of the time, Pallas kernels for 0%

profile of v13, /device:TPU:1, one launch (start us, length us, event | category | flops | bytes accessed | tf_op | source)
XLA Modules:
  0.0 87.6 jit_solution(15275082258984665603)
XLA Ops:
  0.0 0.0 copy-start.1
  0.0 1.9 %fusion.18 = f32[10,128,128]{2,1,0:T(8,128)S(1)} fusion(bf16[10,512,128]{2,1,0:T(8,128)(2,1)} %param.7, bf16[512,128]{1,0:T(8,128)(2,1)} %param.4), kind=kOutput, calls=%fused_computation.23 | convolution fusion | flops 167772160 | bytes 2097152 | tf_op jit(solution)/shard_map/lpr,pq->lrq/dot_general | solution.py:12
  1.9 0.0 copy-start.4
  2.0 0.0 copy-done.1
  2.1 16.0 %collective-permute-start.1 = (f32[1216,128]{1,0:T(8,128)S(1)}, f32[1216,128]{1,0:T(8,128)S(1)}, u32[]{:S(2)}, u32[]{:S(2)}) collective-permute-start(f32[1216,128]{1,0:T(8,128)S(1)} %pad_maximum_fusion), channel_id=1, source_target_pairs={{0,1},{1,0},{2,3},{3,2},{4,5},{5,4},{6,7},{7,6},{8,9},{9,8},{10,11... | collective-permute-start | bytes 1867784 | tf_op jit(solution)/shard_map/ppermute | solution.py:25
  18.1 1.9 %collective-permute-start = (bf16[512,128]{1,0:T(8,128)(2,1)S(1)}, bf16[512,128]{1,0:T(8,128)(2,1)S(1)}, u32[]{:S(2)}, u32[]{:S(2)}) collective-permute-start(bf16[512,128]{1,0:T(8,128)(2,1)S(1)} %copy-done.1), channel_id=1, source_target_pairs={{1,2},{2,1},{3,4},{4,3},{5,6},{6,5},{7,8},{8,7},{9,10},{10,9},{11,... | collective-permute-start | bytes 393224 | tf_op jit(solution)/shard_map/ppermute | solution.py:40
  20.1 0.0 copy-done.4
  20.1 0.6 fusion.38
  20.7 0.0 collective-permute-done.1
  20.8 0.7 copy.28
  21.5 0.0 slice-start
  21.5 3.6 %all-to-all-start = ((f32[9,8,8,128]{3,2,0,1:T(8,128)}), f32[9,8,8,128]{3,2,0,1:T(8,128)S(1)}, u32[]{:S(2)}, u32[]{:S(2)}) async-start(f32[9,8,8,128]{3,2,0,1:T(8,128)} %copy.28), calls=%async_computation | async-start | bytes 589824 | tf_op jit(solution)/shard_map/all_to_all | solution.py:57
  27.0 0.0 slice-done
  27.0 0.6 copy.35
  27.6 0.0 slice-start.1
  27.6 1.1 %copy.27 = bf16[512,8,2,9,8]{0,4,3,2,1:T(8,128)(2,1)} copy(bf16[512,8,2,9,8]{0,4,1,2,3:T(8,128)(2,1)S(1)} %bitcast.69) | data formatting | bytes 2359296 | tf_op jit(solution)/shard_map/transpose | solution.py:104
  28.8 0.0 slice-done.1
  28.8 0.8 copy.34
  29.6 0.0 copy-start.3
  29.6 0.0 collective-permute-done
  29.6 0.7 copy-done.3
  30.3 7.7 %all-to-all-done = f32[9,8,8,128]{3,2,0,1:T(8,128)S(1)} async-done(((f32[9,8,8,128]{3,2,0,1:T(8,128)}), f32[9,8,8,128]{3,2,0,1:T(8,128)S(1)}, u32[]{:S(2)}, u32[]{:S(2)}) %all-to-all-start) | async-done | bytes 294944 | tf_op jit(solution)/shard_map/all_to_all | solution.py:57
  38.1 1.9 %select_reduce_fusion = f32[64,8,128]{2,1,0:T(8,128)} fusion(f32[8,8,128]{2,1,0:T(8,128)S(1)} %get-tuple-element.8, f32[8,8,128]{2,1,0:T(8,128)S(1)} %get-tuple-element.9, f32[8,8,128]{2,1,0:T(8,128)S(1)} %get-tuple-element.10, f32[8,8,128]{2,1,0:T(8,128)S(1)} %get-tuple-element.11, f32[8,8,128]{2,1,0:T(8,128)S(1)} %get-tuple-element.12, ...), kind=kLoop, calls=%fused_computation | loop fusion | flops 3080192 | bytes 459072 | tf_op jit(solution)/shard_map/reduce_sum | solution.py:81
  40.0 12.6 %all-to-all-start.1 = ((f32[64,8,128]{2,1,0:T(8,128)}), f32[64,8,128]{2,1,0:T(8,128)S(1)}, u32[]{:S(2)}, u32[]{:S(2)}) async-start(f32[64,8,128]{2,1,0:T(8,128)} %select_reduce_fusion), calls=%async_computation.1 | async-start | bytes 524288 | tf_op jit(solution)/shard_map/all_to_all | solution.py:82
  52.6 0.0 copy-start
  52.7 12.5 %all-to-all-done.1 = f32[64,8,128]{2,1,0:T(8,128)S(1)} async-done(((f32[64,8,128]{2,1,0:T(8,128)}), f32[64,8,128]{2,1,0:T(8,128)S(1)}, u32[]{:S(2)}, u32[]{:S(2)}) %all-to-all-start.1) | async-done | bytes 262176 | tf_op jit(solution)/shard_map/all_to_all | solution.py:82
  65.4 0.7 pad_maximum_fusion.2
  66.2 6.6 %all-to-all-start.2 = ((bf16[16,9,8,128]{3,2,1,0:T(8,128)(2,1)}), bf16[16,9,8,128]{3,2,1,0:T(8,128)(2,1)S(1)}, u32[]{:S(2)}, u32[]{:S(2)}) async-start(bf16[16,9,8,128]{3,2,1,0:T(8,128)(2,1)} %bitcast.33), calls=%async_computation.2 | async-start | bytes 589824 | tf_op jit(solution)/shard_map/all_to_all | solution.py:98
  72.8 0.0 copy-done
  72.8 0.0 copy-start.2
  72.8 0.0 slice-start.2
  72.8 0.3 fusion.9
  73.1 0.3 convolution_add_fusion.1
  73.5 1.0 %fusion.7 = f32[512,128]{0,1:T(8,128)} fusion(f32[128,512]{1,0:T(8,128)S(1)} %convolution_add_fusion.1, bf16[1,3,512,512]{3,2,1,0:T(8,128)(2,1)S(1)} %copy-done, bf16[1536,128]{1,0:T(8,128)(2,1)S(1)} %pad_maximum_fusion.1, s32[]{:T(128)S(6)} %select_n.67), kind=kOutput, calls=%fused_computation.7 | convolution fusion | flops 67174400 | bytes 1179652 | tf_op jit(solution)/shard_map/dot_general | solution.py:53
  74.5 10.9 %all-to-all-done.2 = bf16[16,9,8,128]{3,2,1,0:T(8,128)(2,1)S(1)} async-done(((bf16[16,9,8,128]{3,2,1,0:T(8,128)(2,1)}), bf16[16,9,8,128]{3,2,1,0:T(8,128)(2,1)S(1)}, u32[]{:S(2)}, u32[]{:S(2)}) %all-to-all-start.2) | async-done | bytes 294944 | tf_op jit(solution)/shard_map/all_to_all | solution.py:98
  85.4 0.0 copy-done.2
  85.4 0.0 slice-done.2
  85.4 1.4 %fusion.4 = f32[512,128]{0,1:T(8,128)S(1)} fusion(f32[512,128]{0,1:T(8,128)} %fusion.7, bf16[512,1152]{0,1:T(8,128)(2,1)S(1)} %bitcast.72, bf16[512,128]{0,1:T(8,128)(2,1)} %bitcast.77, bf16[1152,128]{1,0:T(8,128)(2,1)S(1)} %bitcast.73, bf16[128,128]{1,0:T(8,128)(2,1)S(1)} %slice-done.2), kind=kOutput, calls=%fused_computation.5 | convolution fusion | flops 171114496 | bytes 2162688 | tf_op jit(solution)/shard_map/dot_general | solution.py:109
  86.8 0.8 copy.31
  (36 shorter events, 0.6 us)
Async XLA Ops:
  0.0 2.0 %copy-start.1 = (bf16[512,128]{1,0:T(8,128)(2,1)S(1)}, bf16[512,128]{1,0:T(8,128)(2,1)}, u32[]{:S(2)}) copy-start(bf16[512,128]{1,0:T(8,128)(2,1)} %param.4) | copy-start | bytes 393220
  1.9 18.2 %copy-start.4 = (s32[1,3]{1,0:T(1,128)S(1)}, s32[1,3]{1,0:T(1,128)}, u32[]{:S(2)}) copy-start(s32[1,3]{1,0:T(1,128)} %param.6) | copy-start | bytes 40
  2.1 18.6 %collective-permute-start.1 = (f32[1216,128]{1,0:T(8,128)S(1)}, f32[1216,128]{1,0:T(8,128)S(1)}, u32[]{:S(2)}, u32[]{:S(2)}) collective-permute-start(f32[1216,128]{1,0:T(8,128)S(1)} %pad_maximum_fusion), channel_id=1, source_target_pairs={{0,1},{1,0},{2,3},{3,2},{4,5},{5,4},{6,7},{7,6},{8,9},{9,8},{10,11... | collective-permute-start | bytes 1867784 | tf_op jit(solution)/shard_map/ppermute | solution.py:25
  18.1 11.5 %collective-permute-start = (bf16[512,128]{1,0:T(8,128)(2,1)S(1)}, bf16[512,128]{1,0:T(8,128)(2,1)S(1)}, u32[]{:S(2)}, u32[]{:S(2)}) collective-permute-start(bf16[512,128]{1,0:T(8,128)(2,1)S(1)} %copy-done.1), channel_id=1, source_target_pairs={{1,2},{2,1},{3,4},{4,3},{5,6},{6,5},{7,8},{8,7},{9,10},{10,9},{11,... | collective-permute-start | bytes 393224 | tf_op jit(solution)/shard_map/ppermute | solution.py:40
  21.5 5.5 %slice-start = ((bf16[10,512,128]{2,1,0:T(8,128)(2,1)}), bf16[9,512,128]{2,1,0:T(8,128)(2,1)S(1)}, s32[]{:S(2)}) async-start(bf16[10,512,128]{2,1,0:T(8,128)(2,1)} %param.7), calls=%async_computation.3 | async-start | bytes 2359296 | tf_op jit(solution)/shard_map/slice | solution.py:102
  21.5 16.6 %all-to-all-start = ((f32[9,8,8,128]{3,2,0,1:T(8,128)}), f32[9,8,8,128]{3,2,0,1:T(8,128)S(1)}, u32[]{:S(2)}, u32[]{:S(2)}) async-start(f32[9,8,8,128]{3,2,0,1:T(8,128)} %copy.28), calls=%async_computation | async-start | bytes 589824 | tf_op jit(solution)/shard_map/all_to_all | solution.py:57
  27.6 1.1 %slice-start.1 = ((bf16[10,512,128]{2,1,0:T(8,128)(2,1)}), bf16[1,512,128]{2,1,0:T(8,128)(2,1)S(1)}, s32[]{:S(2)}) async-start(bf16[10,512,128]{2,1,0:T(8,128)(2,1)} %param.7), calls=%async_computation.4 | async-start | bytes 262144 | tf_op jit(solution)/shard_map/slice | solution.py:107
  29.6 0.7 copy-start.3
  40.0 25.2 %all-to-all-start.1 = ((f32[64,8,128]{2,1,0:T(8,128)}), f32[64,8,128]{2,1,0:T(8,128)S(1)}, u32[]{:S(2)}, u32[]{:S(2)}) async-start(f32[64,8,128]{2,1,0:T(8,128)} %select_reduce_fusion), calls=%async_computation.1 | async-start | bytes 524288 | tf_op jit(solution)/shard_map/all_to_all | solution.py:82
  52.6 20.2 %copy-start = (bf16[1,3,512,512]{3,2,1,0:T(8,128)(2,1)S(1)}, bf16[1,3,512,512]{3,2,1,0:T(8,128)(2,1)}, u32[]{:S(2)}) copy-start(bf16[1,3,512,512]{3,2,1,0:T(8,128)(2,1)} %param.5) | copy-start | bytes 4718596
  66.2 19.2 %all-to-all-start.2 = ((bf16[16,9,8,128]{3,2,1,0:T(8,128)(2,1)}), bf16[16,9,8,128]{3,2,1,0:T(8,128)(2,1)S(1)}, u32[]{:S(2)}, u32[]{:S(2)}) async-start(bf16[16,9,8,128]{3,2,1,0:T(8,128)(2,1)} %bitcast.33), calls=%async_computation.2 | async-start | bytes 589824 | tf_op jit(solution)/shard_map/all_to_all | solution.py:98
  72.8 12.6 %copy-start.2 = (bf16[512,8,2,9,8]{0,4,3,2,1:T(8,128)(2,1)S(1)}, bf16[512,8,2,9,8]{0,4,3,2,1:T(8,128)(2,1)}, u32[]{:S(2)}) copy-start(bf16[512,8,2,9,8]{0,4,3,2,1:T(8,128)(2,1)} %copy.27) | copy-start | bytes 3538948
  72.8 12.6 %slice-start.2 = ((bf16[1216,128]{1,0:T(8,128)(2,1)}), bf16[128,128]{1,0:T(8,128)(2,1)S(1)}, s32[]{:S(2)}) async-start(bf16[1216,128]{1,0:T(8,128)(2,1)} %copy-done.3), calls=%async_computation.5 | async-start | bytes 65536 | tf_op jit(solution)/shard_map/slice | solution.py:32
